TPU v7x, 128 devices: a whole 4x4x4 slice. The times are simulated.
128 devices in a mesh: expert: 32 (over y, x, core), dp: 4 (over z).
Axes of the slice: x: 4, y: 4, z: 4, core: 2. Of those that a mesh axis runs over, the one named last changes fastest.
Arguments:
- tokens: bfloat16 [8192, 3584], P(('expert', 'dp')), may hold values from -6 to 6
- out_grad: bfloat16 [8192, 3584], P(('expert', 'dp')), may hold values from -6 to 6
- route_ids: int32 [8192, 8], P(('expert', 'dp')), may hold values from 0 to 31, all different within a row; in each aligned block of 64 rows (0 to 63, 64 to 127, ...) at most 20 rows name the same one
- route_logits: float32 [8192, 8], P(('expert', 'dp')), may hold values from -6 to 6
- gate_up: bfloat16 [32, 2, 3584, 1024], P('expert', None, None, 'dp'), may hold values from -0.09375 to 0.09375
- down: bfloat16 [32, 1024, 3584], P('expert', 'dp'), may hold values from -0.1875 to 0.1875
- moment1: bfloat16 [32, 1024, 3584], P('expert', 'dp'), may hold values from -8 to 8
- moment2: bfloat16 [32, 1024, 3584], P('expert', 'dp'), may hold values from 0.5 to 20
Outputs:
- token_grad: bfloat16 [8192, 3584], P(('expert', 'dp'))
- router_grad: float32 [8192, 8], P(('expert', 'dp'))
- new_down: bfloat16 [32, 1024, 3584], P('expert', 'dp')
- new_moment1: bfloat16 [32, 1024, 3584], P('expert', 'dp')
- new_moment2: bfloat16 [32, 1024, 3584], P('expert', 'dp')
Inputs may be any that keep to these rules, and one draw needn't show every extreme that they name: `route_ids`: each row names 8 different experts. Within the 64 rows of one device no expert is named more than 20 times, and in every draw the rows of some device name some expert exactly 20 times.
All inputs are finite; a program needn't handle non-finite values.
Results may differ from a plain program's by a relative error of at most 0.012.
Values may be sent and summed in bfloat16 or wider, within the bound.
No kernel may reach another device: no remote copies, remote signals or barrier semaphores. Data moves between devices by JAX's collectives and lax.ppermute only.
A program may use at most 192 MiB of HBM per device.

v0:
```python
import jax
import jax.numpy as jnp
from jax import lax
from jax.sharding import PartitionSpec as P

STEP = 10


ROUTE_SCALE = 2.5
BETA_ONE = 0.9
BETA_TWO = 0.95
LEARN_RATE = 0.001
DECAY = 0.1
EPSILON = 1e-08


def contract_last(left, right):
    return lax.dot_general(
        left, right, (((1,), (1,)), ((), ())), preferred_element_type=jnp.float32
    )


def contract_first(left, right):
    return lax.dot_general(
        left, right, (((0,), (0,)), ((), ())), preferred_element_type=jnp.float32
    )


def shards(tokens, out_grad, route_ids, route_logits, gate_up, down, moment1, moment2):
    experts = lax.axis_size("expert")
    data_ways = lax.axis_size("dp")
    tok_rows, model_width = tokens.shape
    top_count = route_ids.shape[1]
    capacity = min(tok_rows, max(2, 5 * tok_rows * top_count // (4 * experts)))
    slot_count = experts * capacity
    scores = jax.nn.sigmoid(route_logits)
    score_sum = jnp.sum(scores, axis=1, keepdims=True)
    route_weight = (ROUTE_SCALE * scores / score_sum).astype(jnp.bfloat16)
    flat_ids = route_ids.reshape(-1)
    onehot = (flat_ids[:, None] == jnp.arange(experts, dtype=jnp.int32)[None, :]).astype(jnp.int32)
    before = jnp.cumsum(onehot, axis=0) - onehot
    places = jnp.sum(before * onehot, axis=1)
    slot_index = flat_ids * capacity + places
    matched = (jnp.arange(slot_count, dtype=jnp.int32)[:, None] == slot_index[None, :]).astype(
        jnp.float32
    )
    tok_match = jnp.sum(matched.reshape(slot_count, tok_rows, top_count), axis=2).astype(
        jnp.bfloat16
    )
    payload = jnp.concatenate([tokens, out_grad], axis=1)
    send_rows = jnp.dot(tok_match, payload, preferred_element_type=jnp.float32).astype(jnp.bfloat16)
    send_rows = send_rows.reshape(experts, capacity, 2 * model_width)
    send_weight = jnp.sum(matched * route_weight.astype(jnp.float32).reshape(-1)[None, :], axis=1)
    send_weight = send_weight.astype(jnp.bfloat16).reshape(experts, capacity)
    recv_rows, recv_weight = (
        lax.all_to_all(send_rows, "expert", split_axis=0, concat_axis=0, tiled=True),
        lax.all_to_all(send_weight, "expert", split_axis=0, concat_axis=0, tiled=True),
    )
    recv_rows = recv_rows.reshape(slot_count, 2 * model_width)
    xs_rows = recv_rows[:, :model_width]
    gs_rows = recv_rows[:, model_width:]
    slot_weight = recv_weight.reshape(slot_count).astype(jnp.float32)
    full_gu, full_down = (
        lax.all_gather(gate_up, "dp", axis=3, tiled=True),
        lax.all_gather(down, "dp", axis=1, tiled=True),
    )
    back_raw = contract_last(gs_rows, full_down[0])
    gate_w = full_gu[0, 0]
    up_w = full_gu[0, 1]
    pre_gate = jnp.dot(xs_rows, gate_w, preferred_element_type=jnp.float32)
    pre_up = jnp.dot(xs_rows, up_w, preferred_element_type=jnp.float32)
    sig_gate = jax.nn.sigmoid(pre_gate)
    silu_gate = pre_gate * sig_gate
    hidden = (silu_gate * pre_up).astype(jnp.bfloat16)
    affinity = jnp.sum(hidden.astype(jnp.float32) * back_raw, axis=1).astype(jnp.bfloat16)
    scaled = (slot_weight[:, None] * gs_rows.astype(jnp.float32)).astype(jnp.bfloat16)
    local_grad = contract_first(hidden, scaled)
    grad_shard = lax.psum_scatter(
        local_grad.astype(jnp.bfloat16), "dp", scatter_dimension=0, tiled=True
    ).astype(jnp.float32)
    down_grad = (grad_shard / data_ways)[None]
    back = slot_weight[:, None] * back_raw
    gate_grad = (back * pre_up * sig_gate * (1.0 + pre_gate * (1.0 - sig_gate))).astype(
        jnp.bfloat16
    )
    up_grad = (back * silu_gate).astype(jnp.bfloat16)
    route_in = (contract_last(gate_grad, gate_w) + contract_last(up_grad, up_w)).astype(
        jnp.bfloat16
    )
    back_rows, back_affinity = (
        lax.all_to_all(
            route_in.reshape(experts, capacity, model_width),
            "expert",
            split_axis=0,
            concat_axis=0,
            tiled=True,
        ),
        lax.all_to_all(
            affinity.reshape(experts, capacity), "expert", split_axis=0, concat_axis=0, tiled=True
        ),
    )
    back_rows = back_rows.reshape(slot_count, model_width)
    token_grad = contract_first(tok_match, back_rows).astype(jnp.bfloat16)
    route_affinity = jnp.sum(
        matched * back_affinity.reshape(slot_count, 1).astype(jnp.float32), axis=0
    )
    route_affinity = route_affinity.reshape(tok_rows, top_count)
    mixed = jnp.sum(route_affinity * scores, axis=1, keepdims=True) / score_sum
    router_grad = ROUTE_SCALE * scores * (1.0 - scores) * (route_affinity - mixed) / score_sum
    corr_one = 1.0 - BETA_ONE**STEP
    corr_two = 1.0 - BETA_TWO**STEP
    down_wide = down.astype(jnp.float32)
    first = BETA_ONE * moment1.astype(jnp.float32) + (1.0 - BETA_ONE) * down_grad
    second = BETA_TWO * moment2.astype(jnp.float32) + (1.0 - BETA_TWO) * down_grad * down_grad
    update = first / corr_one / (jnp.sqrt(second / corr_two) + EPSILON) + DECAY * down_wide
    new_down = (down_wide - LEARN_RATE * update).astype(jnp.bfloat16)
    return (
        token_grad,
        router_grad,
        new_down,
        first.astype(jnp.bfloat16),
        second.astype(jnp.bfloat16),
    )


def solution(mesh):
    placed = (
        P(("expert", "dp"), None),
        P(("expert", "dp"), None),
        P(("expert", "dp"), None),
        P(("expert", "dp"), None),
        P("expert", None, None, "dp"),
        P("expert", "dp", None),
        P("expert", "dp", None),
        P("expert", "dp", None),
    )
    return jax.shard_map(
        shards,
        mesh=mesh,
        in_specs=placed,
        out_specs=(
            P(("expert", "dp"), None),
            P(("expert", "dp"), None),
            P("expert", "dp", None),
            P("expert", "dp", None),
            P("expert", "dp", None),
        ),
        check_vma=False,
    )
```

profile of v0, /device:TPU:1, one launch (start us, length us, event | category | flops | bytes accessed | tf_op | source)
XLA Modules:
  0.0 413.4 jit_solution(15730780176443406466)
XLA Ops:
  7.2 0.7 all-gather.5.cloned.1.call-update
  8.2 1.2 reduce-window.6
  9.4 0.2 slice_reduce_fusion
  10.0 0.5 convert_reduce_fusion
  10.5 6.0 %convolution_convert_fusion = bf16[640,7168]{1,0:T(8,128)(2,1)} fusion(bf16[64,3584]{1,0:T(8,128)(2,1)S(1)} %copy-done.2, bf16[64,3584]{1,0:T(8,128)(2,1)S(1)} %copy-done.3, bf16[640,64]{0,1:T(8,128)(2,1)S(1)} %convert_reduce_fusion), kind=kOutput, calls=%fused_computation | convolution fusion | flops 593625088 | bytes 10174464 | tf_op jit(solution)/shard_map/dot_general | solution.py:51
  16.5 13.7 %reshape.123 = bf16[32,20,7168]{2,1,0:T(8,128)(2,1)} reshape(bf16[640,7168]{1,0:T(8,128)(2,1)} %convolution_convert_fusion) | data formatting | bytes 18350080 | tf_op jit(solution)/shard_map/reshape | solution.py:52
  30.2 8.7 %all-to-all-start.1 = ((bf16[32,20,7168]{2,1,0:T(8,128)(2,1)}), bf16[32,20,7168]{2,1,0:T(8,128)(2,1)}, u32[]{:S(2)}, u32[]{:S(2)}) async-start(bf16[32,20,7168]{2,1,0:T(8,128)(2,1)} %reshape.123), calls=%async_computation.1 | async-start | bytes 22020096 | tf_op jit(solution)/shard_map/all_to_all | solution.py:56
  38.9 0.2 all-gather.3.cloned.1.call-start
  39.1 0.5 all-gather.3.cloned.1.call-update
  39.7 131.6 %all-to-all-done.1 = bf16[32,20,7168]{2,1,0:T(8,128)(2,1)} async-done(((bf16[32,20,7168]{2,1,0:T(8,128)(2,1)}), bf16[32,20,7168]{2,1,0:T(8,128)(2,1)}, u32[]{:S(2)}, u32[]{:S(2)}) %all-to-all-start.1) | async-done | bytes 9175072 | tf_op jit(solution)/shard_map/all_to_all | solution.py:56
  171.2 13.4 %reshape.124 = bf16[640,7168]{1,0:T(8,128)(2,1)} reshape(bf16[32,20,7168]{2,1,0:T(8,128)(2,1)} %all-to-all-done.1) | data formatting | bytes 18350080 | tf_op jit(solution)/shard_map/reshape | solution.py:59
  184.6 11.2 %fusion.4 = f32[640,1024]{1,0:T(8,128)} fusion(bf16[1,2,3584,1024]{3,2,1,0:T(8,128)(2,1)} %all-gather.5.cloned.1.call-done, bf16[640,7168]{1,0:T(8,128)(2,1)} %reshape.124), kind=kOutput, calls=%fused_computation.10 | convolution fusion | flops 4697620480 | bytes 14548992 | tf_op jit(solution)/shard_map/dot_general | solution.py:70
  195.9 1.3 copy-done.6
  197.2 6.4 %fusion.2 = f32[640,1024]{1,0:T(8,128)} fusion(bf16[1,2,3584,1024]{3,2,1,0:T(8,128)(2,1)S(1)} %copy-done.6, bf16[640,7168]{1,0:T(8,128)(2,1)S(1)} %copy-done), kind=kOutput, calls=%fused_computation.8 | convolution fusion | flops 4697620480 | bytes 14548992 | tf_op jit(solution)/shard_map/dot_general | solution.py:71
  203.6 25.8 %all-gather.3.cloned.1.call-done = bf16[1,1024,3584]{2,1,0:T(8,128)(2,1)} async-done(((bf16[1,256,3584]{2,1,0:T(8,128)(2,1)}), bf16[1,1024,3584]{2,1,0:T(8,128)(2,1)}) %all-gather.3.cloned.1.call-update) | async-done | bytes 7340048 | tf_op jit(solution)/shard_map/all_gather | solution.py:65
  229.4 12.4 %multiply_reduce_fusion = (bf16[640]{0:T(1024)(128)(2,1)S(1)}, bf16[640,1024]{1,0:T(8,128)(2,1)S(1)}, f32[640,1024]{1,0:T(8,128)}) fusion(f32[640,1024]{1,0:T(8,128)} %fusion.2, f32[640,1024]{1,0:T(8,128)} %fusion.4, bf16[1,1024,3584]{2,1,0:T(8,128)(2,1)} %all-gather.3.cloned.1.call-done, bf16[640,7168]{1,0:T(8,128)(2,1)} %reshape.124), kind=kOutput, calls=%fused_computation.30 | convolution fusion | flops 4703518208 | bytes 21103872 | tf_op jit(solution)/shard_map/dot_general | solution.py:18
  241.8 0.7 convert_element_type.151
  242.5 7.7 %all-to-all-start.3 = ((bf16[32,1,20]{2,1,0:T(2,128)(2,1)}), bf16[32,1,20]{2,1,0:T(2,128)(2,1)S(1)}, u32[]{:S(2)}, u32[]{:S(2)}) async-start(bf16[32,1,20]{2,1,0:T(2,128)(2,1)} %convert_element_type.151), calls=%async_computation.3 | async-start | bytes 32768 | tf_op jit(solution)/shard_map/all_to_all | solution.py:98
  250.3 6.8 %all-to-all-done.3 = bf16[32,1,20]{2,1,0:T(2,128)(2,1)S(1)} async-done(((bf16[32,1,20]{2,1,0:T(2,128)(2,1)}), bf16[32,1,20]{2,1,0:T(2,128)(2,1)S(1)}, u32[]{:S(2)}, u32[]{:S(2)}) %all-to-all-start.3) | async-done | bytes 1312 | tf_op jit(solution)/shard_map/all_to_all | solution.py:98
  257.3 0.3 select_reduce_fusion
  257.8 0.6 multiply_divide_fusion
  258.6 0.2 select_reduce_fusion.1
  258.8 0.1 convert_element_type.150
  258.9 10.7 %all_to_all.22 = bf16[32,1,20]{2,1,0:T(2,128)(2,1)S(1)} all-to-all(bf16[32,1,20]{2,1,0:T(2,128)(2,1)S(1)} %convert_element_type.150), channel_id=1, replica_groups=mesh['expert'=32,'dp'=4] {'expert'}, dimensions={0} | all-to-all | bytes 2560 | tf_op jit(solution)/shard_map/all_to_all | solution.py:57
  269.7 10.6 %convolution_convert_fusion.1 = bf16[1024,3584]{1,0:T(8,128)(2,1)} fusion(bf16[640,1024]{1,0:T(8,128)(2,1)S(1)} %get-tuple-element.23, f32[640]{0:T(1024)S(1)} %reshape.129, bf16[640,7168]{1,0:T(8,128)(2,1)} %reshape.124), kind=kOutput, calls=%fused_computation.3 | convolution fusion | flops 4708171776 | bytes 13240832 | tf_op jit(solution)/shard_map/dot_general | solution.py:24
  280.4 14.8 %fusion.3 = f32[640,3584]{1,0:T(8,128)} fusion(bf16[1,2,3584,1024]{3,2,1,0:T(8,128)(2,1)} %all-gather.5.cloned.1.call-done, f32[640,1024]{1,0:T(8,128)} %fusion.4, f32[640,1024]{1,0:T(8,128)} %fusion.2, f32[640,1024]{1,0:T(8,128)} %get-tuple-element.29, f32[640]{0:T(1024)S(1)} %reshape.129), kind=kOutput, calls=%fused_computation.9 | convolution fusion | flops 4704829440 | bytes 24381952 | tf_op jit(solution)/shard_map/dot_general | solution.py:18
  295.1 15.1 %add_convert_fusion = bf16[640,3584]{1,0:T(8,128)(2,1)} fusion(f32[640,3584]{1,0:T(8,128)} %fusion.3, bf16[1,2,3584,1024]{3,2,1,0:T(8,128)(2,1)} %all-gather.5.cloned.1.call-done, f32[640,1024]{1,0:T(8,128)} %get-tuple-element.29, f32[640]{0:T(1024)S(1)} %reshape.129, f32[640,1024]{1,0:T(8,128)} %fusion.4), kind=kOutput, calls=%fused_computation.2 | convolution fusion | flops 4706795520 | bytes 26348032 | tf_op jit(solution)/shard_map/dot_general | solution.py:18
  310.3 7.3 %reshape.125 = bf16[32,20,3584]{2,1,0:T(8,128)(2,1)} reshape(bf16[640,3584]{1,0:T(8,128)(2,1)} %add_convert_fusion) | data formatting | bytes 9175040 | tf_op jit(solution)/shard_map/reshape | solution.py:92
  317.6 70.3 %all_to_all.23 = bf16[32,20,3584]{2,1,0:T(8,128)(2,1)} all-to-all(bf16[32,20,3584]{2,1,0:T(8,128)(2,1)} %reshape.125), channel_id=1, replica_groups=mesh['expert'=32,'dp'=4] {'expert'}, dimensions={0} | all-to-all | bytes 9175040 | tf_op jit(solution)/shard_map/all_to_all | solution.py:91
  387.9 7.3 %reshape.126 = bf16[640,3584]{1,0:T(8,128)(2,1)} reshape(bf16[32,20,3584]{2,1,0:T(8,128)(2,1)} %all_to_all.23) | data formatting | bytes 9175040 | tf_op jit(solution)/shard_map/reshape | solution.py:102
  395.1 4.1 convolution_convert_fusion.2
  399.2 7.7 %fusion.20 = (bf16[1,256,3584]{2,1,0:T(8,128)(2,1)}, bf16[1,256,3584]{2,1,0:T(8,128)(2,1)}, bf16[1,256,3584]{2,1,0:T(8,128)(2,1)}) fusion(bf16[256,3584]{1,0:T(8,128)(2,1)} %reduce-scatter.2.cloned.1.call-done, bf16[1,256,3584]{2,1,0:T(8,128)(2,1)} %param.15, bf16[1,256,3584]{2,1,0:T(8,128)(2,1)} %param.14, bf16[1,256,3584]{2,1,0:T(8,128)(2,1)S(1)} %copy-done.1), kind=kLoop, calls=%fused_computation.37 | loop fusion | flops 21102592 | bytes 12845056 | tf_op jit(solution)/shard_map/convert_element_type | solution.py:122
  (40 shorter events, 1.4 us)
Async XLA Ops:
  7.2 0.8 copy-start.4
  7.2 3.3 copy-start.3
  7.2 3.3 copy-start.2
  7.2 177.4 %all-gather.5.cloned.1.call-start = ((), (), s32[]{:S(2)}) async-start(), calls=%async_computation.6 | async-start | bytes 18350080 | tf_op jit(solution)/shard_map/all_gather | solution.py:64
  30.2 141.0 %all-to-all-start.1 = ((bf16[32,20,7168]{2,1,0:T(8,128)(2,1)}), bf16[32,20,7168]{2,1,0:T(8,128)(2,1)}, u32[]{:S(2)}, u32[]{:S(2)}) async-start(bf16[32,20,7168]{2,1,0:T(8,128)(2,1)} %reshape.123), calls=%async_computation.1 | async-start | bytes 22020096 | tf_op jit(solution)/shard_map/all_to_all | solution.py:56
  38.9 190.5 %all-gather.3.cloned.1.call-start = ((), (), s32[]{:S(2)}) async-start(), calls=%async_computation.5 | async-start | bytes 9175040 | tf_op jit(solution)/shard_map/all_gather | solution.py:65
  184.6 11.2 %copy-start = (bf16[640,7168]{1,0:T(8,128)(2,1)S(1)}, bf16[640,7168]{1,0:T(8,128)(2,1)}, u32[]{:S(2)}) copy-start(bf16[640,7168]{1,0:T(8,128)(2,1)} %reshape.124) | copy-start | bytes 27525124
  184.6 12.5 %copy-start.6 = (bf16[1,2,3584,1024]{3,2,1,0:T(8,128)(2,1)S(1)}, bf16[1,2,3584,1024]{3,2,1,0:T(8,128)(2,1)}, u32[]{:S(2)}) copy-start(bf16[1,2,3584,1024]{3,2,1,0:T(8,128)(2,1)} %all-gather.5.cloned.1.call-done) | copy-start | bytes 44040196
  203.6 54.1 %copy-start.5 = (f32[64,8]{0,1:T(8,128)S(1)}, f32[64,8]{0,1:T(8,128)}, u32[]{:S(2)}) copy-start(f32[64,8]{0,1:T(8,128)} %param.11) | copy-start | bytes 6148
  242.5 14.6 %all-to-all-start.3 = ((bf16[32,1,20]{2,1,0:T(2,128)(2,1)}), bf16[32,1,20]{2,1,0:T(2,128)(2,1)S(1)}, u32[]{:S(2)}, u32[]{:S(2)}) async-start(bf16[32,1,20]{2,1,0:T(2,128)(2,1)} %convert_element_type.151), calls=%async_computation.3 | async-start | bytes 32768 | tf_op jit(solution)/shard_map/all_to_all | solution.py:98
  250.2 149.0 %reduce-scatter.2.cloned.1.call-start = ((), (), s32[]{:S(2)}) async-start(), calls=%async_computation.7 | async-start | bytes 9175040 | tf_op jit(solution)/shard_map/reduce_scatter | solution.py:78
  395.1 4.1 copy-start.1
Sparse Core Ops, SparseCore 0:
  9.7 142.1 all-gather.4
  153.5 75.8 all-gather.2
  280.5 69.7 reduce-scatter.1
where the time goes:
time: 415 us; the launch traced here: 413 us
  waiting for transfers between devices  165 us (40%)
  blocking collectives  81 us (20%)
  matrix products  80.6 us (19%)
  local copies, waits for them, and re-layouts  45.1 us (11%)
  starting transfers between devices  16.6 us (4%)
  between operations  13.9 us (3%)
  other arithmetic  10.7 us (3%)
    all_to_all x1, waiting for transfers between devices, shards(): lax.all_to_all(send_rows, 'expert', split_axis=0, concat_axis=0, tiled=True)  132 us
    all_to_all x1, blocking collectives, shards(): lax.all_to_all(route_in.reshape(experts, capacity, model_width), 'expert'...  70.3 us
    dot_general x3, matrix products, contract_last(): lax.dot_general(left, right, (((1,), (1,)), ((), ())), preferred_element_...  42.3 us
    all_gather x1, waiting for transfers between devices, shards(): lax.all_gather(down, 'dp', axis=1, tiled=True)  25.8 us
    dot_general x2, matrix products, contract_first(): lax.dot_general(left, right, (((0,), (0,)), ((), ())), preferred_element_...  14.7 us
    reshape x1, local copies, waits for them, and re-layouts, shards(): send_rows = send_rows.reshape(experts, capacity, 2 * model_width)  13.7 us
    reshape x1, local copies, waits for them, and re-layouts, shards(): recv_rows = recv_rows.reshape(slot_count, 2 * model_width)  13.4 us
    dot_general x1, matrix products, shards(): pre_gate = jnp.dot(xs_rows, gate_w, preferred_element_type=jnp.float32)  11.2 us
  transfers between devices with their start and end apart: 5, of which 3 were waited for; matrix products, arithmetic and copies ran while one was open for 25% of the time, Pallas kernels for 0%

commit v1 on v0

v1 whole, which is shorter than its diff:
```python
import jax
import jax.numpy as jnp
from jax import lax
from jax.sharding import PartitionSpec as P

STEP = 10


ROUTE_SCALE = 2.5
BETA_ONE = 0.9
BETA_TWO = 0.95
LEARN_RATE = 0.001
DECAY = 0.1
EPSILON = 1e-08
LANE = 128
HALVES = 2


def contract_last(left, right):
    return lax.dot_general(
        left, right, (((1,), (1,)), ((), ())), preferred_element_type=jnp.float32
    )


def contract_first(left, right):
    return lax.dot_general(
        left, right, (((0,), (0,)), ((), ())), preferred_element_type=jnp.float32
    )


def shards(tokens, out_grad, route_ids, route_logits, gate_up, down, moment1, moment2):
    experts = lax.axis_size("expert")
    data_ways = lax.axis_size("dp")
    tok_rows, model_width = tokens.shape
    top_count = route_ids.shape[1]
    local_ffw = down.shape[1]
    part_ffw = local_ffw // HALVES
    capacity = min(tok_rows, max(2, 5 * tok_rows * top_count // (4 * experts)))
    capacity = -(-capacity // 8) * 8
    slot_count = experts * capacity
    scores = jax.nn.sigmoid(route_logits)
    score_sum = jnp.sum(scores, axis=1, keepdims=True)
    route_weight = (ROUTE_SCALE * scores / score_sum).astype(jnp.bfloat16)
    flat_ids = route_ids.reshape(-1)
    onehot = (flat_ids[:, None] == jnp.arange(experts, dtype=jnp.int32)[None, :]).astype(jnp.int32)
    before = jnp.cumsum(onehot, axis=0) - onehot
    places = jnp.sum(before * onehot, axis=1)
    slot_index = flat_ids * capacity + places
    matched = (jnp.arange(slot_count, dtype=jnp.int32)[:, None] == slot_index[None, :]).astype(
        jnp.float32
    )
    tok_match = jnp.sum(matched.reshape(slot_count, tok_rows, top_count), axis=2).astype(
        jnp.bfloat16
    )
    send_weight = jnp.sum(matched * route_weight.astype(jnp.float32).reshape(-1)[None, :], axis=1)
    weight_block = jnp.zeros((slot_count, LANE), jnp.float32).at[:, 0].set(send_weight)
    payload = jnp.concatenate([tokens, out_grad], axis=1)
    send_rows = jnp.dot(tok_match, payload, preferred_element_type=jnp.float32)
    send_rows = jnp.concatenate([send_rows, weight_block], axis=1).astype(jnp.bfloat16)
    send_rows = send_rows.reshape(experts, capacity, 2 * model_width + LANE)

    full_down = lax.all_gather(down, "dp", axis=1, tiled=True)[0]
    gu_parts = [
        lax.all_gather(
            gate_up[:, :, :, h * part_ffw:(h + 1) * part_ffw], "dp", axis=3, tiled=True
        )[0]
        for h in range(HALVES)
    ]

    recv_rows = lax.all_to_all(send_rows, "expert", split_axis=0, concat_axis=0, tiled=True)
    recv_rows = recv_rows.reshape(slot_count, 2 * model_width + LANE)
    xs_rows = recv_rows[:, :model_width]
    gs_rows = recv_rows[:, model_width:2 * model_width]
    slot_weight = recv_rows[:, 2 * model_width].astype(jnp.float32)

    back_full = contract_last(gs_rows, full_down)
    back_full = back_full.reshape(slot_count, data_ways, HALVES, part_ffw)
    scaled = (slot_weight[:, None] * gs_rows.astype(jnp.float32)).astype(jnp.bfloat16)

    grad_parts = []
    affinity = jnp.zeros((slot_count,), jnp.float32)
    route_acc = jnp.zeros((slot_count, model_width), jnp.float32)
    for h in range(HALVES):
        gate_w = gu_parts[h][0]
        up_w = gu_parts[h][1]
        back_raw = back_full[:, :, h, :].reshape(slot_count, data_ways * part_ffw)
        pre_gate = jnp.dot(xs_rows, gate_w, preferred_element_type=jnp.float32)
        pre_up = jnp.dot(xs_rows, up_w, preferred_element_type=jnp.float32)
        sig_gate = jax.nn.sigmoid(pre_gate)
        silu_gate = pre_gate * sig_gate
        hidden = (silu_gate * pre_up).astype(jnp.bfloat16)
        affinity = affinity + jnp.sum(hidden.astype(jnp.float32) * back_raw, axis=1)
        local_grad = contract_first(hidden, scaled)
        grad_parts.append(
            lax.psum_scatter(local_grad.astype(jnp.bfloat16), "dp", scatter_dimension=0, tiled=True)
        )
        back = slot_weight[:, None] * back_raw
        gate_grad = (back * pre_up * sig_gate * (1.0 + pre_gate * (1.0 - sig_gate))).astype(
            jnp.bfloat16
        )
        up_grad = (back * silu_gate).astype(jnp.bfloat16)
        route_acc = route_acc + contract_last(gate_grad, gate_w) + contract_last(up_grad, up_w)

    affinity_block = jnp.zeros((slot_count, LANE), jnp.float32).at[:, 0].set(
        affinity.astype(jnp.bfloat16).astype(jnp.float32)
    )
    ret_rows = jnp.concatenate([route_acc.astype(jnp.bfloat16).astype(jnp.float32), affinity_block], axis=1)
    ret_rows = ret_rows.astype(jnp.bfloat16).reshape(experts, capacity, model_width + LANE)
    back_rows = lax.all_to_all(ret_rows, "expert", split_axis=0, concat_axis=0, tiled=True)
    back_rows = back_rows.reshape(slot_count, model_width + LANE)
    token_grad = contract_first(tok_match, back_rows[:, :model_width]).astype(jnp.bfloat16)
    back_affinity = back_rows[:, model_width].astype(jnp.float32)
    route_affinity = jnp.sum(matched * back_affinity[:, None], axis=0)
    route_affinity = route_affinity.reshape(tok_rows, top_count)
    mixed = jnp.sum(route_affinity * scores, axis=1, keepdims=True) / score_sum
    router_grad = ROUTE_SCALE * scores * (1.0 - scores) * (route_affinity - mixed) / score_sum

    grad_shard = jnp.concatenate(grad_parts, axis=0).astype(jnp.float32)
    down_grad = (grad_shard / data_ways)[None]
    corr_one = 1.0 - BETA_ONE**STEP
    corr_two = 1.0 - BETA_TWO**STEP
    down_wide = down.astype(jnp.float32)
    first = BETA_ONE * moment1.astype(jnp.float32) + (1.0 - BETA_ONE) * down_grad
    second = BETA_TWO * moment2.astype(jnp.float32) + (1.0 - BETA_TWO) * down_grad * down_grad
    update = first / corr_one / (jnp.sqrt(second / corr_two) + EPSILON) + DECAY * down_wide
    new_down = (down_wide - LEARN_RATE * update).astype(jnp.bfloat16)
    return (
        token_grad,
        router_grad,
        new_down,
        first.astype(jnp.bfloat16),
        second.astype(jnp.bfloat16),
    )


def solution(mesh):
    placed = (
        P(("expert", "dp"), None),
        P(("expert", "dp"), None),
        P(("expert", "dp"), None),
        P(("expert", "dp"), None),
        P("expert", None, None, "dp"),
        P("expert", "dp", None),
        P("expert", "dp", None),
        P("expert", "dp", None),
    )
    return jax.shard_map(
        shards,
        mesh=mesh,
        in_specs=placed,
        out_specs=(
            P(("expert", "dp"), None),
            P(("expert", "dp"), None),
            P("expert", "dp", None),
            P("expert", "dp", None),
            P("expert", "dp", None),
        ),
        check_vma=False,
    )
```

time: 415 us -> 412 us (level)
  local copies, waits for them, and re-layouts: 45.1 us -> 9.74 us
  matrix products: 80.6 us -> 101 us
  waiting for transfers between devices: 165 us -> 180 us
  other arithmetic: 10.7 us -> 22 us
  starting transfers between devices: 16.6 us -> 9.23 us
  blocking collectives: 81 us -> 75.7 us
    reshape x4 -> x0, local copies, waits for them, and re-layouts: 41.7 us -> none  [the longest x1 13.7 us: shards(): send_rows = send_rows.reshape(experts, capacity, 2 * model_width)]
    all_gather x2 -> x3, waiting for transfers between devices: 25.8 us -> 44.6 us  [the longest x2 44.5 us: shards(): lax.all_gather(gate_up[:, :, :, h * part_ffw:(h + 1) * part_ffw], 'dp', a...]
    dot_general x1 -> x2, matrix products: 6.38 us -> 15.3 us  [shards(): pre_up = jnp.dot(xs_rows, up_w, preferred_element_type=jnp.float32)]
    concatenate x0 -> x2, other arithmetic: none -> 7.97 us  [the longest x1 4.99 us: shards(): jnp.concatenate([send_rows, weight_block], axis=1).astype(jnp.bfloat16)]
    all_to_all x1 -> x0, starting transfers between devices: 7.7 us -> none  [shards(): lax.all_to_all(affinity.reshape(experts, capacity), 'expert', split_axis=...]
    all_to_all x1 -> x0, waiting for transfers between devices: 6.83 us -> none  [shards(): lax.all_to_all(affinity.reshape(experts, capacity), 'expert', split_axis=...]
    dot_general x3 -> x5, matrix products: 42.3 us -> 47.8 us  [contract_last(): lax.dot_general(left, right, (((1,), (1,)), ((), ())), preferred_element_...]
    all_to_all x2 -> x1, blocking collectives: 81 us -> 75.7 us  [shards(): lax.all_to_all(ret_rows, 'expert', split_axis=0, concat_axis=0, tiled=True)]
  transfers between devices with their start and end apart: 5 -> 6, of which waited for: 3 -> 2; matrix products, arithmetic and copies ran while one was open for 25% -> 29% of each run, Pallas kernels for 0% -> 0%
where the time goes in v1:
time: 412 us; the launch traced here: 411 us
  waiting for transfers between devices  180 us (44%)
  matrix products  101 us (25%)
  blocking collectives  75.7 us (18%)
  other arithmetic  22 us (5%)
  between operations  14.1 us (3%)
  local copies, waits for them, and re-layouts  9.74 us (2%)
  starting transfers between devices  9.23 us (2%)
    all_to_all x1, waiting for transfers between devices, shards(): lax.all_to_all(send_rows, 'expert', split_axis=0, concat_axis=0, tiled=True)  134 us
    all_to_all x1, blocking collectives, shards(): lax.all_to_all(ret_rows, 'expert', split_axis=0, concat_axis=0, tiled=True)  75.7 us
    dot_general x5, matrix products, contract_last(): lax.dot_general(left, right, (((1,), (1,)), ((), ())), preferred_element_...  47.8 us
    all_gather x2, waiting for transfers between devices, shards(): lax.all_gather(gate_up[:, :, :, h * part_ffw:(h + 1) * part_ffw], 'dp', a...  44.5 us
    dot_general x3, matrix products, contract_first(): lax.dot_general(left, right, (((0,), (0,)), ((), ())), preferred_element_...  19.4 us
    dot_general x2, matrix products, shards(): pre_up = jnp.dot(xs_rows, up_w, preferred_element_type=jnp.float32)  15.3 us
    dot_general x2, matrix products, shards(): pre_gate = jnp.dot(xs_rows, gate_w, preferred_element_type=jnp.float32)  14.8 us
    all_to_all x1, starting transfers between devices, shards(): lax.all_to_all(send_rows, 'expert', split_axis=0, concat_axis=0, tiled=True)  8.63 us
  transfers between devices with their start and end apart: 6, of which 2 were waited for; matrix products, arithmetic and copies ran while one was open for 29% of the time, Pallas kernels for 0%

profile of v1, /device:TPU:1, one launch (start us, length us, event | category | flops | bytes accessed | tf_op | source)
XLA Modules:
  0.0 411.3 jit_solution(7383616715635387772)
XLA Ops:
  7.2 0.7 all-gather.4.cloned.1.call-update
  8.0 4.2 %fusion.43 = (bf16[1,2,3584,128]{3,2,1,0:T(8,128)(2,1)}, bf16[1,2,3584,128]{3,2,1,0:T(8,128)(2,1)}) fusion(bf16[1,2,3584,256]{3,2,1,0:T(8,128)(2,1)} %param.16), kind=kLoop, calls=%fused_computation.92 | loop fusion | bytes 7340032 | tf_op jit(solution)/shard_map/slice | solution.py:65
  12.5 1.2 reduce-window.6
  14.4 0.6 compare_reduce_fusion
  15.3 0.7 select_convert_fusion.1
  16.3 0.5 convert_reduce_fusion
  16.9 3.3 convolution_convert_fusion
  20.1 5.0 %pad_maximum_fusion = bf16[32,24,7296]{2,1,0:T(8,128)(2,1)} fusion(bf16[32,24,128]{2,1,0:T(8,128)(2,1)S(1)} %bitcast.86, bf16[32,24,7168]{2,1,0:T(8,128)(2,1)S(1)} %bitcast.80), kind=kLoop, calls=%fused_computation.1 | loop fusion | flops 22413312 | bytes 22413312 | tf_op jit(solution)/shard_map/concatenate | solution.py:59
  25.1 8.6 %all-to-all-start = ((bf16[32,24,7296]{2,1,0:T(8,128)(2,1)}), bf16[32,24,7296]{2,1,0:T(8,128)(2,1)}, u32[]{:S(2)}, u32[]{:S(2)}) async-start(bf16[32,24,7296]{2,1,0:T(8,128)(2,1)} %pad_maximum_fusion), calls=%async_computation | async-start | bytes 22413312 | tf_op jit(solution)/shard_map/all_to_all | solution.py:70
  33.8 0.7 all-gather.6.cloned.1.call-update
  34.7 134.1 %all-to-all-done = bf16[32,24,7296]{2,1,0:T(8,128)(2,1)} async-done(((bf16[32,24,7296]{2,1,0:T(8,128)(2,1)}), bf16[32,24,7296]{2,1,0:T(8,128)(2,1)}, u32[]{:S(2)}, u32[]{:S(2)}) %all-to-all-start) | async-done | bytes 11206688 | tf_op jit(solution)/shard_map/all_to_all | solution.py:70
  168.8 1.1 convert_reduce_fusion.2
  169.9 9.8 %fusion.2 = f32[768,4,2,128]{0,3,2,1:T(8,128)S(1)} fusion(bf16[4,2,128,3584]{3,2,1,0:T(8,128)(2,1)} %bitcast.88, bf16[768,7296]{1,0:T(8,128)(2,1)} %bitcast.3), kind=kOutput, calls=%fused_computation.9 | convolution fusion | flops 5637144576 | bytes 15990784 | tf_op jit(solution)/shard_map/dot_general | solution.py:20
  180.1 7.8 %fusion.14 = f32[768,512]{0,1:T(8,128)S(1)} fusion(bf16[768,7296]{1,0:T(8,128)(2,1)} %bitcast.3, bf16[1,2,3584,512]{3,2,1,0:T(8,128)(2,1)} %all-gather.8.cloned.1.call-done), kind=kOutput, calls=%fused_computation.28 | convolution fusion | flops 2818572288 | bytes 10747904 | tf_op jit(solution)/shard_map/dot_general | solution.py:87
  188.0 7.7 %fusion.27 = (f32[768]{0:T(1024)S(1)}, bf16[768,512]{0,1:T(8,128)(2,1)S(1)}, bf16[768,512]{0,1:T(8,128)(2,1)}, bf16[768,512]{0,1:T(8,128)(2,1)}) fusion(f32[768,4,1,128]{0,3,2,1:T(8,128)S(1)} %get-tuple-element.57, f32[768,512]{0,1:T(8,128)S(1)} %fusion.14, f32[768]{0:T(1024)S(1)} %convert_reduce_fusion.2, bf16[1,2,3584,512]{3,2,1,0:T(8,128)(2,1)S(1)} %copy-done.2, ...), kind=kOutput, calls=%fused_computation.44 | convolution fusion | flops 2826042624 | bytes 14687232 | tf_op jit(solution)/shard_map/dot_general | solution.py:88
  195.6 7.5 %convolution_convert_fusion.1 = bf16[512,3584]{1,0:T(8,128)(2,1)} fusion(bf16[768,512]{0,1:T(8,128)(2,1)S(1)} %get-tuple-element.45, f32[768]{0:T(1024)S(1)} %convert_reduce_fusion.2, bf16[768,7296]{1,0:T(8,128)(2,1)} %bitcast.3), kind=kOutput, calls=%fused_computation.4 | convolution fusion | flops 2828664832 | bytes 9964544 | tf_op jit(solution)/shard_map/dot_general | solution.py:26
  203.5 44.5 %all-gather.6.cloned.1.call-done = bf16[1,2,3584,512]{3,2,1,0:T(8,128)(2,1)} async-done(((bf16[1,2,3584,128]{3,2,1,0:T(8,128)(2,1)}), bf16[1,2,3584,512]{3,2,1,0:T(8,128)(2,1)}) %all-gather.6.cloned.1.call-update) | async-done | bytes 7340048 | tf_op jit(solution)/shard_map/all_gather | solution.py:64
  248.0 6.9 %fusion.18 = f32[768,512]{0,1:T(8,128)S(1)} fusion(bf16[768,7296]{1,0:T(8,128)(2,1)} %bitcast.3, bf16[1,2,3584,512]{3,2,1,0:T(8,128)(2,1)} %all-gather.6.cloned.1.call-done), kind=kOutput, calls=%fused_computation.32 | convolution fusion | flops 2818572288 | bytes 10747904 | tf_op jit(solution)/shard_map/dot_general | solution.py:87
  254.9 7.6 %fusion.28 = (f32[768]{0:T(1024)S(1)}, bf16[768,512]{0,1:T(8,128)(2,1)S(1)}, bf16[768,512]{0,1:T(8,128)(2,1)}, bf16[768,512]{0,1:T(8,128)(2,1)}) fusion(f32[768,4,1,128]{0,3,2,1:T(8,128)S(1)} %get-tuple-element.58, f32[768,512]{0,1:T(8,128)S(1)} %fusion.18, f32[768]{0:T(1024)S(1)} %convert_reduce_fusion.2, bf16[1,2,3584,512]{3,2,1,0:T(8,128)(2,1)S(1)} %copy-done.8, ...), kind=kOutput, calls=%fused_computation.47 | convolution fusion | flops 2826042624 | bytes 14687232 | tf_op jit(solution)/shard_map/dot_general | solution.py:88
  262.5 7.5 %convolution_convert_fusion.2 = bf16[512,3584]{1,0:T(8,128)(2,1)} fusion(bf16[768,512]{0,1:T(8,128)(2,1)S(1)} %get-tuple-element.47, f32[768]{0:T(1024)S(1)} %convert_reduce_fusion.2, bf16[768,7296]{1,0:T(8,128)(2,1)} %bitcast.3), kind=kOutput, calls=%fused_computation.5 | convolution fusion | flops 2828664832 | bytes 9964544 | tf_op jit(solution)/shard_map/dot_general | solution.py:26
  270.1 1.1 copy-done.9
  271.2 8.2 %fusion.24 = f32[768,3584]{1,0:T(8,128)} fusion(bf16[768,512]{0,1:T(8,128)(2,1)S(1)} %copy-done.9, bf16[1,2,3584,512]{3,2,1,0:T(8,128)(2,1)} %all-gather.8.cloned.1.call-done), kind=kOutput, calls=%fused_computation.38 | convolution fusion | flops 2818572288 | bytes 15466496 | tf_op jit(solution)/shard_map/dot_general | solution.py:20
  279.3 8.1 %fusion.22 = f32[768,3584]{1,0:T(8,128)} fusion(bf16[768,512]{0,1:T(8,128)(2,1)S(1)} %copy-done.11, bf16[1,2,3584,512]{3,2,1,0:T(8,128)(2,1)} %all-gather.6.cloned.1.call-done), kind=kOutput, calls=%fused_computation.36 | convolution fusion | flops 2818572288 | bytes 15466496 | tf_op jit(solution)/shard_map/dot_general | solution.py:20
  287.4 5.8 %fusion.23 = f32[768,3584]{1,0:T(8,128)} fusion(bf16[768,512]{0,1:T(8,128)(2,1)S(1)} %copy-done.10, bf16[1,2,3584,512]{3,2,1,0:T(8,128)(2,1)S(1)} %bitcast.90), kind=kOutput, calls=%fused_computation.37 | convolution fusion | flops 2818572288 | bytes 15466496 | tf_op jit(solution)/shard_map/dot_general | solution.py:20
  293.2 15.9 %add_convert_fusion = bf16[768,3584]{1,0:T(8,128)(2,1)} fusion(f32[768,3584]{1,0:T(8,128)} %fusion.24, f32[768,3584]{1,0:T(8,128)} %fusion.23, f32[768,3584]{1,0:T(8,128)} %fusion.22, bf16[768,512]{0,1:T(8,128)(2,1)S(1)} %copy-done.3, bf16[1,2,3584,512]{3,2,1,0:T(8,128)(2,1)} %all-gather.8.cloned.1.call-done), kind=kOutput, calls=%fused_computation.3 | convolution fusion | flops 2829582336 | bytes 42991616 | tf_op jit(solution)/shard_map/dot_general | solution.py:20
  309.2 0.6 select_convert_fusion
  310.1 3.0 pad_maximum_fusion.1
  313.0 75.7 %all_to_all.10 = bf16[32,24,3712]{2,1,0:T(8,128)(2,1)S(1)} all-to-all(bf16[32,24,3712]{2,1,0:T(8,128)(2,1)S(1)} %pad_maximum_fusion.1), channel_id=1, replica_groups=mesh['expert'=32,'dp'=4] {'expert'}, dimensions={0} | all-to-all | bytes 11403264 | tf_op jit(solution)/shard_map/all_to_all | solution.py:109
  388.8 2.5 copy-done.1
  391.9 0.6 multiply_divide_fusion
  392.6 4.4 %fusion.5 = bf16[64,3584]{1,0:T(8,128)(2,1)} fusion(bf16[768,3712]{1,0:T(8,128)(2,1)} %bitcast.83, bf16[768,64]{0,1:T(8,128)(2,1)S(1)} %convert_reduce_fusion), kind=kOutput, calls=%fused_computation.15 | convolution fusion | flops 352550912 | bytes 6062080 | tf_op jit(solution)/shard_map/dot_general | solution.py:26
  397.0 7.8 %fusion.26 = (bf16[1,256,3584]{2,1,0:T(8,128)(2,1)}, bf16[1,256,3584]{2,1,0:T(8,128)(2,1)}, bf16[1,256,3584]{2,1,0:T(8,128)(2,1)}) fusion(bf16[1,256,3584]{2,1,0:T(8,128)(2,1)} %param.19, bf16[1,128,3584]{2,1,0:T(8,128)(2,1)} %bitcast.84, bf16[1,128,3584]{2,1,0:T(8,128)(2,1)} %bitcast.85, bf16[1,256,3584]{2,1,0:T(8,128)(2,1)} %param.18, ...), kind=kLoop, calls=%fused_computation.40 | loop fusion | flops 23855104 | bytes 12845056 | tf_op jit(solution)/shard_map/convert_element_type | solution.py:132
  (68 shorter events, 3.5 us)
Async XLA Ops:
  7.2 162.7 %all-gather.4.cloned.1.call-start = ((), (), s32[]{:S(2)}) async-start(), calls=%async_computation.4 | async-start | bytes 9175040 | tf_op jit(solution)/shard_map/all_gather | solution.py:62
  7.9 4.3 %copy-start.7 = (s32[64,8]{0,1:T(8,128)S(1)}, s32[64,8]{0,1:T(8,128)}, u32[]{:S(2)}) copy-start(s32[64,8]{0,1:T(8,128)} %param.14) | copy-start | bytes 6148
  7.9 6.0 %copy-start.6 = (f32[64,8]{0,1:T(8,128)S(1)}, f32[64,8]{0,1:T(8,128)}, u32[]{:S(2)}) copy-start(f32[64,8]{0,1:T(8,128)} %param.15) | copy-start | bytes 6148
  7.9 8.9 %copy-start.4 = (bf16[64,3584]{1,0:T(8,128)(2,1)S(1)}, bf16[64,3584]{1,0:T(8,128)(2,1)}, u32[]{:S(2)}) copy-start(bf16[64,3584]{1,0:T(8,128)(2,1)} %param.13) | copy-start | bytes 1376260
  7.9 8.9 %copy-start.5 = (bf16[64,3584]{1,0:T(8,128)(2,1)S(1)}, bf16[64,3584]{1,0:T(8,128)(2,1)}, u32[]{:S(2)}) copy-start(bf16[64,3584]{1,0:T(8,128)(2,1)} %param.12) | copy-start | bytes 1376260
  7.9 172.1 %all-gather.8.cloned.1.call-start = ((), (), s32[]{:S(2)}) async-start(), calls=%async_computation.6 | async-start | bytes 9175040 | tf_op jit(solution)/shard_map/all_gather | solution.py:64
  25.1 143.7 %all-to-all-start = ((bf16[32,24,7296]{2,1,0:T(8,128)(2,1)}), bf16[32,24,7296]{2,1,0:T(8,128)(2,1)}, u32[]{:S(2)}, u32[]{:S(2)}) async-start(bf16[32,24,7296]{2,1,0:T(8,128)(2,1)} %pad_maximum_fusion), calls=%async_computation | async-start | bytes 22413312 | tf_op jit(solution)/shard_map/all_to_all | solution.py:70
  33.8 214.2 %all-gather.6.cloned.1.call-start = ((), (), s32[]{:S(2)}) async-start(), calls=%async_computation.5 | async-start | bytes 9175040 | tf_op jit(solution)/shard_map/all_gather | solution.py:64
  34.5 362.5 %reduce-scatter.5.cloned.1.call-start = ((), (), s32[]{:S(2)}) async-start(), calls=%async_computation.8 | async-start | bytes 4587520 | tf_op jit(solution)/shard_map/reduce_scatter | solution.py:95
  180.1 7.9 %copy-start.2 = (bf16[1,2,3584,512]{3,2,1,0:T(8,128)(2,1)S(1)}, bf16[1,2,3584,512]{3,2,1,0:T(8,128)(2,1)}, u32[]{:S(2)}) copy-start(bf16[1,2,3584,512]{3,2,1,0:T(8,128)(2,1)} %all-gather.8.cloned.1.call-done) | copy-start | bytes 22020100
  203.2 193.8 %reduce-scatter.3.cloned.1.call-start = ((), (), s32[]{:S(2)}) async-start(), calls=%async_computation.7 | async-start | bytes 4587520 | tf_op jit(solution)/shard_map/reduce_scatter | solution.py:95
  248.0 6.9 %copy-start.8 = (bf16[1,2,3584,512]{3,2,1,0:T(8,128)(2,1)S(1)}, bf16[1,2,3584,512]{3,2,1,0:T(8,128)(2,1)}, u32[]{:S(2)}) copy-start(bf16[1,2,3584,512]{3,2,1,0:T(8,128)(2,1)} %all-gather.6.cloned.1.call-done) | copy-start | bytes 22020100
  270.0 1.1 copy-start.9
  271.2 8.2 %copy-start.11 = (bf16[768,512]{0,1:T(8,128)(2,1)S(1)}, bf16[768,512]{0,1:T(8,128)(2,1)}, u32[]{:S(2)}) copy-start(bf16[768,512]{0,1:T(8,128)(2,1)} %get-tuple-element.56) | copy-start | bytes 2359300
  271.2 16.2 %slice-start = ((s8[7340032]{0:T(1024)(128)(4,1)}), s8[4194304]{0:T(1024)(128)(4,1)S(1)}, s32[]{:S(2)}) async-start(s8[7340032]{0:T(1024)(128)(4,1)} %bitcast.89), calls=%async_computation.9 | async-start | bytes 8388608
  279.3 8.1 %slice-start.1 = ((s8[7340032]{0:T(1024)(128)(4,1)}), s8[3145728]{0:T(1024)(128)(4,1)S(1)}, s32[]{:S(2)}) async-start(s8[7340032]{0:T(1024)(128)(4,1)} %bitcast.89), calls=%async_computation.10 | async-start | bytes 6291456
  279.3 8.1 %copy-start.10 = (bf16[768,512]{0,1:T(8,128)(2,1)S(1)}, bf16[768,512]{0,1:T(8,128)(2,1)}, u32[]{:S(2)}) copy-start(bf16[768,512]{0,1:T(8,128)(2,1)} %get-tuple-element.48) | copy-start | bytes 2359300
  287.4 5.8 %copy-start.3 = (bf16[768,512]{0,1:T(8,128)(2,1)S(1)}, bf16[768,512]{0,1:T(8,128)(2,1)}, u32[]{:S(2)}) copy-start(bf16[768,512]{0,1:T(8,128)(2,1)} %get-tuple-element.55) | copy-start | bytes 2359300
  388.8 2.6 copy-start.1
  388.8 8.2 %copy-start = (bf16[1,256,3584]{2,1,0:T(8,128)(2,1)S(1)}, bf16[1,256,3584]{2,1,0:T(8,128)(2,1)}, u32[]{:S(2)}) copy-start(bf16[1,256,3584]{2,1,0:T(8,128)(2,1)} %param.17) | copy-start | bytes 5505028
Sparse Core Ops, SparseCore 0:
  9.6 77.5 all-gather.3
  89.5 77.6 all-gather.7
  169.4 78.5 all-gather.5
  250.3 44.3 reduce-scatter.4
  297.0 42.3 reduce-scatter.2

commit v2 on v0

--- a/solution.py
+++ b/solution.py
@@ -32,6 +32,8 @@
     tok_rows, model_width = tokens.shape
     top_count = route_ids.shape[1]
     capacity = min(tok_rows, max(2, 5 * tok_rows * top_count // (4 * experts)))
+    side_row = capacity
+    capacity = -(-(capacity + 1) // 8) * 8
     slot_count = experts * capacity
     scores = jax.nn.sigmoid(route_logits)
     score_sum = jnp.sum(scores, axis=1, keepdims=True)
@@ -47,38 +49,37 @@
     tok_match = jnp.sum(matched.reshape(slot_count, tok_rows, top_count), axis=2).astype(
         jnp.bfloat16
     )
+    send_weight = jnp.sum(matched * route_weight.astype(jnp.float32).reshape(-1)[None, :], axis=1)
     payload = jnp.concatenate([tokens, out_grad], axis=1)
     send_rows = jnp.dot(tok_match, payload, preferred_element_type=jnp.float32).astype(jnp.bfloat16)
     send_rows = send_rows.reshape(experts, capacity, 2 * model_width)
-    send_weight = jnp.sum(matched * route_weight.astype(jnp.float32).reshape(-1)[None, :], axis=1)
-    send_weight = send_weight.astype(jnp.bfloat16).reshape(experts, capacity)
-    recv_rows, recv_weight = (
-        lax.all_to_all(send_rows, "expert", split_axis=0, concat_axis=0, tiled=True),
-        lax.all_to_all(send_weight, "expert", split_axis=0, concat_axis=0, tiled=True),
+    send_rows = send_rows.at[:, side_row, :capacity].set(
+        send_weight.astype(jnp.bfloat16).reshape(experts, capacity)
     )
+
+    full_gu = lax.all_gather(gate_up, "dp", axis=3, tiled=True)[0]
+    full_down = lax.all_gather(down, "dp", axis=1, tiled=True)[0]
+
+    recv_rows = lax.all_to_all(send_rows, "expert", split_axis=0, concat_axis=0, tiled=True)
+    slot_weight = recv_rows[:, side_row, :capacity].reshape(slot_count).astype(jnp.float32)
     recv_rows = recv_rows.reshape(slot_count, 2 * model_width)
     xs_rows = recv_rows[:, :model_width]
     gs_rows = recv_rows[:, model_width:]
-    slot_weight = recv_weight.reshape(slot_count).astype(jnp.float32)
-    full_gu, full_down = (
-        lax.all_gather(gate_up, "dp", axis=3, tiled=True),
-        lax.all_gather(down, "dp", axis=1, tiled=True),
-    )
-    back_raw = contract_last(gs_rows, full_down[0])
-    gate_w = full_gu[0, 0]
-    up_w = full_gu[0, 1]
+
+    gate_w = full_gu[0]
+    up_w = full_gu[1]
     pre_gate = jnp.dot(xs_rows, gate_w, preferred_element_type=jnp.float32)
     pre_up = jnp.dot(xs_rows, up_w, preferred_element_type=jnp.float32)
     sig_gate = jax.nn.sigmoid(pre_gate)
     silu_gate = pre_gate * sig_gate
     hidden = (silu_gate * pre_up).astype(jnp.bfloat16)
-    affinity = jnp.sum(hidden.astype(jnp.float32) * back_raw, axis=1).astype(jnp.bfloat16)
     scaled = (slot_weight[:, None] * gs_rows.astype(jnp.float32)).astype(jnp.bfloat16)
     local_grad = contract_first(hidden, scaled)
     grad_shard = lax.psum_scatter(
         local_grad.astype(jnp.bfloat16), "dp", scatter_dimension=0, tiled=True
     ).astype(jnp.float32)
-    down_grad = (grad_shard / data_ways)[None]
+    back_raw = contract_last(gs_rows, full_down)
+    affinity = jnp.sum(hidden.astype(jnp.float32) * back_raw, axis=1).astype(jnp.bfloat16)
     back = slot_weight[:, None] * back_raw
     gate_grad = (back * pre_up * sig_gate * (1.0 + pre_gate * (1.0 - sig_gate))).astype(
         jnp.bfloat16
@@ -87,26 +88,18 @@
     route_in = (contract_last(gate_grad, gate_w) + contract_last(up_grad, up_w)).astype(
         jnp.bfloat16
     )
-    back_rows, back_affinity = (
-        lax.all_to_all(
-            route_in.reshape(experts, capacity, model_width),
-            "expert",
-            split_axis=0,
-            concat_axis=0,
-            tiled=True,
-        ),
-        lax.all_to_all(
-            affinity.reshape(experts, capacity), "expert", split_axis=0, concat_axis=0, tiled=True
-        ),
-    )
+    ret_rows = route_in.reshape(experts, capacity, model_width)
+    ret_rows = ret_rows.at[:, side_row, :capacity].set(affinity.reshape(experts, capacity))
+    back_rows = lax.all_to_all(ret_rows, "expert", split_axis=0, concat_axis=0, tiled=True)
+    back_affinity = back_rows[:, side_row, :capacity].reshape(slot_count).astype(jnp.float32)
     back_rows = back_rows.reshape(slot_count, model_width)
     token_grad = contract_first(tok_match, back_rows).astype(jnp.bfloat16)
-    route_affinity = jnp.sum(
-        matched * back_affinity.reshape(slot_count, 1).astype(jnp.float32), axis=0
-    )
+    route_affinity = jnp.sum(matched * back_affinity[:, None], axis=0)
     route_affinity = route_affinity.reshape(tok_rows, top_count)
     mixed = jnp.sum(route_affinity * scores, axis=1, keepdims=True) / score_sum
     router_grad = ROUTE_SCALE * scores * (1.0 - scores) * (route_affinity - mixed) / score_sum
+
+    down_grad = (grad_shard / data_ways)[None]
     corr_one = 1.0 - BETA_ONE**STEP
     corr_two = 1.0 - BETA_TWO**STEP
     down_wide = down.astype(jnp.float32)

time: 415 us -> 379 us (0.913)
  local copies, waits for them, and re-layouts: 45.1 us -> 7.6 us
  waiting for transfers between devices: 165 us -> 181 us
  blocking collectives: 81 us -> 72.7 us
  starting transfers between devices: 16.6 us -> 8.92 us
    reshape x4 -> x0, local copies, waits for them, and re-layouts: 41.7 us -> none  [the longest x1 13.7 us: shards(): send_rows = send_rows.reshape(experts, capacity, 2 * model_width)]
    all_gather x2, waiting for transfers between devices: 25.8 us -> 48.4 us  [the longest x1 48.3 us: shards(): full_down = lax.all_gather(down, 'dp', axis=1, tiled=True)[0]]
    all_to_all x2 -> x1, blocking collectives: 81 us -> 72.7 us  [shards(): lax.all_to_all(ret_rows, 'expert', split_axis=0, concat_axis=0, tiled=True)]
    all_to_all x1 -> x0, starting transfers between devices: 7.7 us -> none  [shards(): lax.all_to_all(affinity.reshape(experts, capacity), 'expert', split_axis=...]
    all_to_all x1 -> x0, waiting for transfers between devices: 6.83 us -> none  [shards(): lax.all_to_all(affinity.reshape(experts, capacity), 'expert', split_axis=...]
  transfers between devices with their start and end apart: 5 -> 4, of which waited for: 3 -> 2; matrix products, arithmetic and copies ran while one was open for 25% -> 18% of each run, Pallas kernels for 0% -> 0%
where the time goes in v2:
time: 379 us; the launch traced here: 378 us
  waiting for transfers between devices  181 us (48%)
  matrix products  82.2 us (22%)
  blocking collectives  72.7 us (19%)
  between operations  13.9 us (4%)
  other arithmetic  11.7 us (3%)
  starting transfers between devices  8.92 us (2%)
  local copies, waits for them, and re-layouts  7.6 us (2%)
    all_to_all x1, waiting for transfers between devices, shards(): lax.all_to_all(send_rows, 'expert', split_axis=0, concat_axis=0, tiled=True)  131 us
    all_to_all x1, blocking collectives, shards(): lax.all_to_all(ret_rows, 'expert', split_axis=0, concat_axis=0, tiled=True)  72.7 us
    all_gather x1, waiting for transfers between devices, shards(): full_down = lax.all_gather(down, 'dp', axis=1, tiled=True)[0]  48.3 us
    dot_general x3, matrix products, contract_last(): lax.dot_general(left, right, (((1,), (1,)), ((), ())), preferred_element_...  40.8 us
    dot_general x2, matrix products, contract_first(): lax.dot_general(left, right, (((0,), (0,)), ((), ())), preferred_element_...  15.3 us
    dot_general x1, matrix products, shards(): pre_gate = jnp.dot(xs_rows, gate_w, preferred_element_type=jnp.float32)  11.3 us
    dot_general x1, matrix products, shards(): pre_up = jnp.dot(xs_rows, up_w, preferred_element_type=jnp.float32)  8.95 us
    all_to_all x1, starting transfers between devices, shards(): lax.all_to_all(send_rows, 'expert', split_axis=0, concat_axis=0, tiled=True)  8.63 us
  transfers between devices with their start and end apart: 4, of which 2 were waited for; matrix products, arithmetic and copies ran while one was open for 18% of the time, Pallas kernels for 0%

profile of v2, /device:TPU:1, one launch (start us, length us, event | category | flops | bytes accessed | tf_op | source)
XLA Modules:
  0.0 378.2 jit_solution(2949747389659827211)
XLA Ops:
  7.3 0.7 all-gather.5.cloned.1.call-update
  8.0 0.1 eq.50
  8.2 1.2 reduce-window.6
  9.4 0.2 slice_reduce_fusion
  9.8 0.1 reshape.187
  9.9 0.1 fusion.30
  10.0 0.1 reduce_sum.66
  10.1 0.2 select_reduce_fusion.1
  10.4 0.1 convert_element_type.147
  10.6 0.5 convert_reduce_fusion
  11.2 5.8 %convolution_convert_fusion = bf16[768,7168]{1,0:T(8,128)(2,1)} fusion(bf16[64,3584]{1,0:T(8,128)(2,1)S(1)} %copy-done.2, bf16[64,3584]{1,0:T(8,128)(2,1)S(1)} %copy-done.3, bf16[768,64]{0,1:T(8,128)(2,1)S(1)} %convert_reduce_fusion), kind=kOutput, calls=%fused_computation | convolution fusion | flops 711983104 | bytes 12025856 | tf_op jit(solution)/shard_map/dot_general | solution.py:54
  17.0 1.9 scatter.6
  18.8 8.6 %all-to-all-start = ((bf16[32,24,7168]{2,1,0:T(8,128)(2,1)}), bf16[32,24,7168]{2,1,0:T(8,128)(2,1)}, u32[]{:S(2)}, u32[]{:S(2)}) async-start(bf16[32,24,7168]{2,1,0:T(8,128)(2,1)} %scatter.6), calls=%async_computation | async-start | bytes 22020096 | tf_op jit(solution)/shard_map/all_to_all | solution.py:63
  27.5 0.7 all-gather.3.cloned.1.call-update
  28.2 0.2 reduce-scatter.2.cloned.1.call-start
  28.5 131.3 %all-to-all-done = bf16[32,24,7168]{2,1,0:T(8,128)(2,1)} async-done(((bf16[32,24,7168]{2,1,0:T(8,128)(2,1)}), bf16[32,24,7168]{2,1,0:T(8,128)(2,1)}, u32[]{:S(2)}, u32[]{:S(2)}) %all-to-all-start) | async-done | bytes 11010080 | tf_op jit(solution)/shard_map/all_to_all | solution.py:63
  159.8 0.9 fusion.35
  160.8 11.3 %fusion.4 = f32[768,1024]{1,0:T(8,128)} fusion(bf16[1,2,3584,1024]{3,2,1,0:T(8,128)(2,1)} %all-gather.5.cloned.1.call-done, bf16[768,7168]{1,0:T(8,128)(2,1)} %bitcast.2), kind=kOutput, calls=%fused_computation.10 | convolution fusion | flops 5637144576 | bytes 15990784 | tf_op jit(solution)/shard_map/dot_general | solution.py:71
  172.1 9.0 %fusion.2 = f32[768,1024]{1,0:T(8,128)} fusion(bf16[1,2,3584,1024]{3,2,1,0:T(8,128)(2,1)S(1)} %copy-done.6, bf16[768,7168]{1,0:T(8,128)(2,1)} %bitcast.2), kind=kOutput, calls=%fused_computation.8 | convolution fusion | flops 5637144576 | bytes 15990784 | tf_op jit(solution)/shard_map/dot_general | solution.py:72
  181.1 48.3 %all-gather.3.cloned.1.call-done = bf16[1,1024,3584]{2,1,0:T(8,128)(2,1)} async-done(((bf16[1,256,3584]{2,1,0:T(8,128)(2,1)}), bf16[1,1024,3584]{2,1,0:T(8,128)(2,1)}) %all-gather.3.cloned.1.call-update) | async-done | bytes 7340048 | tf_op jit(solution)/shard_map/all_gather | solution.py:61
  229.5 12.7 %multiply_reduce_fusion = (bf16[768]{0:T(1024)(128)(2,1)S(1)}, bf16[768,1024]{1,0:T(8,128)(2,1)S(1)}, f32[768,1024]{1,0:T(8,128)}) fusion(f32[768,1024]{1,0:T(8,128)} %fusion.2, f32[768,1024]{1,0:T(8,128)} %fusion.4, bf16[1,1024,3584]{2,1,0:T(8,128)(2,1)} %all-gather.3.cloned.1.call-done, bf16[768,7168]{1,0:T(8,128)(2,1)} %bitcast.2), kind=kOutput, calls=%fused_computation.30 | convolution fusion | flops 5644221440 | bytes 23856640 | tf_op jit(solution)/shard_map/dot_general | solution.py:18
  242.2 10.9 %convolution_convert_fusion.1 = bf16[1024,3584]{1,0:T(8,128)(2,1)} fusion(bf16[768,1024]{1,0:T(8,128)(2,1)S(1)} %get-tuple-element.45, f32[768]{0:T(1024)S(1)} %reshape.188, bf16[768,7168]{1,0:T(8,128)(2,1)} %bitcast.2), kind=kOutput, calls=%fused_computation.3 | convolution fusion | flops 5649072128 | bytes 14420992 | tf_op jit(solution)/shard_map/dot_general | solution.py:24
  253.1 0.1 convert_element_type.148
  253.2 14.6 %fusion.3 = f32[768,3584]{1,0:T(8,128)} fusion(bf16[1,2,3584,1024]{3,2,1,0:T(8,128)(2,1)} %all-gather.5.cloned.1.call-done, f32[768,1024]{1,0:T(8,128)} %fusion.4, f32[768,1024]{1,0:T(8,128)} %fusion.2, f32[768,1024]{1,0:T(8,128)} %get-tuple-element.49, f32[768]{0:T(1024)S(1)} %reshape.188), kind=kOutput, calls=%fused_computation.9 | convolution fusion | flops 5645795328 | bytes 27790336 | tf_op jit(solution)/shard_map/dot_general | solution.py:18
  267.8 13.5 %add_convert_fusion = bf16[768,3584]{1,0:T(8,128)(2,1)} fusion(f32[768,3584]{1,0:T(8,128)} %fusion.3, bf16[1,2,3584,1024]{3,2,1,0:T(8,128)(2,1)} %all-gather.5.cloned.1.call-done, f32[768,1024]{1,0:T(8,128)S(1)} %copy-done.8, f32[768]{0:T(1024)S(1)} %reshape.188, f32[768,1024]{1,0:T(8,128)S(1)} %copy-done.7), kind=kOutput, calls=%fused_computation.2 | convolution fusion | flops 5648154624 | bytes 30149632 | tf_op jit(solution)/shard_map/dot_general | solution.py:18
  281.3 1.9 scatter.9
  283.2 72.7 %all_to_all.10 = bf16[32,24,3584]{2,1,0:T(8,128)(2,1)S(1)} all-to-all(bf16[32,24,3584]{2,1,0:T(8,128)(2,1)} %scatter.9), channel_id=1, replica_groups=mesh['expert'=32,'dp'=4] {'expert'}, dimensions={0} | all-to-all | bytes 11010048 | tf_op jit(solution)/shard_map/all_to_all | solution.py:93
  355.9 2.4 copy-done
  358.4 0.3 select_reduce_fusion
  358.9 0.6 multiply_divide_fusion
  359.6 4.4 %convolution_convert_fusion.2 = bf16[64,3584]{1,0:T(8,128)(2,1)} fusion(bf16[768,3584]{1,0:T(8,128)(2,1)} %bitcast.57, bf16[768,64]{0,1:T(8,128)(2,1)S(1)} %convert_reduce_fusion), kind=kOutput, calls=%fused_computation.19 | convolution fusion | flops 352550912 | bytes 6062080 | tf_op jit(solution)/shard_map/dot_general | solution.py:24
  364.0 7.7 %fusion.20 = (bf16[1,256,3584]{2,1,0:T(8,128)(2,1)}, bf16[1,256,3584]{2,1,0:T(8,128)(2,1)}, bf16[1,256,3584]{2,1,0:T(8,128)(2,1)}) fusion(bf16[256,3584]{1,0:T(8,128)(2,1)} %reduce-scatter.2.cloned.1.call-done, bf16[1,256,3584]{2,1,0:T(8,128)(2,1)} %param.19, bf16[1,256,3584]{2,1,0:T(8,128)(2,1)} %param.18, bf16[1,256,3584]{2,1,0:T(8,128)(2,1)S(1)} %copy-done.1), kind=kLoop, calls=%fused_computation.37 | loop fusion | flops 21102592 | bytes 12845056 | tf_op jit(solution)/shard_map/convert_element_type | solution.py:115
  (41 shorter events, 1.1 us)
Async XLA Ops:
  7.2 0.8 copy-start.5
  7.2 2.5 copy-start.4
  7.2 4.0 %copy-start.3 = (bf16[64,3584]{1,0:T(8,128)(2,1)S(1)}, bf16[64,3584]{1,0:T(8,128)(2,1)}, u32[]{:S(2)}) copy-start(bf16[64,3584]{1,0:T(8,128)(2,1)} %param.12) | copy-start | bytes 1376260
  7.2 4.0 %copy-start.2 = (bf16[64,3584]{1,0:T(8,128)(2,1)S(1)}, bf16[64,3584]{1,0:T(8,128)(2,1)}, u32[]{:S(2)}) copy-start(bf16[64,3584]{1,0:T(8,128)(2,1)} %param.13) | copy-start | bytes 1376260
  7.2 153.6 %all-gather.5.cloned.1.call-start = ((), (), s32[]{:S(2)}) async-start(), calls=%async_computation.4 | async-start | bytes 18350080 | tf_op jit(solution)/shard_map/all_gather | solution.py:60
  18.8 141.0 %all-to-all-start = ((bf16[32,24,7168]{2,1,0:T(8,128)(2,1)}), bf16[32,24,7168]{2,1,0:T(8,128)(2,1)}, u32[]{:S(2)}, u32[]{:S(2)}) async-start(bf16[32,24,7168]{2,1,0:T(8,128)(2,1)} %scatter.6), calls=%async_computation | async-start | bytes 22020096 | tf_op jit(solution)/shard_map/all_to_all | solution.py:63
  27.5 202.0 %all-gather.3.cloned.1.call-start = ((), (), s32[]{:S(2)}) async-start(), calls=%async_computation.3 | async-start | bytes 9175040 | tf_op jit(solution)/shard_map/all_gather | solution.py:61
  28.2 335.7 %reduce-scatter.2.cloned.1.call-start = ((), (), s32[]{:S(2)}) async-start(), calls=%async_computation.5 | async-start | bytes 9175040 | tf_op jit(solution)/shard_map/reduce_scatter | solution.py:78
  160.8 11.3 %copy-start.6 = (bf16[1,2,3584,1024]{3,2,1,0:T(8,128)(2,1)S(1)}, bf16[1,2,3584,1024]{3,2,1,0:T(8,128)(2,1)}, u32[]{:S(2)}) copy-start(bf16[1,2,3584,1024]{3,2,1,0:T(8,128)(2,1)} %all-gather.5.cloned.1.call-done) | copy-start | bytes 44040196
  253.2 14.7 %copy-start.7 = (f32[768,1024]{1,0:T(8,128)S(1)}, f32[768,1024]{1,0:T(8,128)}, u32[]{:S(2)}) copy-start(f32[768,1024]{1,0:T(8,128)} %fusion.4) | copy-start | bytes 9437188
  253.2 14.7 %copy-start.8 = (f32[768,1024]{1,0:T(8,128)S(1)}, f32[768,1024]{1,0:T(8,128)}, u32[]{:S(2)}) copy-start(f32[768,1024]{1,0:T(8,128)} %get-tuple-element.49) | copy-start | bytes 9437188
  355.9 2.4 copy-start
  358.3 5.7 %copy-start.1 = (bf16[1,256,3584]{2,1,0:T(8,128)(2,1)S(1)}, bf16[1,256,3584]{2,1,0:T(8,128)(2,1)}, u32[]{:S(2)}) copy-start(bf16[1,256,3584]{2,1,0:T(8,128)(2,1)} %param.17) | copy-start | bytes 5505028
Sparse Core Ops, SparseCore 0:
  9.7 142.1 all-gather.4
  153.6 75.8 all-gather.2
  253.2 73.4 reduce-scatter.1

commit v3 on v2

--- a/solution.py
+++ b/solution.py
@@ -74,10 +74,11 @@
     silu_gate = pre_gate * sig_gate
     hidden = (silu_gate * pre_up).astype(jnp.bfloat16)
     scaled = (slot_weight[:, None] * gs_rows.astype(jnp.float32)).astype(jnp.bfloat16)
-    local_grad = contract_first(hidden, scaled)
-    grad_shard = lax.psum_scatter(
-        local_grad.astype(jnp.bfloat16), "dp", scatter_dimension=0, tiled=True
-    ).astype(jnp.float32)
+    local_grad = contract_first(hidden, scaled).astype(jnp.bfloat16)
+    local_grad, gs_rows = lax.optimization_barrier((local_grad, gs_rows))
+    grad_shard = lax.psum_scatter(local_grad, "dp", scatter_dimension=0, tiled=True).astype(
+        jnp.float32
+    )
     back_raw = contract_last(gs_rows, full_down)
     affinity = jnp.sum(hidden.astype(jnp.float32) * back_raw, axis=1).astype(jnp.bfloat16)
     back = slot_weight[:, None] * back_raw
@@ -85,15 +86,21 @@
         jnp.bfloat16
     )
     up_grad = (back * silu_gate).astype(jnp.bfloat16)
-    route_in = (contract_last(gate_grad, gate_w) + contract_last(up_grad, up_w)).astype(
-        jnp.bfloat16
-    )
-    ret_rows = route_in.reshape(experts, capacity, model_width)
-    ret_rows = ret_rows.at[:, side_row, :capacity].set(affinity.reshape(experts, capacity))
-    back_rows = lax.all_to_all(ret_rows, "expert", split_axis=0, concat_axis=0, tiled=True)
-    back_affinity = back_rows[:, side_row, :capacity].reshape(slot_count).astype(jnp.float32)
-    back_rows = back_rows.reshape(slot_count, model_width)
-    token_grad = contract_first(tok_match, back_rows).astype(jnp.bfloat16)
+    half_width = model_width // 2
+    pieces = []
+    for c in range(2):
+        cols = slice(c * half_width, (c + 1) * half_width)
+        route_in = (
+            contract_last(gate_grad, gate_w[cols]) + contract_last(up_grad, up_w[cols])
+        ).astype(jnp.bfloat16)
+        ret_rows = route_in.reshape(experts, capacity, half_width)
+        if c == 0:
+            ret_rows = ret_rows.at[:, side_row, :capacity].set(affinity.reshape(experts, capacity))
+        pieces.append(lax.all_to_all(ret_rows, "expert", split_axis=0, concat_axis=0, tiled=True))
+    back_affinity = pieces[0][:, side_row, :capacity].reshape(slot_count).astype(jnp.float32)
+    token_grad = jnp.concatenate(
+        [contract_first(tok_match, p.reshape(slot_count, half_width)) for p in pieces], axis=1
+    ).astype(jnp.bfloat16)
     route_affinity = jnp.sum(matched * back_affinity[:, None], axis=0)
     route_affinity = route_affinity.reshape(tok_rows, top_count)
     mixed = jnp.sum(route_affinity * scores, axis=1, keepdims=True) / score_sum

time: 379 us -> 363 us (0.958)
  blocking collectives: 72.7 us -> 0 us
  waiting for transfers between devices: 181 us -> 221 us
  starting transfers between devices: 8.92 us -> 23.6 us
    all_to_all x1 -> x0, blocking collectives: 72.7 us -> none  [shards(): lax.all_to_all(ret_rows, 'expert', split_axis=0, concat_axis=0, tiled=True)]
    all_to_all x0 -> x2, waiting for transfers between devices: none -> 57 us  [shards(): lax.all_to_all(ret_rows, 'expert', split_axis=0, concat_axis=0, tiled=True)]
    all_gather x1, waiting for transfers between devices: 48.3 us -> 31.2 us  [shards(): full_down = lax.all_gather(down, 'dp', axis=1, tiled=True)[0]]
    all_to_all x0 -> x2, starting transfers between devices: none -> 14.6 us  [shards(): lax.all_to_all(ret_rows, 'expert', split_axis=0, concat_axis=0, tiled=True)]
    slice x0 -> x1, local copies, waits for them, and re-layouts: none -> 5.57 us  [shards(): gs_rows = recv_rows[:, model_width:]]
    dot_general x3 -> x5, matrix products: 40.8 us -> 38.4 us  [contract_last(): lax.dot_general(left, right, (((1,), (1,)), ((), ())), preferred_element_...]
    dot_general x2 -> x3, matrix products: 15.3 us -> 13.9 us  [contract_first(): lax.dot_general(left, right, (((0,), (0,)), ((), ())), preferred_element_...]
  transfers between devices with their start and end apart: 4 -> 6, of which waited for: 2 -> 4; matrix products, arithmetic and copies ran while one was open for 18% -> 26% of each run, Pallas kernels for 0% -> 0%
where the time goes in v3:
time: 363 us; the launch traced here: 361 us
  waiting for transfers between devices  221 us (61%)
  matrix products  78.9 us (22%)
  starting transfers between devices  23.6 us (7%)
  between operations  14 us (4%)
  other arithmetic  12.8 us (4%)
  local copies, waits for them, and re-layouts  10.8 us (3%)
    all_to_all x1, waiting for transfers between devices, shards(): lax.all_to_all(send_rows, 'expert', split_axis=0, concat_axis=0, tiled=True)  131 us
    all_to_all x2, waiting for transfers between devices, shards(): lax.all_to_all(ret_rows, 'expert', split_axis=0, concat_axis=0, tiled=True)  57 us
    dot_general x5, matrix products, contract_last(): lax.dot_general(left, right, (((1,), (1,)), ((), ())), preferred_element_...  38.4 us
    all_gather x1, waiting for transfers between devices, shards(): full_down = lax.all_gather(down, 'dp', axis=1, tiled=True)[0]  31.2 us
    all_to_all x2, starting transfers between devices, shards(): lax.all_to_all(ret_rows, 'expert', split_axis=0, concat_axis=0, tiled=True)  14.6 us
    dot_general x3, matrix products, contract_first(): lax.dot_general(left, right, (((0,), (0,)), ((), ())), preferred_element_...  13.9 us
    dot_general x1, matrix products, shards(): pre_gate = jnp.dot(xs_rows, gate_w, preferred_element_type=jnp.float32)  10.6 us
    dot_general x1, matrix products, shards(): pre_up = jnp.dot(xs_rows, up_w, preferred_element_type=jnp.float32)  10.3 us
  transfers between devices with their start and end apart: 6, of which 4 were waited for; matrix products, arithmetic and copies ran while one was open for 26% of the time, Pallas kernels for 0%

profile of v3, /device:TPU:1, one launch (start us, length us, event | category | flops | bytes accessed | tf_op | source)
XLA Modules:
  0.0 361.1 jit_solution(9815599811936528560)
XLA Ops:
  7.3 0.7 all-gather.3.cloned.1.call-update
  8.2 1.2 reduce-window.6
  9.4 0.2 slice_reduce_fusion
  10.3 0.2 select_reduce_fusion.1
  10.6 0.5 convert_reduce_fusion
  11.2 5.8 %convolution_convert_fusion = bf16[768,7168]{1,0:T(8,128)(2,1)} fusion(bf16[64,3584]{1,0:T(8,128)(2,1)S(1)} %copy-done, bf16[64,3584]{1,0:T(8,128)(2,1)S(1)} %copy-done.1, bf16[768,64]{0,1:T(8,128)(2,1)S(1)} %convert_reduce_fusion), kind=kOutput, calls=%fused_computation | convolution fusion | flops 711983104 | bytes 12025856 | tf_op jit(solution)/shard_map/dot_general | solution.py:54
  17.0 1.9 scatter.6
  18.8 8.6 %all-to-all-start = ((bf16[32,24,7168]{2,1,0:T(8,128)(2,1)}), bf16[32,24,7168]{2,1,0:T(8,128)(2,1)}, u32[]{:S(2)}, u32[]{:S(2)}) async-start(bf16[32,24,7168]{2,1,0:T(8,128)(2,1)} %scatter.6), calls=%async_computation | async-start | bytes 22020096 | tf_op jit(solution)/shard_map/all_to_all | solution.py:63
  27.5 0.7 all-gather.5.cloned.1.call-update
  28.5 131.3 %all-to-all-done = bf16[32,24,7168]{2,1,0:T(8,128)(2,1)} async-done(((bf16[32,24,7168]{2,1,0:T(8,128)(2,1)}), bf16[32,24,7168]{2,1,0:T(8,128)(2,1)}, u32[]{:S(2)}, u32[]{:S(2)}) %all-to-all-start) | async-done | bytes 11010080 | tf_op jit(solution)/shard_map/all_to_all | solution.py:63
  159.8 0.9 fusion.30
  160.8 5.6 %slice.125 = bf16[768,3584]{1,0:T(8,128)(2,1)} slice(bf16[768,7168]{1,0:T(8,128)(2,1)} %bitcast.2), slice={[0:768], [3584:7168]} | slice | bytes 11010048 | tf_op jit(solution)/shard_map/slice | solution.py:67
  166.4 10.6 %fusion.1 = f32[768,1024]{1,0:T(8,128)S(1)} fusion(bf16[1,2,3584,1024]{3,2,1,0:T(8,128)(2,1)} %all-gather.3.cloned.1.call-done, bf16[768,7168]{1,0:T(8,128)(2,1)} %bitcast.2), kind=kOutput, calls=%fused_computation.6 | convolution fusion | flops 5637144576 | bytes 15990784 | tf_op jit(solution)/shard_map/dot_general | solution.py:71
  177.0 10.3 %multiply_convert_fusion.4 = (bf16[768,1024]{1,0:T(8,128)(2,1)S(1)}, f32[768,1024]{1,0:T(8,128)}) fusion(f32[768,1024]{1,0:T(8,128)S(1)} %fusion.1, bf16[1,2,3584,1024]{3,2,1,0:T(8,128)(2,1)S(1)} %copy-done.4, bf16[768,7168]{1,0:T(8,128)(2,1)} %bitcast.2), kind=kOutput, calls=%fused_computation.38 | convolution fusion | flops 5641863168 | bytes 20709376 | tf_op jit(solution)/shard_map/dot_general | solution.py:72
  187.2 10.9 %convolution_convert_fusion.1 = bf16[1024,3584]{1,0:T(8,128)(2,1)} fusion(bf16[768,1024]{1,0:T(8,128)(2,1)S(1)} %get-tuple-element.54, f32[768]{0:T(1024)S(1)} %reshape.200, bf16[768,7168]{1,0:T(8,128)(2,1)} %bitcast.2), kind=kOutput, calls=%fused_computation.2 | convolution fusion | flops 5649072128 | bytes 14420992 | tf_op jit(solution)/shard_map/dot_general | solution.py:24
  198.2 31.2 %all-gather.5.cloned.1.call-done = bf16[1,1024,3584]{2,1,0:T(8,128)(2,1)} async-done(((bf16[1,256,3584]{2,1,0:T(8,128)(2,1)}), bf16[1,1024,3584]{2,1,0:T(8,128)(2,1)}) %all-gather.5.cloned.1.call-update) | async-done | bytes 7340048 | tf_op jit(solution)/shard_map/all_gather | solution.py:61
  229.4 13.6 %multiply_convert_fusion.3 = (bf16[768,1024]{1,0:T(8,128)(2,1)}, bf16[768,1024]{1,0:T(8,128)(2,1)}, bf16[768]{0:T(1024)(128)(2,1)S(1)}) fusion(f32[768,1024]{1,0:T(8,128)} %copy-done.7, f32[768,1024]{1,0:T(8,128)} %get-tuple-element.55, f32[768]{0:T(1024)S(1)} %reshape.200, bf16[768,1024]{1,0:T(8,128)(2,1)S(1)} %get-tuple-element.54, ...), kind=kOutput, calls=%fused_computation.37 | convolution fusion | flops 5650512896 | bytes 23859712 | tf_op jit(solution)/shard_map/dot_general | solution.py:18
  243.1 5.7 %fusion.17 = f32[768,1792]{1,0:T(8,128)S(1)} fusion(bf16[768,1024]{1,0:T(8,128)(2,1)} %get-tuple-element.49, bf16[1,2,3584,1024]{3,2,1,0:T(8,128)(2,1)} %all-gather.3.cloned.1.call-done), kind=kOutput, calls=%fused_computation.32 | convolution fusion | flops 2818572288 | bytes 10747904 | tf_op jit(solution)/shard_map/dot_general | solution.py:18
  248.9 6.7 %add_convert_fusion.1 = bf16[768,1792]{1,0:T(8,128)(2,1)} fusion(f32[768,1792]{1,0:T(8,128)S(1)} %fusion.17, bf16[768,1024]{1,0:T(8,128)(2,1)S(1)} %copy-done.5, bf16[1,2,3584,1024]{3,2,1,0:T(8,128)(2,1)} %all-gather.3.cloned.1.call-done), kind=kOutput, calls=%fused_computation.13 | convolution fusion | flops 2821324800 | bytes 13500416 | tf_op jit(solution)/shard_map/dot_general | solution.py:18
  255.6 1.9 scatter.9
  257.4 7.7 %all-to-all-start.1 = ((bf16[32,24,1792]{2,1,0:T(8,128)(2,1)}), bf16[32,24,1792]{2,1,0:T(8,128)(2,1)S(1)}, u32[]{:S(2)}, u32[]{:S(2)}) async-start(bf16[32,24,1792]{2,1,0:T(8,128)(2,1)} %scatter.9), calls=%async_computation.1 | async-start | bytes 5505024 | tf_op jit(solution)/shard_map/all_to_all | solution.py:99
  265.1 5.8 %fusion.15 = f32[768,1792]{1,0:T(8,128)S(1)} fusion(bf16[768,1024]{1,0:T(8,128)(2,1)} %get-tuple-element.49, bf16[1,2,3584,1024]{3,2,1,0:T(8,128)(2,1)} %all-gather.3.cloned.1.call-done), kind=kOutput, calls=%fused_computation.28 | convolution fusion | flops 2818572288 | bytes 10747904 | tf_op jit(solution)/shard_map/dot_general | solution.py:18
  271.0 6.6 %add_convert_fusion = bf16[768,1792]{1,0:T(8,128)(2,1)} fusion(f32[768,1792]{1,0:T(8,128)S(1)} %fusion.15, bf16[768,1024]{1,0:T(8,128)(2,1)S(1)} %copy-done.6, bf16[1,2,3584,1024]{3,2,1,0:T(8,128)(2,1)} %all-gather.3.cloned.1.call-done), kind=kOutput, calls=%fused_computation.12 | convolution fusion | flops 2821324800 | bytes 13500416 | tf_op jit(solution)/shard_map/dot_general | solution.py:18
  277.5 22.9 %all-to-all-done.1 = bf16[32,24,1792]{2,1,0:T(8,128)(2,1)S(1)} async-done(((bf16[32,24,1792]{2,1,0:T(8,128)(2,1)}), bf16[32,24,1792]{2,1,0:T(8,128)(2,1)S(1)}, u32[]{:S(2)}, u32[]{:S(2)}) %all-to-all-start.1) | async-done | bytes 2752544 | tf_op jit(solution)/shard_map/all_to_all | solution.py:99
  300.4 7.0 %all-to-all-start.2 = ((bf16[32,24,1792]{2,1,0:T(8,128)(2,1)}), bf16[32,24,1792]{2,1,0:T(8,128)(2,1)}, u32[]{:S(2)}, u32[]{:S(2)}) async-start(bf16[32,24,1792]{2,1,0:T(8,128)(2,1)} %bitcast.83), calls=%async_computation.2 | async-start | bytes 5505024 | tf_op jit(solution)/shard_map/all_to_all | solution.py:99
  307.5 0.3 select_reduce_fusion
  308.0 0.6 multiply_divide_fusion
  308.7 34.2 %all-to-all-done.2 = bf16[32,24,1792]{2,1,0:T(8,128)(2,1)} async-done(((bf16[32,24,1792]{2,1,0:T(8,128)(2,1)}), bf16[32,24,1792]{2,1,0:T(8,128)(2,1)}, u32[]{:S(2)}, u32[]{:S(2)}) %all-to-all-start.2) | async-done | bytes 2752544 | tf_op jit(solution)/shard_map/all_to_all | solution.py:99
  342.8 2.4 convolution_convert_fusion.2
  345.2 0.6 convolution_convert_fusion.3
  345.8 0.8 pad_maximum_fusion
  346.6 7.9 %fusion.21 = (bf16[1,256,3584]{2,1,0:T(8,128)(2,1)}, bf16[1,256,3584]{2,1,0:T(8,128)(2,1)}, bf16[1,256,3584]{2,1,0:T(8,128)(2,1)}) fusion(bf16[256,3584]{1,0:T(8,128)(2,1)} %reduce-scatter.2.cloned.1.call-done, bf16[1,256,3584]{2,1,0:T(8,128)(2,1)} %param.19, bf16[1,256,3584]{2,1,0:T(8,128)(2,1)} %param.18, bf16[1,256,3584]{2,1,0:T(8,128)(2,1)} %param.17), kind=kLoop, calls=%fused_computation.44 | loop fusion | flops 21102592 | bytes 12845056 | tf_op jit(solution)/shard_map/convert_element_type | solution.py:122
  (47 shorter events, 1.9 us)
Async XLA Ops:
  7.2 0.8 copy-start.3
  7.2 2.9 copy-start.2
  7.2 4.0 %copy-start = (bf16[64,3584]{1,0:T(8,128)(2,1)S(1)}, bf16[64,3584]{1,0:T(8,128)(2,1)}, u32[]{:S(2)}) copy-start(bf16[64,3584]{1,0:T(8,128)(2,1)} %param.13) | copy-start | bytes 1376260
  7.2 4.0 %copy-start.1 = (bf16[64,3584]{1,0:T(8,128)(2,1)S(1)}, bf16[64,3584]{1,0:T(8,128)(2,1)}, u32[]{:S(2)}) copy-start(bf16[64,3584]{1,0:T(8,128)(2,1)} %param.12) | copy-start | bytes 1376260
  7.2 159.1 %all-gather.3.cloned.1.call-start = ((), (), s32[]{:S(2)}) async-start(), calls=%async_computation.4 | async-start | bytes 18350080 | tf_op jit(solution)/shard_map/all_gather | solution.py:60
  18.8 141.0 %all-to-all-start = ((bf16[32,24,7168]{2,1,0:T(8,128)(2,1)}), bf16[32,24,7168]{2,1,0:T(8,128)(2,1)}, u32[]{:S(2)}, u32[]{:S(2)}) async-start(bf16[32,24,7168]{2,1,0:T(8,128)(2,1)} %scatter.6), calls=%async_computation | async-start | bytes 22020096 | tf_op jit(solution)/shard_map/all_to_all | solution.py:63
  27.5 201.9 %all-gather.5.cloned.1.call-start = ((), (), s32[]{:S(2)}) async-start(), calls=%async_computation.5 | async-start | bytes 9175040 | tf_op jit(solution)/shard_map/all_gather | solution.py:61
  28.2 318.4 %reduce-scatter.2.cloned.1.call-start = ((), (), s32[]{:S(2)}) async-start(), calls=%async_computation.6 | async-start | bytes 9175040 | tf_op jit(solution)/shard_map/reduce_scatter | solution.py:79
  166.4 10.6 %copy-start.4 = (bf16[1,2,3584,1024]{3,2,1,0:T(8,128)(2,1)S(1)}, bf16[1,2,3584,1024]{3,2,1,0:T(8,128)(2,1)}, u32[]{:S(2)}) copy-start(bf16[1,2,3584,1024]{3,2,1,0:T(8,128)(2,1)} %all-gather.3.cloned.1.call-done) | copy-start | bytes 44040196
  177.0 10.3 %copy-start.7 = (f32[768,1024]{1,0:T(8,128)}, f32[768,1024]{1,0:T(8,128)S(1)}, u32[]{:S(2)}) copy-start(f32[768,1024]{1,0:T(8,128)S(1)} %fusion.1) | copy-start | bytes 9437188
  243.1 5.7 %copy-start.5 = (bf16[768,1024]{1,0:T(8,128)(2,1)S(1)}, bf16[768,1024]{1,0:T(8,128)(2,1)}, u32[]{:S(2)}) copy-start(bf16[768,1024]{1,0:T(8,128)(2,1)} %get-tuple-element.48) | copy-start | bytes 4718596
  257.4 43.0 %all-to-all-start.1 = ((bf16[32,24,1792]{2,1,0:T(8,128)(2,1)}), bf16[32,24,1792]{2,1,0:T(8,128)(2,1)S(1)}, u32[]{:S(2)}, u32[]{:S(2)}) async-start(bf16[32,24,1792]{2,1,0:T(8,128)(2,1)} %scatter.9), calls=%async_computation.1 | async-start | bytes 5505024 | tf_op jit(solution)/shard_map/all_to_all | solution.py:99
  265.1 5.8 %copy-start.6 = (bf16[768,1024]{1,0:T(8,128)(2,1)S(1)}, bf16[768,1024]{1,0:T(8,128)(2,1)}, u32[]{:S(2)}) copy-start(bf16[768,1024]{1,0:T(8,128)(2,1)} %get-tuple-element.48) | copy-start | bytes 4718596
  300.4 42.4 %all-to-all-start.2 = ((bf16[32,24,1792]{2,1,0:T(8,128)(2,1)}), bf16[32,24,1792]{2,1,0:T(8,128)(2,1)}, u32[]{:S(2)}, u32[]{:S(2)}) async-start(bf16[32,24,1792]{2,1,0:T(8,128)(2,1)} %bitcast.83), calls=%async_computation.2 | async-start | bytes 5505024 | tf_op jit(solution)/shard_map/all_to_all | solution.py:99
Sparse Core Ops, SparseCore 0:
  9.7 142.1 all-gather.2
  153.5 75.8 all-gather.4
  231.8 73.5 reduce-scatter.1

commit v4 on v3

--- a/solution.py
+++ b/solution.py
@@ -58,42 +58,72 @@
     )
 
     full_gu = lax.all_gather(gate_up, "dp", axis=3, tiled=True)[0]
-    full_down = lax.all_gather(down, "dp", axis=1, tiled=True)[0]
+    local_ffw = down.shape[1]
+    part_ffw = local_ffw // 2
+    down_parts = [
+        lax.all_gather(down[:, h * part_ffw:(h + 1) * part_ffw], "dp", axis=1, tiled=True)[0]
+        for h in range(2)
+    ]
 
     recv_rows = lax.all_to_all(send_rows, "expert", split_axis=0, concat_axis=0, tiled=True)
     slot_weight = recv_rows[:, side_row, :capacity].reshape(slot_count).astype(jnp.float32)
     recv_rows = recv_rows.reshape(slot_count, 2 * model_width)
     xs_rows = recv_rows[:, :model_width]
     gs_rows = recv_rows[:, model_width:]
+    scaled = (slot_weight[:, None] * gs_rows.astype(jnp.float32)).astype(jnp.bfloat16)
 
-    gate_w = full_gu[0]
-    up_w = full_gu[1]
-    pre_gate = jnp.dot(xs_rows, gate_w, preferred_element_type=jnp.float32)
-    pre_up = jnp.dot(xs_rows, up_w, preferred_element_type=jnp.float32)
-    sig_gate = jax.nn.sigmoid(pre_gate)
-    silu_gate = pre_gate * sig_gate
-    hidden = (silu_gate * pre_up).astype(jnp.bfloat16)
-    scaled = (slot_weight[:, None] * gs_rows.astype(jnp.float32)).astype(jnp.bfloat16)
-    local_grad = contract_first(hidden, scaled).astype(jnp.bfloat16)
+    def half_cols(w, h):
+        return w.reshape(model_width, data_ways, 2, part_ffw)[:, :, h, :].reshape(
+            model_width, data_ways * part_ffw
+        )
+
+    gate_h, up_h, pre_gate_h, pre_up_h, sig_h, silu_h, hidden_h, grad_h = ([] for _ in range(8))
+    for h in range(2):
+        gate_w = half_cols(full_gu[0], h)
+        up_w = half_cols(full_gu[1], h)
+        pre_gate = jnp.dot(xs_rows, gate_w, preferred_element_type=jnp.float32)
+        pre_up = jnp.dot(xs_rows, up_w, preferred_element_type=jnp.float32)
+        sig_gate = jax.nn.sigmoid(pre_gate)
+        silu_gate = pre_gate * sig_gate
+        hidden = (silu_gate * pre_up).astype(jnp.bfloat16)
+        local_grad = contract_first(hidden, scaled).astype(jnp.bfloat16)
+        for lst, val in zip(
+            (gate_h, up_h, pre_gate_h, pre_up_h, sig_h, silu_h, hidden_h, grad_h),
+            (gate_w, up_w, pre_gate, pre_up, sig_gate, silu_gate, hidden, local_grad),
+        ):
+            lst.append(val)
+    local_grad = jnp.stack(
+        [g.reshape(data_ways, part_ffw, model_width) for g in grad_h], axis=1
+    ).reshape(data_ways * local_ffw, model_width)
     local_grad, gs_rows = lax.optimization_barrier((local_grad, gs_rows))
     grad_shard = lax.psum_scatter(local_grad, "dp", scatter_dimension=0, tiled=True).astype(
         jnp.float32
     )
-    back_raw = contract_last(gs_rows, full_down)
-    affinity = jnp.sum(hidden.astype(jnp.float32) * back_raw, axis=1).astype(jnp.bfloat16)
-    back = slot_weight[:, None] * back_raw
-    gate_grad = (back * pre_up * sig_gate * (1.0 + pre_gate * (1.0 - sig_gate))).astype(
-        jnp.bfloat16
-    )
-    up_grad = (back * silu_gate).astype(jnp.bfloat16)
     half_width = model_width // 2
+    affinity = jnp.zeros((slot_count,), jnp.float32)
+    route_acc = [jnp.zeros((slot_count, half_width), jnp.float32) for _ in range(2)]
+    for h in range(2):
+        back_raw = contract_last(gs_rows, down_parts[h])
+        affinity = affinity + jnp.sum(hidden_h[h].astype(jnp.float32) * back_raw, axis=1)
+        back = slot_weight[:, None] * back_raw
+        pre_gate, pre_up, sig_gate, silu_gate = pre_gate_h[h], pre_up_h[h], sig_h[h], silu_h[h]
+        gate_grad = (back * pre_up * sig_gate * (1.0 + pre_gate * (1.0 - sig_gate))).astype(
+            jnp.bfloat16
+        )
+        up_grad = (back * silu_gate).astype(jnp.bfloat16)
+        for c in range(2):
+            cols = slice(c * half_width, (c + 1) * half_width)
+            route_acc[c] = (
+                route_acc[c]
+                + contract_last(gate_grad, gate_h[h][cols])
+                + contract_last(up_grad, up_h[h][cols])
+            )
+        if h == 0:
+            *route_acc, gs_rows = lax.optimization_barrier((*route_acc, gs_rows))
+    affinity = affinity.astype(jnp.bfloat16)
     pieces = []
     for c in range(2):
-        cols = slice(c * half_width, (c + 1) * half_width)
-        route_in = (
-            contract_last(gate_grad, gate_w[cols]) + contract_last(up_grad, up_w[cols])
-        ).astype(jnp.bfloat16)
-        ret_rows = route_in.reshape(experts, capacity, half_width)
+        ret_rows = route_acc[c].astype(jnp.bfloat16).reshape(experts, capacity, half_width)
         if c == 0:
             ret_rows = ret_rows.at[:, side_row, :capacity].set(affinity.reshape(experts, capacity))
         pieces.append(lax.all_to_all(ret_rows, "expert", split_axis=0, concat_axis=0, tiled=True))

time: 363 us -> 401 us (1.10); the launches traced: 361 us -> 395 us
  local copies, waits for them, and re-layouts: 10.8 us -> 48.5 us
  waiting for transfers between devices: 221 us -> 193 us
  matrix products: 78.9 us -> 95.6 us
    all_gather x1 -> x2, waiting for transfers between devices: 31.2 us -> 0.01 us  [shards(): lax.all_gather(down[:, h * part_ffw:(h + 1) * part_ffw], 'dp', axis=1, ti...]
    slice x0 -> x6, local copies, waits for them, and re-layouts: none -> 22 us  [the longest x1 6.19 us: shards(): up_w = half_cols(full_gu[1], h)]
    unnamed x17 -> x54, local copies, waits for them, and re-layouts: 0.12 us -> 12.4 us
    dot_general x5 -> x10, matrix products: 38.4 us -> 44.4 us  [contract_last(): lax.dot_general(left, right, (((1,), (1,)), ((), ())), preferred_element_...]
    dot_general x3 -> x4, matrix products: 13.9 us -> 18.9 us  [contract_first(): lax.dot_general(left, right, (((0,), (0,)), ((), ())), preferred_element_...]
    all_to_all x2, waiting for transfers between devices: 57 us -> 62 us  [shards(): lax.all_to_all(ret_rows, 'expert', split_axis=0, concat_axis=0, tiled=True)]
    dot_general x1 -> x2, matrix products: 10.3 us -> 14.7 us  [shards(): pre_up = jnp.dot(xs_rows, up_w, preferred_element_type=jnp.float32)]
    dot_general x1 -> x2, matrix products: 10.6 us -> 11.8 us  [shards(): pre_gate = jnp.dot(xs_rows, gate_w, preferred_element_type=jnp.float32)]
  transfers between devices with their start and end apart: 6 -> 7, of which waited for: 4 -> 3; matrix products, arithmetic and copies ran while one was open for 26% -> 36% of each run, Pallas kernels for 0% -> 0%
where the time goes in v4:
time: 401 us; the launch traced here: 395 us
  waiting for transfers between devices  193 us (48%)
  matrix products  95.6 us (24%)
  local copies, waits for them, and re-layouts  48.5 us (12%)
  starting transfers between devices  27 us (7%)
  other arithmetic  16.3 us (4%)
  between operations  14.6 us (4%)
    all_to_all x1, waiting for transfers between devices, shards(): lax.all_to_all(send_rows, 'expert', split_axis=0, concat_axis=0, tiled=True)  130 us
    all_to_all x2, waiting for transfers between devices, shards(): lax.all_to_all(ret_rows, 'expert', split_axis=0, concat_axis=0, tiled=True)  62 us
    dot_general x10, matrix products, contract_last(): lax.dot_general(left, right, (((1,), (1,)), ((), ())), preferred_element_...  44.4 us
    dot_general x4, matrix products, contract_first(): lax.dot_general(left, right, (((0,), (0,)), ((), ())), preferred_element_...  18.9 us
    all_to_all x2, starting transfers between devices, shards(): lax.all_to_all(ret_rows, 'expert', split_axis=0, concat_axis=0, tiled=True)  18 us
    dot_general x2, matrix products, shards(): pre_up = jnp.dot(xs_rows, up_w, preferred_element_type=jnp.float32)  14.7 us
    unnamed x54, local copies, waits for them, and re-layouts  12.4 us
    dot_general x2, matrix products, shards(): pre_gate = jnp.dot(xs_rows, gate_w, preferred_element_type=jnp.float32)  11.8 us
  transfers between devices with their start and end apart: 7, of which 3 were waited for; matrix products, arithmetic and copies ran while one was open for 36% of the time, Pallas kernels for 0%

profile of v4, /device:TPU:1, one launch (start us, length us, event | category | flops | bytes accessed | tf_op | source)
XLA Modules:
  0.0 394.9 jit_solution(12146516022227138466)
XLA Ops:
  7.2 6.0 %copy.54 = bf16[1,2,3584,256]{2,3,1,0:T(8,128)(2,1)} copy(bf16[1,2,3584,256]{3,2,1,0:T(8,128)(2,1)} %param.16) | data formatting | bytes 7340032 | tf_op args[4]
  17.2 5.7 %convolution_convert_fusion = bf16[768,7168]{1,0:T(8,128)(2,1)} fusion(bf16[64,3584]{1,0:T(8,128)(2,1)S(1)} %copy-done.14, bf16[64,3584]{1,0:T(8,128)(2,1)S(1)} %copy-done.15, bf16[768,64]{0,1:T(8,128)(2,1)S(1)} %convert_reduce_fusion), kind=kOutput, calls=%fused_computation | convolution fusion | flops 711983104 | bytes 12025856 | tf_op jit(solution)/shard_map/dot_general | solution.py:54
  24.7 8.9 %all-to-all-start = ((bf16[32,24,7168]{2,1,0:T(8,128)(2,1)}), bf16[32,24,7168]{2,1,0:T(8,128)(2,1)}, u32[]{:S(2)}, u32[]{:S(2)}) async-start(bf16[32,24,7168]{2,1,0:T(8,128)(2,1)} %scatter.6), calls=%async_computation | async-start | bytes 22020096 | tf_op jit(solution)/shard_map/all_to_all | solution.py:68
  35.9 130.1 %all-to-all-done = bf16[32,24,7168]{2,1,0:T(8,128)(2,1)} async-done(((bf16[32,24,7168]{2,1,0:T(8,128)(2,1)}), bf16[32,24,7168]{2,1,0:T(8,128)(2,1)}, u32[]{:S(2)}, u32[]{:S(2)}) %all-to-all-start) | async-done | bytes 11010080 | tf_op jit(solution)/shard_map/all_to_all | solution.py:68
  166.9 5.6 %slice.189 = bf16[768,3584]{1,0:T(8,128)(2,1)} slice(bf16[768,7168]{1,0:T(8,128)(2,1)} %bitcast.2), slice={[0:768], [3584:7168]} | slice | bytes 11010048 | tf_op jit(solution)/shard_map/slice | solution.py:72
  172.5 6.2 %fusion.41 = (bf16[1,1,3584,1024]{2,3,1,0:T(8,128)(2,1)S(1)}, bf16[1,1,3584,1024]{2,3,1,0:T(8,128)(2,1)S(1)}) fusion(bf16[1,2,3584,1024]{2,3,1,0:T(8,128)(2,1)} %all-gather.4.cloned.1.call-done), kind=kLoop, calls=%fused_computation.87 | loop fusion | bytes 29360128 | tf_op jit(solution)/shard_map/slice | solution.py:83
  178.7 2.9 fusion.44
  185.1 2.5 fusion.45
  188.4 5.8 %fusion.14 = f32[768,512]{0,1:T(8,128)S(1)} fusion(bf16[3584,512]{0,1:T(8,128)(2,1)S(1)} %bitcast.120, bf16[768,7168]{1,0:T(8,128)(2,1)} %bitcast.2), kind=kOutput, calls=%fused_computation.28 | convolution fusion | flops 2818572288 | bytes 10747904 | tf_op jit(solution)/shard_map/dot_general | solution.py:84
  194.2 7.4 %multiply_convert_fusion.7 = (bf16[768,512]{0,1:T(8,128)(2,1)S(1)}, f32[768,512]{0,1:T(8,128)}) fusion(f32[768,512]{0,1:T(8,128)S(1)} %fusion.14, bf16[3584,512]{0,1:T(8,128)(2,1)S(1)} %bitcast.121, bf16[768,7168]{1,0:T(8,128)(2,1)} %bitcast.2), kind=kOutput, calls=%fused_computation.45 | convolution fusion | flops 2820931584 | bytes 13107200 | tf_op jit(solution)/shard_map/dot_general | solution.py:85
  201.5 7.8 %convolution_convert_fusion.1 = bf16[512,3584]{1,0:T(8,128)(2,1)} fusion(bf16[768,512]{0,1:T(8,128)(2,1)S(1)} %get-tuple-element.79, f32[768]{0:T(1024)S(1)} %reshape.219, bf16[768,7168]{1,0:T(8,128)(2,1)} %bitcast.2), kind=kOutput, calls=%fused_computation.3 | convolution fusion | flops 2828664832 | bytes 9964544 | tf_op jit(solution)/shard_map/dot_general | solution.py:24
  209.4 6.1 %fusion.18 = f32[768,512]{0,1:T(8,128)S(1)} fusion(bf16[3584,512]{0,1:T(8,128)(2,1)S(1)} %bitcast.118, bf16[768,7168]{1,0:T(8,128)(2,1)} %bitcast.2), kind=kOutput, calls=%fused_computation.32 | convolution fusion | flops 2818572288 | bytes 10747904 | tf_op jit(solution)/shard_map/dot_general | solution.py:84
  215.5 7.3 %multiply_convert_fusion.8 = (bf16[768,512]{0,1:T(8,128)(2,1)S(1)}, f32[768,512]{0,1:T(8,128)}) fusion(f32[768,512]{0,1:T(8,128)S(1)} %fusion.18, bf16[3584,512]{0,1:T(8,128)(2,1)S(1)} %bitcast.117, bf16[768,7168]{1,0:T(8,128)(2,1)} %bitcast.2), kind=kOutput, calls=%fused_computation.48 | convolution fusion | flops 2820931584 | bytes 13107200 | tf_op jit(solution)/shard_map/dot_general | solution.py:85
  222.8 8.0 %convolution_convert_fusion.2 = bf16[512,3584]{1,0:T(8,128)(2,1)} fusion(bf16[768,512]{0,1:T(8,128)(2,1)S(1)} %get-tuple-element.81, f32[768]{0:T(1024)S(1)} %reshape.219, bf16[768,7168]{1,0:T(8,128)(2,1)} %bitcast.2), kind=kOutput, calls=%fused_computation.4 | convolution fusion | flops 2828664832 | bytes 9964544 | tf_op jit(solution)/shard_map/dot_general | solution.py:24
  230.8 3.0 pad_maximum_fusion
  233.8 3.4 copy.55
  237.3 5.7 %fusion.43 = (bf16[1792,4,1,128]{0,3,2,1:T(8,128)(2,1)}, bf16[1792,4,1,128]{0,3,2,1:T(8,128)(2,1)S(1)}, bf16[1792,4,1,128]{0,3,2,1:T(8,128)(2,1)}, bf16[1792,4,1,128]{0,3,2,1:T(8,128)(2,1)}) fusion(bf16[3584,4,2,128]{0,3,2,1:T(8,128)(2,1)} %bitcast.102), kind=kLoop, calls=%fused_computation.89 | loop fusion | bytes 14680064 | tf_op jit(solution)/shard_map/slice | solution.py:118
  243.0 8.4 %multiply_convert_fusion.5 = (bf16[768,512]{0,1:T(8,128)(2,1)S(1)}, bf16[768,512]{0,1:T(8,128)(2,1)S(1)}, f32[768]{0:T(1024)S(1)}) fusion(f32[768]{0:T(1024)S(1)} %reshape.219, f32[768,512]{0,1:T(8,128)} %copy-done.19, f32[768,512]{0,1:T(8,128)} %get-tuple-element.82, bf16[768,512]{0,1:T(8,128)(2,1)} %copy-done.21, bf16[768,3584]{1,0:T(8,128)(2,1)} %slice.189, ...), kind=kOutput, calls=%fused_computation.43 | convolution fusion | flops 2825256192 | bytes 14686208 | tf_op jit(solution)/shard_map/dot_general | solution.py:18
  255.3 3.3 fusion.42
  258.6 5.7 %convolution_add_fusion.1 = f32[768,1792]{1,0:T(8,128)} fusion(f32[768,1792]{1,0:T(8,128)S(1)} %fusion.47, bf16[768,512]{0,1:T(8,128)(2,1)S(1)} %get-tuple-element.73, bf16[1792,512]{0,1:T(8,128)(2,1)} %bitcast.116), kind=kOutput, calls=%fused_computation.13 | convolution fusion | flops 1410662400 | bytes 13631488 | tf_op jit(solution)/shard_map/dot_general | solution.py:18
  264.2 4.1 %convolution_add_fusion = f32[768,1792]{1,0:T(8,128)} fusion(f32[768,1792]{1,0:T(8,128)S(1)} %fusion.48, bf16[768,512]{0,1:T(8,128)(2,1)S(1)} %get-tuple-element.73, bf16[1792,512]{0,1:T(8,128)(2,1)S(1)} %bitcast.115), kind=kOutput, calls=%fused_computation.12 | convolution fusion | flops 1410662400 | bytes 13631488 | tf_op jit(solution)/shard_map/dot_general | solution.py:18
  268.3 9.5 %multiply_convert_fusion.3 = (bf16[768,512]{0,1:T(8,128)(2,1)S(1)}, bf16[768,512]{0,1:T(8,128)(2,1)}, f32[768]{0:T(1024)S(1)}) fusion(f32[768]{0:T(1024)S(1)} %reshape.219, f32[768,512]{0,1:T(8,128)} %copy-done.18, f32[768,512]{0,1:T(8,128)} %get-tuple-element.80, bf16[768,512]{0,1:T(8,128)(2,1)} %copy-done.20, bf16[768,3584]{1,0:T(8,128)(2,1)} %slice.189, ...), kind=kOutput, calls=%fused_computation.41 | convolution fusion | flops 2825256192 | bytes 14686208 | tf_op jit(solution)/shard_map/dot_general | solution.py:18
  278.0 3.6 fusion.49
  282.1 3.5 add_convert_fusion.1
  287.5 11.6 %all-to-all-start.1 = ((bf16[32,24,1792]{2,1,0:T(8,128)(2,1)}), bf16[32,24,1792]{2,1,0:T(8,128)(2,1)}, u32[]{:S(2)}, u32[]{:S(2)}) async-start(bf16[32,24,1792]{2,1,0:T(8,128)(2,1)} %scatter.9), calls=%async_computation.1 | async-start | bytes 5505024 | tf_op jit(solution)/shard_map/all_to_all | solution.py:129
  299.2 2.9 fusion.50
  302.3 3.5 add_convert_fusion
  305.8 28.7 %all-to-all-done.1 = bf16[32,24,1792]{2,1,0:T(8,128)(2,1)} async-done(((bf16[32,24,1792]{2,1,0:T(8,128)(2,1)}), bf16[32,24,1792]{2,1,0:T(8,128)(2,1)}, u32[]{:S(2)}, u32[]{:S(2)}) %all-to-all-start.1) | async-done | bytes 2752544 | tf_op jit(solution)/shard_map/all_to_all | solution.py:129
  334.6 6.3 %all-to-all-start.2 = ((bf16[32,24,1792]{2,1,0:T(8,128)(2,1)}), bf16[32,24,1792]{2,1,0:T(8,128)(2,1)S(1)}, u32[]{:S(2)}, u32[]{:S(2)}) async-start(bf16[32,24,1792]{2,1,0:T(8,128)(2,1)} %bitcast.108), calls=%async_computation.2 | async-start | bytes 5505024 | tf_op jit(solution)/shard_map/all_to_all | solution.py:129
  343.0 33.3 %all-to-all-done.2 = bf16[32,24,1792]{2,1,0:T(8,128)(2,1)S(1)} async-done(((bf16[32,24,1792]{2,1,0:T(8,128)(2,1)}), bf16[32,24,1792]{2,1,0:T(8,128)(2,1)S(1)}, u32[]{:S(2)}, u32[]{:S(2)}) %all-to-all-start.2) | async-done | bytes 2752544 | tf_op jit(solution)/shard_map/all_to_all | solution.py:129
  376.9 2.5 convolution_convert_fusion.4
  380.2 7.7 %fusion.21 = (bf16[1,256,3584]{2,1,0:T(8,128)(2,1)}, bf16[1,256,3584]{2,1,0:T(8,128)(2,1)}, bf16[1,256,3584]{2,1,0:T(8,128)(2,1)}) fusion(bf16[256,3584]{1,0:T(8,128)(2,1)} %reduce-scatter.2.cloned.1.call-done, bf16[1,256,3584]{2,1,0:T(8,128)(2,1)} %param.19, bf16[1,256,3584]{2,1,0:T(8,128)(2,1)} %param.18, bf16[1,256,3584]{2,1,0:T(8,128)(2,1)S(1)} %copy-done.4), kind=kLoop, calls=%fused_computation.37 | loop fusion | flops 21102592 | bytes 12845056 | tf_op jit(solution)/shard_map/convert_element_type | solution.py:152
  (106 shorter events, 23.3 us)
Async XLA Ops:
  7.2 165.3 %all-gather.4.cloned.1.call-start = ((), (), s32[]{:S(2)}) async-start(), calls=%async_computation.4 | async-start | bytes 18350080 | tf_op jit(solution)/shard_map/all_gather | solution.py:60
  13.2 2.8 copy-start.16
  13.2 3.9 copy-start.14
  13.2 3.9 copy-start.15
  24.7 8.9 %copy-start.3 = (bf16[1,256,3584]{2,1,0:T(8,128)(2,1)S(1)}, bf16[1,256,3584]{2,1,0:T(8,128)(2,1)}, u32[]{:S(2)}) copy-start(bf16[1,256,3584]{2,1,0:T(8,128)(2,1)} %param.17) | copy-start | bytes 5505028
  24.7 141.2 %all-to-all-start = ((bf16[32,24,7168]{2,1,0:T(8,128)(2,1)}), bf16[32,24,7168]{2,1,0:T(8,128)(2,1)}, u32[]{:S(2)}, u32[]{:S(2)}) async-start(bf16[32,24,7168]{2,1,0:T(8,128)(2,1)} %scatter.6), calls=%async_computation | async-start | bytes 22020096 | tf_op jit(solution)/shard_map/all_to_all | solution.py:68
  33.6 209.4 %all-gather.6.cloned.1.call-start = ((), (), s32[]{:S(2)}) async-start(), calls=%async_computation.5 | async-start | bytes 4587520 | tf_op jit(solution)/shard_map/all_gather | solution.py:64
  35.1 233.2 %all-gather.8.cloned.1.call-start = ((), (), s32[]{:S(2)}) async-start(), calls=%async_computation.6 | async-start | bytes 4587520 | tf_op jit(solution)/shard_map/all_gather | solution.py:64
  35.8 344.4 %reduce-scatter.2.cloned.1.call-start = ((), (), s32[]{:S(2)}) async-start(), calls=%async_computation.7 | async-start | bytes 9175040 | tf_op jit(solution)/shard_map/reduce_scatter | solution.py:99
  178.7 4.0 %copy-start.1 = (bf16[1,1,3584,1024]{2,3,1,0:T(8,128)(2,1)}, bf16[1,1,3584,1024]{2,3,1,0:T(8,128)(2,1)S(1)}, u32[]{:S(2)}) copy-start(bf16[1,1,3584,1024]{2,3,1,0:T(8,128)(2,1)S(1)} %get-tuple-element.55) | copy-start | bytes 22020100
  178.7 6.4 %copy-start = (bf16[1,1,3584,1024]{2,3,1,0:T(8,128)(2,1)}, bf16[1,1,3584,1024]{2,3,1,0:T(8,128)(2,1)S(1)}, u32[]{:S(2)}) copy-start(bf16[1,1,3584,1024]{2,3,1,0:T(8,128)(2,1)S(1)} %get-tuple-element.54) | copy-start | bytes 22020100
  185.1 3.2 copy-start.10
  188.4 5.8 %copy-start.11 = (bf16[3584,4,1,128]{0,3,2,1:T(8,128)(2,1)S(1)}, bf16[3584,4,1,128]{0,3,2,1:T(8,128)(2,1)}, u32[]{:S(2)}) copy-start(bf16[3584,4,1,128]{0,3,2,1:T(8,128)(2,1)} %get-tuple-element.66) | copy-start | bytes 11010052
  194.1 7.4 %copy-start.18 = (f32[768,512]{0,1:T(8,128)}, f32[768,512]{0,1:T(8,128)S(1)}, u32[]{:S(2)}) copy-start(f32[768,512]{0,1:T(8,128)S(1)} %fusion.14) | copy-start | bytes 4718596
  201.5 7.8 %copy-start.20 = (bf16[768,512]{0,1:T(8,128)(2,1)}, bf16[768,512]{0,1:T(8,128)(2,1)S(1)}, u32[]{:S(2)}) copy-start(bf16[768,512]{0,1:T(8,128)(2,1)S(1)} %get-tuple-element.79) | copy-start | bytes 2359300
  215.4 7.3 %copy-start.19 = (f32[768,512]{0,1:T(8,128)}, f32[768,512]{0,1:T(8,128)S(1)}, u32[]{:S(2)}) copy-start(f32[768,512]{0,1:T(8,128)S(1)} %fusion.18) | copy-start | bytes 4718596
  222.8 8.0 %copy-start.21 = (bf16[768,512]{0,1:T(8,128)(2,1)}, bf16[768,512]{0,1:T(8,128)(2,1)S(1)}, u32[]{:S(2)}) copy-start(bf16[768,512]{0,1:T(8,128)(2,1)S(1)} %get-tuple-element.81) | copy-start | bytes 2359300
  222.8 8.0 %copy-start.9 = (bf16[512,3584]{1,0:T(8,128)(2,1)S(1)}, bf16[512,3584]{1,0:T(8,128)(2,1)}, u32[]{:S(2)}) copy-start(bf16[512,3584]{1,0:T(8,128)(2,1)} %convolution_convert_fusion.1) | copy-start | bytes 11010052
  243.0 8.4 %copy-start.8 = (bf16[1792,4,1,128]{0,3,2,1:T(8,128)(2,1)S(1)}, bf16[1792,4,1,128]{0,3,2,1:T(8,128)(2,1)}, u32[]{:S(2)}) copy-start(bf16[1792,4,1,128]{0,3,2,1:T(8,128)(2,1)} %get-tuple-element.63) | copy-start | bytes 5505028
  251.4 1.7 copy-start.7
  251.4 3.3 slice-start
  253.0 2.2 slice-start.1
  277.9 3.7 copy-start.12
  278.0 3.6 copy-start.2
  278.0 4.1 %copy-start.6 = (bf16[1792,4,1,128]{0,3,2,1:T(8,128)(2,1)S(1)}, bf16[1792,4,1,128]{0,3,2,1:T(8,128)(2,1)}, u32[]{:S(2)}) copy-start(bf16[1792,4,1,128]{0,3,2,1:T(8,128)(2,1)} %get-tuple-element.56) | copy-start | bytes 5505028
  287.5 14.6 %slice-start.2 = ((s8[5505024]{0:T(1024)(128)(4,1)}), s8[1310720]{0:T(1024)(128)(4,1)S(1)}, s32[]{:S(2)}) async-start(s8[5505024]{0:T(1024)(128)(4,1)} %bitcast.104), calls=%async_computation.10 | async-start | bytes 2621440
  287.5 47.1 %all-to-all-start.1 = ((bf16[32,24,1792]{2,1,0:T(8,128)(2,1)}), bf16[32,24,1792]{2,1,0:T(8,128)(2,1)}, u32[]{:S(2)}, u32[]{:S(2)}) async-start(bf16[32,24,1792]{2,1,0:T(8,128)(2,1)} %scatter.9), calls=%async_computation.1 | async-start | bytes 5505024 | tf_op jit(solution)/shard_map/all_to_all | solution.py:129
  299.1 3.0 slice-start.3
  299.1 3.0 copy-start.5
  299.1 3.1 copy-start.13
  334.6 41.7 %all-to-all-start.2 = ((bf16[32,24,1792]{2,1,0:T(8,128)(2,1)}), bf16[32,24,1792]{2,1,0:T(8,128)(2,1)S(1)}, u32[]{:S(2)}, u32[]{:S(2)}) async-start(bf16[32,24,1792]{2,1,0:T(8,128)(2,1)} %bitcast.108), calls=%async_computation.2 | async-start | bytes 5505024 | tf_op jit(solution)/shard_map/all_to_all | solution.py:129
  376.9 3.3 copy-start.4
  (1 other events, 0.7 us)
Sparse Core Ops, SparseCore 0:
  13.4 139.3 all-gather.3
  154.5 45.0 all-gather.5
  201.2 44.1 all-gather.7
  247.7 72.9 reduce-scatter.1

commit v5 on v3

--- a/solution.py
+++ b/solution.py
@@ -86,12 +86,14 @@
         jnp.bfloat16
     )
     up_grad = (back * silu_gate).astype(jnp.bfloat16)
+    grads = jnp.stack([gate_grad, up_grad], axis=1)
     half_width = model_width // 2
     pieces = []
     for c in range(2):
         cols = slice(c * half_width, (c + 1) * half_width)
-        route_in = (
-            contract_last(gate_grad, gate_w[cols]) + contract_last(up_grad, up_w[cols])
+        route_in = lax.dot_general(
+            grads, full_gu[:, cols], (((1, 2), (0, 2)), ((), ())),
+            preferred_element_type=jnp.float32,
         ).astype(jnp.bfloat16)
         ret_rows = route_in.reshape(experts, capacity, half_width)
         if c == 0:

time: 363 us -> 362 us (level)
    dot_general x5 -> x1, matrix products: 38.4 us -> 13.6 us  [contract_last(): lax.dot_general(left, right, (((1,), (1,)), ((), ())), preferred_element_...]
    dot_general x0 -> x2, matrix products: none -> 21.8 us  [shards(): lax.dot_general(grads, full_gu[:, cols], (((1, 2), (0, 2)), ((), ())), pr...]
  transfers between devices with their start and end apart: 6 -> 6, of which waited for: 4 -> 4; matrix products, arithmetic and copies ran while one was open for 26% -> 25% of each run, Pallas kernels for 0% -> 0%
where the time goes in v5:
time: 362 us; the launch traced here: 360 us
  waiting for transfers between devices  223 us (62%)
  matrix products  75.9 us (21%)
  starting transfers between devices  23.6 us (7%)
  between operations  14 us (4%)
  other arithmetic  12.8 us (4%)
  local copies, waits for them, and re-layouts  10.8 us (3%)
    all_to_all x1, waiting for transfers between devices, shards(): lax.all_to_all(send_rows, 'expert', split_axis=0, concat_axis=0, tiled=True)  132 us
    all_to_all x2, waiting for transfers between devices, shards(): lax.all_to_all(ret_rows, 'expert', split_axis=0, concat_axis=0, tiled=True)  58.5 us
    all_gather x1, waiting for transfers between devices, shards(): full_down = lax.all_gather(down, 'dp', axis=1, tiled=True)[0]  31.2 us
    dot_general x2, matrix products, shards(): lax.dot_general(grads, full_gu[:, cols], (((1, 2), (0, 2)), ((), ())), pr...  21.8 us
    all_to_all x2, starting transfers between devices, shards(): lax.all_to_all(ret_rows, 'expert', split_axis=0, concat_axis=0, tiled=True)  14.8 us
    dot_general x3, matrix products, contract_first(): lax.dot_general(left, right, (((0,), (0,)), ((), ())), preferred_element_...  13.9 us
    dot_general x1, matrix products, contract_last(): lax.dot_general(left, right, (((1,), (1,)), ((), ())), preferred_element_...  13.6 us
    dot_general x1, matrix products, shards(): pre_gate = jnp.dot(xs_rows, gate_w, preferred_element_type=jnp.float32)  10.6 us
  transfers between devices with their start and end apart: 6, of which 4 were waited for; matrix products, arithmetic and copies ran while one was open for 25% of the time, Pallas kernels for 0%

profile of v5, /device:TPU:1, one launch (start us, length us, event | category | flops | bytes accessed | tf_op | source)
XLA Modules:
  0.0 359.7 jit_solution(14535515128265471137)
XLA Ops:
  7.3 0.7 all-gather.3.cloned.1.call-update
  8.2 1.2 reduce-window.6
  9.4 0.2 slice_reduce_fusion
  9.7 0.1 fusion.33
  10.2 0.1 reshape.195
  10.3 0.2 select_reduce_fusion.1
  10.6 0.5 convert_reduce_fusion
  11.2 5.8 %convolution_convert_fusion = bf16[768,7168]{1,0:T(8,128)(2,1)} fusion(bf16[64,3584]{1,0:T(8,128)(2,1)S(1)} %copy-done, bf16[64,3584]{1,0:T(8,128)(2,1)S(1)} %copy-done.1, bf16[768,64]{0,1:T(8,128)(2,1)S(1)} %convert_reduce_fusion), kind=kOutput, calls=%fused_computation | convolution fusion | flops 711983104 | bytes 12025856 | tf_op jit(solution)/shard_map/dot_general | solution.py:54
  17.0 1.9 scatter.6
  18.8 8.6 %all-to-all-start = ((bf16[32,24,7168]{2,1,0:T(8,128)(2,1)}), bf16[32,24,7168]{2,1,0:T(8,128)(2,1)}, u32[]{:S(2)}, u32[]{:S(2)}) async-start(bf16[32,24,7168]{2,1,0:T(8,128)(2,1)} %scatter.6), calls=%async_computation | async-start | bytes 22020096 | tf_op jit(solution)/shard_map/all_to_all | solution.py:63
  27.5 0.7 all-gather.5.cloned.1.call-update
  28.3 131.5 %all-to-all-done = bf16[32,24,7168]{2,1,0:T(8,128)(2,1)} async-done(((bf16[32,24,7168]{2,1,0:T(8,128)(2,1)}), bf16[32,24,7168]{2,1,0:T(8,128)(2,1)}, u32[]{:S(2)}, u32[]{:S(2)}) %all-to-all-start) | async-done | bytes 11010080 | tf_op jit(solution)/shard_map/all_to_all | solution.py:63
  159.8 0.9 fusion.36
  160.8 5.6 %slice.97 = bf16[768,3584]{1,0:T(8,128)(2,1)} slice(bf16[768,7168]{1,0:T(8,128)(2,1)} %bitcast.2), slice={[0:768], [3584:7168]} | slice | bytes 11010048 | tf_op jit(solution)/shard_map/slice | solution.py:67
  166.4 10.6 %fusion.5 = f32[768,1024]{1,0:T(8,128)S(1)} fusion(bf16[1,2,3584,1024]{3,2,1,0:T(8,128)(2,1)} %all-gather.3.cloned.1.call-done, bf16[768,7168]{1,0:T(8,128)(2,1)} %bitcast.2), kind=kOutput, calls=%fused_computation.10 | convolution fusion | flops 5637144576 | bytes 15990784 | tf_op jit(solution)/shard_map/dot_general | solution.py:71
  177.0 10.3 %multiply_convert_fusion.4 = (bf16[768,1024]{1,0:T(8,128)(2,1)S(1)}, f32[768,1024]{1,0:T(8,128)}) fusion(f32[768,1024]{1,0:T(8,128)S(1)} %fusion.5, bf16[1,2,3584,1024]{3,2,1,0:T(8,128)(2,1)S(1)} %copy-done.4, bf16[768,7168]{1,0:T(8,128)(2,1)} %bitcast.2), kind=kOutput, calls=%fused_computation.35 | convolution fusion | flops 5641863168 | bytes 20709376 | tf_op jit(solution)/shard_map/dot_general | solution.py:72
  187.2 10.9 %convolution_convert_fusion.1 = bf16[1024,3584]{1,0:T(8,128)(2,1)} fusion(bf16[768,1024]{1,0:T(8,128)(2,1)S(1)} %get-tuple-element.54, f32[768]{0:T(1024)S(1)} %reshape.196, bf16[768,7168]{1,0:T(8,128)(2,1)} %bitcast.2), kind=kOutput, calls=%fused_computation.2 | convolution fusion | flops 5649072128 | bytes 14420992 | tf_op jit(solution)/shard_map/dot_general | solution.py:24
  198.2 31.2 %all-gather.5.cloned.1.call-done = bf16[1,1024,3584]{2,1,0:T(8,128)(2,1)} async-done(((bf16[1,256,3584]{2,1,0:T(8,128)(2,1)}), bf16[1,1024,3584]{2,1,0:T(8,128)(2,1)}) %all-gather.5.cloned.1.call-update) | async-done | bytes 7340048 | tf_op jit(solution)/shard_map/all_gather | solution.py:61
  229.4 13.6 %fusion.27 = (bf16[768,1,1024]{2,0,1:T(8,128)(2,1)}, bf16[768,1,1024]{2,0,1:T(8,128)(2,1)}, bf16[768]{0:T(1024)(128)(2,1)S(1)}) fusion(f32[768,1024]{1,0:T(8,128)} %copy-done.5, f32[768,1024]{1,0:T(8,128)} %get-tuple-element.55, f32[768]{0:T(1024)S(1)} %reshape.196, bf16[768,1024]{1,0:T(8,128)(2,1)S(1)} %get-tuple-element.54, bf16[768,3584]{1,0:T(8,128)(2,1)} %slice.97, ...), kind=kOutput, calls=%fused_computation.48 | convolution fusion | flops 5650512896 | bytes 23859712 | tf_op jit(solution)/shard_map/dot_general | solution.py:18
  243.1 10.9 %bitcast_convert_fusion.1 = bf16[768,1792]{1,0:T(8,128)(2,1)} fusion(bf16[2,3584,1024]{2,1,0:T(8,128)(2,1)} %bitcast.73, bf16[768,1,1024]{2,0,1:T(8,128)(2,1)} %get-tuple-element.49, bf16[768,1,1024]{2,0,1:T(8,128)(2,1)} %get-tuple-element.48), kind=kOutput, calls=%fused_computation.14 | convolution fusion | flops 5640093696 | bytes 13238272 | tf_op jit(solution)/shard_map/dot_general | solution.py:94
  254.0 1.9 scatter.9
  255.8 7.9 %all-to-all-start.1 = ((bf16[32,24,1792]{2,1,0:T(8,128)(2,1)}), bf16[32,24,1792]{2,1,0:T(8,128)(2,1)S(1)}, u32[]{:S(2)}, u32[]{:S(2)}) async-start(bf16[32,24,1792]{2,1,0:T(8,128)(2,1)} %scatter.9), calls=%async_computation.1 | async-start | bytes 5505024 | tf_op jit(solution)/shard_map/all_to_all | solution.py:101
  263.7 10.9 %bitcast_convert_fusion = bf16[768,1792]{1,0:T(8,128)(2,1)} fusion(bf16[2,3584,1024]{2,1,0:T(8,128)(2,1)} %bitcast.74, bf16[768,1,1024]{2,0,1:T(8,128)(2,1)} %get-tuple-element.49, bf16[768,1,1024]{2,0,1:T(8,128)(2,1)} %get-tuple-element.48), kind=kOutput, calls=%fused_computation.13 | convolution fusion | flops 5640093696 | bytes 13238272 | tf_op jit(solution)/shard_map/dot_general | solution.py:94
  274.6 24.4 %all-to-all-done.1 = bf16[32,24,1792]{2,1,0:T(8,128)(2,1)S(1)} async-done(((bf16[32,24,1792]{2,1,0:T(8,128)(2,1)}), bf16[32,24,1792]{2,1,0:T(8,128)(2,1)S(1)}, u32[]{:S(2)}, u32[]{:S(2)}) %all-to-all-start.1) | async-done | bytes 2752544 | tf_op jit(solution)/shard_map/all_to_all | solution.py:101
  299.0 7.0 %all-to-all-start.2 = ((bf16[32,24,1792]{2,1,0:T(8,128)(2,1)}), bf16[32,24,1792]{2,1,0:T(8,128)(2,1)}, u32[]{:S(2)}, u32[]{:S(2)}) async-start(bf16[32,24,1792]{2,1,0:T(8,128)(2,1)} %bitcast.72), calls=%async_computation.2 | async-start | bytes 5505024 | tf_op jit(solution)/shard_map/all_to_all | solution.py:101
  306.1 0.3 select_reduce_fusion
  306.6 0.6 multiply_divide_fusion
  307.3 34.2 %all-to-all-done.2 = bf16[32,24,1792]{2,1,0:T(8,128)(2,1)} async-done(((bf16[32,24,1792]{2,1,0:T(8,128)(2,1)}), bf16[32,24,1792]{2,1,0:T(8,128)(2,1)}, u32[]{:S(2)}, u32[]{:S(2)}) %all-to-all-start.2) | async-done | bytes 2752544 | tf_op jit(solution)/shard_map/all_to_all | solution.py:101
  341.4 2.4 convolution_convert_fusion.2
  343.8 0.6 convolution_convert_fusion.3
  344.4 0.8 pad_maximum_fusion.3
  345.2 7.9 %fusion.25 = (bf16[1,256,3584]{2,1,0:T(8,128)(2,1)}, bf16[1,256,3584]{2,1,0:T(8,128)(2,1)}, bf16[1,256,3584]{2,1,0:T(8,128)(2,1)}) fusion(bf16[256,3584]{1,0:T(8,128)(2,1)} %reduce-scatter.2.cloned.1.call-done, bf16[1,256,3584]{2,1,0:T(8,128)(2,1)} %param.19, bf16[1,256,3584]{2,1,0:T(8,128)(2,1)} %param.18, bf16[1,256,3584]{2,1,0:T(8,128)(2,1)} %param.17), kind=kLoop, calls=%fused_computation.41 | loop fusion | flops 21102592 | bytes 12845056 | tf_op jit(solution)/shard_map/convert_element_type | solution.py:124
  (41 shorter events, 1.4 us)
Async XLA Ops:
  7.2 0.8 copy-start.3
  7.2 2.9 copy-start.2
  7.2 4.0 %copy-start = (bf16[64,3584]{1,0:T(8,128)(2,1)S(1)}, bf16[64,3584]{1,0:T(8,128)(2,1)}, u32[]{:S(2)}) copy-start(bf16[64,3584]{1,0:T(8,128)(2,1)} %param.13) | copy-start | bytes 1376260
  7.2 4.0 %copy-start.1 = (bf16[64,3584]{1,0:T(8,128)(2,1)S(1)}, bf16[64,3584]{1,0:T(8,128)(2,1)}, u32[]{:S(2)}) copy-start(bf16[64,3584]{1,0:T(8,128)(2,1)} %param.12) | copy-start | bytes 1376260
  7.2 159.1 %all-gather.3.cloned.1.call-start = ((), (), s32[]{:S(2)}) async-start(), calls=%async_computation.4 | async-start | bytes 18350080 | tf_op jit(solution)/shard_map/all_gather | solution.py:60
  18.8 141.0 %all-to-all-start = ((bf16[32,24,7168]{2,1,0:T(8,128)(2,1)}), bf16[32,24,7168]{2,1,0:T(8,128)(2,1)}, u32[]{:S(2)}, u32[]{:S(2)}) async-start(bf16[32,24,7168]{2,1,0:T(8,128)(2,1)} %scatter.6), calls=%async_computation | async-start | bytes 22020096 | tf_op jit(solution)/shard_map/all_to_all | solution.py:63
  27.5 201.9 %all-gather.5.cloned.1.call-start = ((), (), s32[]{:S(2)}) async-start(), calls=%async_computation.5 | async-start | bytes 9175040 | tf_op jit(solution)/shard_map/all_gather | solution.py:61
  28.2 317.0 %reduce-scatter.2.cloned.1.call-start = ((), (), s32[]{:S(2)}) async-start(), calls=%async_computation.6 | async-start | bytes 9175040 | tf_op jit(solution)/shard_map/reduce_scatter | solution.py:79
  166.4 10.6 %copy-start.4 = (bf16[1,2,3584,1024]{3,2,1,0:T(8,128)(2,1)S(1)}, bf16[1,2,3584,1024]{3,2,1,0:T(8,128)(2,1)}, u32[]{:S(2)}) copy-start(bf16[1,2,3584,1024]{3,2,1,0:T(8,128)(2,1)} %all-gather.3.cloned.1.call-done) | copy-start | bytes 44040196
  177.0 10.3 %copy-start.5 = (f32[768,1024]{1,0:T(8,128)}, f32[768,1024]{1,0:T(8,128)S(1)}, u32[]{:S(2)}) copy-start(f32[768,1024]{1,0:T(8,128)S(1)} %fusion.5) | copy-start | bytes 9437188
  255.8 43.2 %all-to-all-start.1 = ((bf16[32,24,1792]{2,1,0:T(8,128)(2,1)}), bf16[32,24,1792]{2,1,0:T(8,128)(2,1)S(1)}, u32[]{:S(2)}, u32[]{:S(2)}) async-start(bf16[32,24,1792]{2,1,0:T(8,128)(2,1)} %scatter.9), calls=%async_computation.1 | async-start | bytes 5505024 | tf_op jit(solution)/shard_map/all_to_all | solution.py:101
  299.0 42.4 %all-to-all-start.2 = ((bf16[32,24,1792]{2,1,0:T(8,128)(2,1)}), bf16[32,24,1792]{2,1,0:T(8,128)(2,1)}, u32[]{:S(2)}, u32[]{:S(2)}) async-start(bf16[32,24,1792]{2,1,0:T(8,128)(2,1)} %bitcast.72), calls=%async_computation.2 | async-start | bytes 5505024 | tf_op jit(solution)/shard_map/all_to_all | solution.py:101
Sparse Core Ops, SparseCore 0:
  9.7 142.1 all-gather.2
  153.5 75.8 all-gather.4
  231.8 73.5 reduce-scatter.1

commit v6 on v2

--- a/solution.py
+++ b/solution.py
@@ -74,10 +74,11 @@
     silu_gate = pre_gate * sig_gate
     hidden = (silu_gate * pre_up).astype(jnp.bfloat16)
     scaled = (slot_weight[:, None] * gs_rows.astype(jnp.float32)).astype(jnp.bfloat16)
-    local_grad = contract_first(hidden, scaled)
-    grad_shard = lax.psum_scatter(
-        local_grad.astype(jnp.bfloat16), "dp", scatter_dimension=0, tiled=True
-    ).astype(jnp.float32)
+    local_grad = contract_first(hidden, scaled).astype(jnp.bfloat16)
+    local_grad, gs_rows = lax.optimization_barrier((local_grad, gs_rows))
+    grad_shard = lax.psum_scatter(local_grad, "dp", scatter_dimension=0, tiled=True).astype(
+        jnp.float32
+    )
     back_raw = contract_last(gs_rows, full_down)
     affinity = jnp.sum(hidden.astype(jnp.float32) * back_raw, axis=1).astype(jnp.bfloat16)
     back = slot_weight[:, None] * back_raw
@@ -85,15 +86,17 @@
         jnp.bfloat16
     )
     up_grad = (back * silu_gate).astype(jnp.bfloat16)
-    route_in = (contract_last(gate_grad, gate_w) + contract_last(up_grad, up_w)).astype(
-        jnp.bfloat16
-    )
+    grads = jnp.stack([gate_grad, up_grad], axis=1)
+    route_in = lax.dot_general(
+        grads, full_gu, (((1, 2), (0, 2)), ((), ())), preferred_element_type=jnp.float32
+    ).astype(jnp.bfloat16)
     ret_rows = route_in.reshape(experts, capacity, model_width)
     ret_rows = ret_rows.at[:, side_row, :capacity].set(affinity.reshape(experts, capacity))
     back_rows = lax.all_to_all(ret_rows, "expert", split_axis=0, concat_axis=0, tiled=True)
     back_affinity = back_rows[:, side_row, :capacity].reshape(slot_count).astype(jnp.float32)
-    back_rows = back_rows.reshape(slot_count, model_width)
-    token_grad = contract_first(tok_match, back_rows).astype(jnp.bfloat16)
+    token_grad = contract_first(tok_match, back_rows.reshape(slot_count, model_width)).astype(
+        jnp.bfloat16
+    )
     route_affinity = jnp.sum(matched * back_affinity[:, None], axis=0)
     route_affinity = route_affinity.reshape(tok_rows, top_count)
     mixed = jnp.sum(route_affinity * scores, axis=1, keepdims=True) / score_sum

time: 379 us -> 357 us (0.942)
  waiting for transfers between devices: 181 us -> 164 us
  matrix products: 82.2 us -> 72.4 us
  local copies, waits for them, and re-layouts: 7.6 us -> 13.2 us
    dot_general x3 -> x1, matrix products: 40.8 us -> 13.3 us  [contract_last(): lax.dot_general(left, right, (((1,), (1,)), ((), ())), preferred_element_...]
    dot_general x0 -> x1, matrix products: none -> 17.2 us  [shards(): lax.dot_general(grads, full_gu, (((1, 2), (0, 2)), ((), ())), preferred_e...]
    all_gather x1, waiting for transfers between devices: 48.3 us -> 31.2 us  [shards(): full_down = lax.all_gather(down, 'dp', axis=1, tiled=True)[0]]
    slice x0 -> x1, local copies, waits for them, and re-layouts: none -> 5.57 us  [shards(): gs_rows = recv_rows[:, model_width:]]
  transfers between devices with their start and end apart: 4 -> 4, of which waited for: 2 -> 2; matrix products, arithmetic and copies ran while one was open for 18% -> 24% of each run, Pallas kernels for 0% -> 0%
where the time goes in v6:
time: 357 us
  waiting for transfers between devices  164 us (46%)
  blocking collectives  72.7 us (20%)
  matrix products  72.4 us (20%)
  between operations  13.9 us (4%)
  local copies, waits for them, and re-layouts  13.2 us (4%)
  other arithmetic  11.7 us (3%)
  starting transfers between devices  8.92 us (2%)
    all_to_all x1, waiting for transfers between devices, shards(): lax.all_to_all(send_rows, 'expert', split_axis=0, concat_axis=0, tiled=True)  131 us
    all_to_all x1, blocking collectives, shards(): lax.all_to_all(ret_rows, 'expert', split_axis=0, concat_axis=0, tiled=True)  72.7 us
    all_gather x1, waiting for transfers between devices, shards(): full_down = lax.all_gather(down, 'dp', axis=1, tiled=True)[0]  31.2 us
    dot_general x1, matrix products, shards(): lax.dot_general(grads, full_gu, (((1, 2), (0, 2)), ((), ())), preferred_e...  17.2 us
    dot_general x2, matrix products, contract_first(): lax.dot_general(left, right, (((0,), (0,)), ((), ())), preferred_element_...  15.3 us
    dot_general x1, matrix products, contract_last(): lax.dot_general(left, right, (((1,), (1,)), ((), ())), preferred_element_...  13.3 us
    dot_general x1, matrix products, shards(): pre_gate = jnp.dot(xs_rows, gate_w, preferred_element_type=jnp.float32)  10.6 us
    dot_general x1, matrix products, shards(): pre_up = jnp.dot(xs_rows, up_w, preferred_element_type=jnp.float32)  10.3 us
  transfers between devices with their start and end apart: 4, of which 2 were waited for; matrix products, arithmetic and copies ran while one was open for 24% of the time, Pallas kernels for 0%

profile of v6, /device:TPU:1, one launch (start us, length us, event | category | flops | bytes accessed | tf_op | source)
XLA Modules:
  0.0 356.8 jit_solution(4837269592304441232)
XLA Ops:
  7.3 0.7 all-gather.3.cloned.1.call-update
  8.0 0.1 eq.46
  8.2 1.2 reduce-window.6
  9.4 0.2 slice_reduce_fusion
  9.7 0.1 fusion.32
  9.8 0.1 reduce_sum.66
  10.2 0.1 reshape.187
  10.3 0.2 select_reduce_fusion.1
  10.5 0.1 convert_element_type.147
  10.6 0.5 convert_reduce_fusion
  11.2 5.8 %convolution_convert_fusion = bf16[768,7168]{1,0:T(8,128)(2,1)} fusion(bf16[64,3584]{1,0:T(8,128)(2,1)S(1)} %copy-done.2, bf16[64,3584]{1,0:T(8,128)(2,1)S(1)} %copy-done.3, bf16[768,64]{0,1:T(8,128)(2,1)S(1)} %convert_reduce_fusion), kind=kOutput, calls=%fused_computation.2 | convolution fusion | flops 711983104 | bytes 12025856 | tf_op jit(solution)/shard_map/dot_general | solution.py:54
  17.0 1.9 scatter.6
  18.8 8.6 %all-to-all-start = ((bf16[32,24,7168]{2,1,0:T(8,128)(2,1)}), bf16[32,24,7168]{2,1,0:T(8,128)(2,1)}, u32[]{:S(2)}, u32[]{:S(2)}) async-start(bf16[32,24,7168]{2,1,0:T(8,128)(2,1)} %scatter.6), calls=%async_computation | async-start | bytes 22020096 | tf_op jit(solution)/shard_map/all_to_all | solution.py:63
  27.5 0.7 all-gather.5.cloned.1.call-update
  28.2 0.2 reduce-scatter.2.cloned.1.call-start
  28.5 131.3 %all-to-all-done = bf16[32,24,7168]{2,1,0:T(8,128)(2,1)} async-done(((bf16[32,24,7168]{2,1,0:T(8,128)(2,1)}), bf16[32,24,7168]{2,1,0:T(8,128)(2,1)}, u32[]{:S(2)}, u32[]{:S(2)}) %all-to-all-start) | async-done | bytes 11010080 | tf_op jit(solution)/shard_map/all_to_all | solution.py:63
  159.8 0.9 fusion.37
  160.8 5.6 %slice.89 = bf16[768,3584]{1,0:T(8,128)(2,1)} slice(bf16[768,7168]{1,0:T(8,128)(2,1)} %bitcast.2), slice={[0:768], [3584:7168]} | slice | bytes 11010048 | tf_op jit(solution)/shard_map/slice | solution.py:67
  166.4 10.6 %fusion.5 = f32[768,1024]{1,0:T(8,128)S(1)} fusion(bf16[1,2,3584,1024]{3,2,1,0:T(8,128)(2,1)} %all-gather.3.cloned.1.call-done, bf16[768,7168]{1,0:T(8,128)(2,1)} %bitcast.2), kind=kOutput, calls=%fused_computation.9 | convolution fusion | flops 5637144576 | bytes 15990784 | tf_op jit(solution)/shard_map/dot_general | solution.py:71
  177.0 10.3 %multiply_convert_fusion.4 = (bf16[768,1024]{1,0:T(8,128)(2,1)S(1)}, f32[768,1024]{1,0:T(8,128)}) fusion(f32[768,1024]{1,0:T(8,128)S(1)} %fusion.5, bf16[1,2,3584,1024]{3,2,1,0:T(8,128)(2,1)S(1)} %copy-done.6, bf16[768,7168]{1,0:T(8,128)(2,1)} %bitcast.2), kind=kOutput, calls=%fused_computation.35 | convolution fusion | flops 5641863168 | bytes 20709376 | tf_op jit(solution)/shard_map/dot_general | solution.py:72
  187.2 10.9 %convolution_convert_fusion.1 = bf16[1024,3584]{1,0:T(8,128)(2,1)} fusion(bf16[768,1024]{1,0:T(8,128)(2,1)S(1)} %get-tuple-element.54, f32[768]{0:T(1024)S(1)} %reshape.188, bf16[768,7168]{1,0:T(8,128)(2,1)} %bitcast.2), kind=kOutput, calls=%fused_computation.5 | convolution fusion | flops 5649072128 | bytes 14420992 | tf_op jit(solution)/shard_map/dot_general | solution.py:24
  198.2 31.2 %all-gather.5.cloned.1.call-done = bf16[1,1024,3584]{2,1,0:T(8,128)(2,1)} async-done(((bf16[1,256,3584]{2,1,0:T(8,128)(2,1)}), bf16[1,1024,3584]{2,1,0:T(8,128)(2,1)}) %all-gather.5.cloned.1.call-update) | async-done | bytes 7340048 | tf_op jit(solution)/shard_map/all_gather | solution.py:61
  229.4 13.3 %fusion.26 = (bf16[768,1,1024]{2,0,1:T(8,128)(2,1)S(1)}, bf16[768,1,1024]{2,0,1:T(8,128)(2,1)}, bf16[768]{0:T(1024)(128)(2,1)S(1)}) fusion(f32[768,1024]{1,0:T(8,128)} %copy-done.7, f32[768,1024]{1,0:T(8,128)} %get-tuple-element.55, f32[768]{0:T(1024)S(1)} %reshape.188, bf16[768,1024]{1,0:T(8,128)(2,1)S(1)} %get-tuple-element.54, ...), kind=kOutput, calls=%fused_computation.46 | convolution fusion | flops 5650512896 | bytes 23859712 | tf_op jit(solution)/shard_map/dot_general | solution.py:18
  242.7 0.1 convert_element_type.148
  242.8 17.2 %bitcast_convert_fusion = bf16[768,3584]{1,0:T(8,128)(2,1)} fusion(bf16[1,2,3584,1024]{3,2,1,0:T(8,128)(2,1)} %all-gather.3.cloned.1.call-done, bf16[768,1,1024]{2,0,1:T(8,128)(2,1)} %get-tuple-element.49, bf16[768,1,1024]{2,0,1:T(8,128)(2,1)S(1)} %get-tuple-element.48), kind=kOutput, calls=%fused_computation.3 | convolution fusion | flops 11278614528 | bytes 23330816 | tf_op jit(solution)/shard_map/dot_general | solution.py:90
  260.0 1.9 scatter.9
  261.9 72.7 %all_to_all.10 = bf16[32,24,3584]{2,1,0:T(8,128)(2,1)S(1)} all-to-all(bf16[32,24,3584]{2,1,0:T(8,128)(2,1)} %scatter.9), channel_id=1, replica_groups=mesh['expert'=32,'dp'=4] {'expert'}, dimensions={0} | all-to-all | bytes 11010048 | tf_op jit(solution)/shard_map/all_to_all | solution.py:95
  334.6 2.4 copy-done
  337.1 0.3 select_reduce_fusion
  337.6 0.6 multiply_divide_fusion
  338.2 4.4 %convolution_convert_fusion.2 = bf16[64,3584]{1,0:T(8,128)(2,1)} fusion(bf16[768,3584]{1,0:T(8,128)(2,1)} %bitcast.69, bf16[768,64]{0,1:T(8,128)(2,1)S(1)} %convert_reduce_fusion), kind=kOutput, calls=%fused_computation.18 | convolution fusion | flops 352550912 | bytes 6062080 | tf_op jit(solution)/shard_map/dot_general | solution.py:24
  342.6 7.7 %fusion.24 = (bf16[1,256,3584]{2,1,0:T(8,128)(2,1)}, bf16[1,256,3584]{2,1,0:T(8,128)(2,1)}, bf16[1,256,3584]{2,1,0:T(8,128)(2,1)}) fusion(bf16[256,3584]{1,0:T(8,128)(2,1)} %reduce-scatter.2.cloned.1.call-done, bf16[1,256,3584]{2,1,0:T(8,128)(2,1)} %param.19, bf16[1,256,3584]{2,1,0:T(8,128)(2,1)} %param.18, bf16[1,256,3584]{2,1,0:T(8,128)(2,1)S(1)} %copy-done.1), kind=kLoop, calls=%fused_computation.39 | loop fusion | flops 21102592 | bytes 12845056 | tf_op jit(solution)/shard_map/convert_element_type | solution.py:118
  (39 shorter events, 1.0 us)
Async XLA Ops:
  7.2 0.8 copy-start.5
  7.2 2.9 copy-start.4
  7.2 4.0 %copy-start.2 = (bf16[64,3584]{1,0:T(8,128)(2,1)S(1)}, bf16[64,3584]{1,0:T(8,128)(2,1)}, u32[]{:S(2)}) copy-start(bf16[64,3584]{1,0:T(8,128)(2,1)} %param.13) | copy-start | bytes 1376260
  7.2 4.0 %copy-start.3 = (bf16[64,3584]{1,0:T(8,128)(2,1)S(1)}, bf16[64,3584]{1,0:T(8,128)(2,1)}, u32[]{:S(2)}) copy-start(bf16[64,3584]{1,0:T(8,128)(2,1)} %param.12) | copy-start | bytes 1376260
  7.2 159.1 %all-gather.3.cloned.1.call-start = ((), (), s32[]{:S(2)}) async-start(), calls=%async_computation.3 | async-start | bytes 18350080 | tf_op jit(solution)/shard_map/all_gather | solution.py:60
  18.8 141.0 %all-to-all-start = ((bf16[32,24,7168]{2,1,0:T(8,128)(2,1)}), bf16[32,24,7168]{2,1,0:T(8,128)(2,1)}, u32[]{:S(2)}, u32[]{:S(2)}) async-start(bf16[32,24,7168]{2,1,0:T(8,128)(2,1)} %scatter.6), calls=%async_computation | async-start | bytes 22020096 | tf_op jit(solution)/shard_map/all_to_all | solution.py:63
  27.5 201.9 %all-gather.5.cloned.1.call-start = ((), (), s32[]{:S(2)}) async-start(), calls=%async_computation.4 | async-start | bytes 9175040 | tf_op jit(solution)/shard_map/all_gather | solution.py:61
  28.2 314.4 %reduce-scatter.2.cloned.1.call-start = ((), (), s32[]{:S(2)}) async-start(), calls=%async_computation.5 | async-start | bytes 9175040 | tf_op jit(solution)/shard_map/reduce_scatter | solution.py:79
  166.4 10.6 %copy-start.6 = (bf16[1,2,3584,1024]{3,2,1,0:T(8,128)(2,1)S(1)}, bf16[1,2,3584,1024]{3,2,1,0:T(8,128)(2,1)}, u32[]{:S(2)}) copy-start(bf16[1,2,3584,1024]{3,2,1,0:T(8,128)(2,1)} %all-gather.3.cloned.1.call-done) | copy-start | bytes 44040196
  177.0 10.3 %copy-start.7 = (f32[768,1024]{1,0:T(8,128)}, f32[768,1024]{1,0:T(8,128)S(1)}, u32[]{:S(2)}) copy-start(f32[768,1024]{1,0:T(8,128)S(1)} %fusion.5) | copy-start | bytes 9437188
  334.6 2.4 copy-start
  336.9 5.7 %copy-start.1 = (bf16[1,256,3584]{2,1,0:T(8,128)(2,1)S(1)}, bf16[1,256,3584]{2,1,0:T(8,128)(2,1)}, u32[]{:S(2)}) copy-start(bf16[1,256,3584]{2,1,0:T(8,128)(2,1)} %param.17) | copy-start | bytes 5505028
Sparse Core Ops, SparseCore 0:
  9.7 142.1 all-gather.2
  153.5 75.8 all-gather.4
  231.8 73.5 reduce-scatter.1

commit v7 on v6

--- a/solution.py
+++ b/solution.py
@@ -75,18 +75,16 @@
     hidden = (silu_gate * pre_up).astype(jnp.bfloat16)
     scaled = (slot_weight[:, None] * gs_rows.astype(jnp.float32)).astype(jnp.bfloat16)
     local_grad = contract_first(hidden, scaled).astype(jnp.bfloat16)
-    local_grad, gs_rows = lax.optimization_barrier((local_grad, gs_rows))
+    gate_factor = slot_weight[:, None] * (pre_up * sig_gate * (1.0 + pre_gate * (1.0 - sig_gate)))
+    up_factor = slot_weight[:, None] * silu_gate
+    factors = jnp.stack([gate_factor, up_factor], axis=1)
+    local_grad, factors, gs_rows = lax.optimization_barrier((local_grad, factors, gs_rows))
     grad_shard = lax.psum_scatter(local_grad, "dp", scatter_dimension=0, tiled=True).astype(
         jnp.float32
     )
     back_raw = contract_last(gs_rows, full_down)
     affinity = jnp.sum(hidden.astype(jnp.float32) * back_raw, axis=1).astype(jnp.bfloat16)
-    back = slot_weight[:, None] * back_raw
-    gate_grad = (back * pre_up * sig_gate * (1.0 + pre_gate * (1.0 - sig_gate))).astype(
-        jnp.bfloat16
-    )
-    up_grad = (back * silu_gate).astype(jnp.bfloat16)
-    grads = jnp.stack([gate_grad, up_grad], axis=1)
+    grads = (back_raw[:, None, :] * factors).astype(jnp.bfloat16)
     route_in = lax.dot_general(
         grads, full_gu, (((1, 2), (0, 2)), ((), ())), preferred_element_type=jnp.float32
     ).astype(jnp.bfloat16)

time: 357 us -> 358 us (level)
  waiting for transfers between devices: 164 us -> 160 us
    all_gather x1, waiting for transfers between devices: 31.2 us -> 27.4 us  [shards(): full_down = lax.all_gather(down, 'dp', axis=1, tiled=True)[0]]
  transfers between devices with their start and end apart: 4 -> 4, of which waited for: 2 -> 2; matrix products, arithmetic and copies ran while one was open for 24% -> 26% of each run, Pallas kernels for 0% -> 0%
where the time goes in v7:
time: 358 us
  waiting for transfers between devices  160 us (45%)
  matrix products  74.3 us (21%)
  blocking collectives  72.6 us (20%)
  other arithmetic  14.9 us (4%)
  between operations  13.9 us (4%)
  local copies, waits for them, and re-layouts  13.2 us (4%)
  starting transfers between devices  8.92 us (2%)
    all_to_all x1, waiting for transfers between devices, shards(): lax.all_to_all(send_rows, 'expert', split_axis=0, concat_axis=0, tiled=True)  131 us
    all_to_all x1, blocking collectives, shards(): lax.all_to_all(ret_rows, 'expert', split_axis=0, concat_axis=0, tiled=True)  72.6 us
    all_gather x1, waiting for transfers between devices, shards(): full_down = lax.all_gather(down, 'dp', axis=1, tiled=True)[0]  27.4 us
    dot_general x1, matrix products, shards(): lax.dot_general(grads, full_gu, (((1, 2), (0, 2)), ((), ())), preferred_e...  20.7 us
    dot_general x2, matrix products, contract_first(): lax.dot_general(left, right, (((0,), (0,)), ((), ())), preferred_element_...  15.4 us
    dot_general x1, matrix products, contract_last(): lax.dot_general(left, right, (((1,), (1,)), ((), ())), preferred_element_...  11 us
    dot_general x1, matrix products, shards(): pre_gate = jnp.dot(xs_rows, gate_w, preferred_element_type=jnp.float32)  11 us
    dot_general x1, matrix products, shards(): pre_up = jnp.dot(xs_rows, up_w, preferred_element_type=jnp.float32)  10.4 us
  transfers between devices with their start and end apart: 4, of which 2 were waited for; matrix products, arithmetic and copies ran while one was open for 26% of the time, Pallas kernels for 0%

profile of v7, /device:TPU:1, one launch (start us, length us, event | category | flops | bytes accessed | tf_op | source)
XLA Modules:
  0.0 358.0 jit_solution(5890677800768209266)
XLA Ops:
  7.3 0.7 all-gather.3.cloned.1.call-update
  8.0 0.1 eq.50
  8.2 1.2 reduce-window.6
  9.4 0.2 slice_reduce_fusion
  9.8 0.1 reshape.188
  9.9 0.1 fusion.28
  10.1 0.2 select_reduce_fusion.1
  10.4 0.1 convert_element_type.143
  10.6 0.5 convert_reduce_fusion
  11.2 5.7 %convolution_convert_fusion = bf16[768,7168]{1,0:T(8,128)(2,1)} fusion(bf16[64,3584]{1,0:T(8,128)(2,1)S(1)} %copy-done.2, bf16[64,3584]{1,0:T(8,128)(2,1)S(1)} %copy-done.3, bf16[768,64]{0,1:T(8,128)(2,1)S(1)} %convert_reduce_fusion), kind=kOutput, calls=%fused_computation.2 | convolution fusion | flops 711983104 | bytes 12025856 | tf_op jit(solution)/shard_map/dot_general | solution.py:54
  16.9 1.9 scatter.6
  18.8 8.6 %all-to-all-start = ((bf16[32,24,7168]{2,1,0:T(8,128)(2,1)}), bf16[32,24,7168]{2,1,0:T(8,128)(2,1)}, u32[]{:S(2)}, u32[]{:S(2)}) async-start(bf16[32,24,7168]{2,1,0:T(8,128)(2,1)} %scatter.6), calls=%async_computation | async-start | bytes 22020096 | tf_op jit(solution)/shard_map/all_to_all | solution.py:63
  27.5 0.7 all-gather.5.cloned.1.call-update
  28.2 0.2 reduce-scatter.2.cloned.1.call-start
  28.4 131.3 %all-to-all-done = bf16[32,24,7168]{2,1,0:T(8,128)(2,1)} async-done(((bf16[32,24,7168]{2,1,0:T(8,128)(2,1)}), bf16[32,24,7168]{2,1,0:T(8,128)(2,1)}, u32[]{:S(2)}, u32[]{:S(2)}) %all-to-all-start) | async-done | bytes 11010080 | tf_op jit(solution)/shard_map/all_to_all | solution.py:63
  159.8 0.9 fusion.33
  160.7 5.6 %slice.89 = bf16[768,3584]{1,0:T(8,128)(2,1)} slice(bf16[768,7168]{1,0:T(8,128)(2,1)} %bitcast.2), slice={[0:768], [3584:7168]} | slice | bytes 11010048 | tf_op jit(solution)/shard_map/slice | solution.py:67
  166.3 10.4 %fusion.4 = f32[768,1024]{1,0:T(8,128)S(1)} fusion(bf16[1,2,3584,1024]{3,2,1,0:T(8,128)(2,1)} %all-gather.3.cloned.1.call-done, bf16[768,7168]{1,0:T(8,128)(2,1)} %bitcast.2), kind=kOutput, calls=%fused_computation.7 | convolution fusion | flops 5637144576 | bytes 15990784 | tf_op jit(solution)/shard_map/dot_general | solution.py:72
  176.8 11.0 %multiply_bitcast_fusion.1 = (f32[768,1,1024]{2,0,1:T(8,128)S(1)}, bf16[768,1024]{1,0:T(8,128)(2,1)S(1)}, f32[768,1,1024]{2,0,1:T(8,128)S(1)}) fusion(f32[768,1024]{1,0:T(8,128)S(1)} %fusion.4, f32[768]{0:T(1024)S(1)} %reshape.189, bf16[1,2,3584,1024]{3,2,1,0:T(8,128)(2,1)} %all-gather.3.cloned.1.call-done, bf16[768,7168]{1,0:T(8,128)(2,1)} %bitcast.2), kind=kOutput, calls=%fused_computation.34 | convolution fusion | flops 5647368192 | bytes 23858176 | tf_op jit(solution)/shard_map/dot_general | solution.py:71
  187.8 3.2 pad_maximum_fusion
  191.0 11.0 %convolution_convert_fusion.1 = bf16[1024,3584]{1,0:T(8,128)(2,1)} fusion(bf16[768,1024]{1,0:T(8,128)(2,1)S(1)} %get-tuple-element.51, f32[768]{0:T(1024)S(1)} %reshape.189, bf16[768,7168]{1,0:T(8,128)(2,1)} %bitcast.2), kind=kOutput, calls=%fused_computation.5 | convolution fusion | flops 5649072128 | bytes 14420992 | tf_op jit(solution)/shard_map/dot_general | solution.py:24
  202.1 27.4 %all-gather.5.cloned.1.call-done = bf16[1,1024,3584]{2,1,0:T(8,128)(2,1)} async-done(((bf16[1,256,3584]{2,1,0:T(8,128)(2,1)}), bf16[1,1024,3584]{2,1,0:T(8,128)(2,1)}) %all-gather.5.cloned.1.call-update) | async-done | bytes 7340048 | tf_op jit(solution)/shard_map/all_gather | solution.py:61
  229.4 11.0 %multiply_reduce_fusion = (bf16[768]{0:T(1024)(128)(2,1)S(1)}, f32[768,1024]{1,0:T(8,128)}) fusion(bf16[768,1024]{1,0:T(8,128)(2,1)S(1)} %get-tuple-element.51, bf16[768,3584]{1,0:T(8,128)(2,1)} %slice.89, bf16[1,1024,3584]{2,1,0:T(8,128)(2,1)} %all-gather.5.cloned.1.call-done), kind=kOutput, calls=%fused_computation.31 | convolution fusion | flops 5639502848 | bytes 17565184 | tf_op jit(solution)/shard_map/dot_general | solution.py:18
  240.5 0.1 convert_element_type.144
  240.6 20.7 %bitcast_convert_fusion = bf16[768,3584]{1,0:T(8,128)(2,1)} fusion(bf16[1,2,3584,1024]{3,2,1,0:T(8,128)(2,1)} %all-gather.3.cloned.1.call-done, f32[768,2,1024]{2,0,1:T(8,128)} %pad_maximum_fusion, f32[768,1024]{1,0:T(8,128)} %get-tuple-element.57), kind=kOutput, calls=%fused_computation.3 | convolution fusion | flops 11280187392 | bytes 29622272 | tf_op jit(solution)/shard_map/dot_general | solution.py:88
  261.3 1.9 scatter.9
  263.1 72.6 %all_to_all.10 = bf16[32,24,3584]{2,1,0:T(8,128)(2,1)S(1)} all-to-all(bf16[32,24,3584]{2,1,0:T(8,128)(2,1)} %scatter.9), channel_id=1, replica_groups=mesh['expert'=32,'dp'=4] {'expert'}, dimensions={0} | all-to-all | bytes 11010048 | tf_op jit(solution)/shard_map/all_to_all | solution.py:93
  335.7 2.4 copy-done
  338.3 0.3 select_reduce_fusion
  338.8 0.6 multiply_divide_fusion
  339.4 4.4 %convolution_convert_fusion.2 = bf16[64,3584]{1,0:T(8,128)(2,1)} fusion(bf16[768,3584]{1,0:T(8,128)(2,1)} %bitcast.69, bf16[768,64]{0,1:T(8,128)(2,1)S(1)} %convert_reduce_fusion), kind=kOutput, calls=%fused_computation.20 | convolution fusion | flops 352550912 | bytes 6062080 | tf_op jit(solution)/shard_map/dot_general | solution.py:24
  343.8 7.7 %fusion.22 = (bf16[1,256,3584]{2,1,0:T(8,128)(2,1)}, bf16[1,256,3584]{2,1,0:T(8,128)(2,1)}, bf16[1,256,3584]{2,1,0:T(8,128)(2,1)}) fusion(bf16[256,3584]{1,0:T(8,128)(2,1)} %reduce-scatter.2.cloned.1.call-done, bf16[1,256,3584]{2,1,0:T(8,128)(2,1)} %param.19, bf16[1,256,3584]{2,1,0:T(8,128)(2,1)} %param.18, bf16[1,256,3584]{2,1,0:T(8,128)(2,1)S(1)} %copy-done.1), kind=kLoop, calls=%fused_computation.39 | loop fusion | flops 21102592 | bytes 12845056 | tf_op jit(solution)/shard_map/convert_element_type | solution.py:116
  (36 shorter events, 1.1 us)
Async XLA Ops:
  7.2 0.8 copy-start.5
  7.2 2.5 copy-start.4
  7.2 4.0 %copy-start.3 = (bf16[64,3584]{1,0:T(8,128)(2,1)S(1)}, bf16[64,3584]{1,0:T(8,128)(2,1)}, u32[]{:S(2)}) copy-start(bf16[64,3584]{1,0:T(8,128)(2,1)} %param.12) | copy-start | bytes 1376260
  7.2 4.0 %copy-start.2 = (bf16[64,3584]{1,0:T(8,128)(2,1)S(1)}, bf16[64,3584]{1,0:T(8,128)(2,1)}, u32[]{:S(2)}) copy-start(bf16[64,3584]{1,0:T(8,128)(2,1)} %param.13) | copy-start | bytes 1376260
  7.2 159.1 %all-gather.3.cloned.1.call-start = ((), (), s32[]{:S(2)}) async-start(), calls=%async_computation.3 | async-start | bytes 18350080 | tf_op jit(solution)/shard_map/all_gather | solution.py:60
  18.8 141.0 %all-to-all-start = ((bf16[32,24,7168]{2,1,0:T(8,128)(2,1)}), bf16[32,24,7168]{2,1,0:T(8,128)(2,1)}, u32[]{:S(2)}, u32[]{:S(2)}) async-start(bf16[32,24,7168]{2,1,0:T(8,128)(2,1)} %scatter.6), calls=%async_computation | async-start | bytes 22020096 | tf_op jit(solution)/shard_map/all_to_all | solution.py:63
  27.4 202.0 %all-gather.5.cloned.1.call-start = ((), (), s32[]{:S(2)}) async-start(), calls=%async_computation.4 | async-start | bytes 9175040 | tf_op jit(solution)/shard_map/all_gather | solution.py:61
  28.2 315.6 %reduce-scatter.2.cloned.1.call-start = ((), (), s32[]{:S(2)}) async-start(), calls=%async_computation.5 | async-start | bytes 9175040 | tf_op jit(solution)/shard_map/reduce_scatter | solution.py:82
  335.7 2.4 copy-start
  338.1 5.7 %copy-start.1 = (bf16[1,256,3584]{2,1,0:T(8,128)(2,1)S(1)}, bf16[1,256,3584]{2,1,0:T(8,128)(2,1)}, u32[]{:S(2)}) copy-start(bf16[1,256,3584]{2,1,0:T(8,128)(2,1)} %param.17) | copy-start | bytes 5505028
Sparse Core Ops, SparseCore 0:
  9.7 142.1 all-gather.2
  153.6 75.8 all-gather.4
  231.9 73.5 reduce-scatter.1

commit v8 on v6

--- a/solution.py
+++ b/solution.py
@@ -102,13 +102,15 @@
     mixed = jnp.sum(route_affinity * scores, axis=1, keepdims=True) / score_sum
     router_grad = ROUTE_SCALE * scores * (1.0 - scores) * (route_affinity - mixed) / score_sum
 
-    down_grad = (grad_shard / data_ways)[None]
+    down_grad = (grad_shard * (1.0 / data_ways))[None]
     corr_one = 1.0 - BETA_ONE**STEP
     corr_two = 1.0 - BETA_TWO**STEP
     down_wide = down.astype(jnp.float32)
     first = BETA_ONE * moment1.astype(jnp.float32) + (1.0 - BETA_ONE) * down_grad
     second = BETA_TWO * moment2.astype(jnp.float32) + (1.0 - BETA_TWO) * down_grad * down_grad
-    update = first / corr_one / (jnp.sqrt(second / corr_two) + EPSILON) + DECAY * down_wide
+    update = (first * (1.0 / corr_one)) / (
+        jnp.sqrt(second) * (1.0 / corr_two**0.5) + EPSILON
+    ) + DECAY * down_wide
     new_down = (down_wide - LEARN_RATE * update).astype(jnp.bfloat16)
     return (
         token_grad,

time: 357 us -> 357 us (level)
  no operation moved by 1% of the time
where the time goes in v8:
time: 357 us; the launch traced here: 356 us
  waiting for transfers between devices  164 us (46%)
  blocking collectives  72.7 us (20%)
  matrix products  72.4 us (20%)
  between operations  13.9 us (4%)
  local copies, waits for them, and re-layouts  13.2 us (4%)
  other arithmetic  11.2 us (3%)
  starting transfers between devices  8.92 us (2%)
    all_to_all x1, waiting for transfers between devices, shards(): lax.all_to_all(send_rows, 'expert', split_axis=0, concat_axis=0, tiled=True)  131 us
    all_to_all x1, blocking collectives, shards(): lax.all_to_all(ret_rows, 'expert', split_axis=0, concat_axis=0, tiled=True)  72.7 us
    all_gather x1, waiting for transfers between devices, shards(): full_down = lax.all_gather(down, 'dp', axis=1, tiled=True)[0]  31.2 us
    dot_general x1, matrix products, shards(): lax.dot_general(grads, full_gu, (((1, 2), (0, 2)), ((), ())), preferred_e...  17.2 us
    dot_general x2, matrix products, contract_first(): lax.dot_general(left, right, (((0,), (0,)), ((), ())), preferred_element_...  15.3 us
    dot_general x1, matrix products, contract_last(): lax.dot_general(left, right, (((1,), (1,)), ((), ())), preferred_element_...  13.3 us
    dot_general x1, matrix products, shards(): pre_gate = jnp.dot(xs_rows, gate_w, preferred_element_type=jnp.float32)  10.6 us
    dot_general x1, matrix products, shards(): pre_up = jnp.dot(xs_rows, up_w, preferred_element_type=jnp.float32)  10.3 us
  transfers between devices with their start and end apart: 4, of which 2 were waited for; matrix products, arithmetic and copies ran while one was open for 24% of the time, Pallas kernels for 0%

profile of v8, /device:TPU:1, one launch (start us, length us, event | category | flops | bytes accessed | tf_op | source)
XLA Modules:
  0.0 356.3 jit_solution(4507293132976574887)
XLA Ops:
  7.3 0.7 all-gather.3.cloned.1.call-update
  8.0 0.1 eq.46
  8.2 1.2 reduce-window.6
  9.4 0.2 slice_reduce_fusion
  9.7 0.1 fusion.32
  9.8 0.1 reduce_sum.66
  10.2 0.1 reshape.187
  10.3 0.2 select_reduce_fusion.1
  10.5 0.1 convert_element_type.147
  10.6 0.5 convert_reduce_fusion
  11.2 5.8 %convolution_convert_fusion = bf16[768,7168]{1,0:T(8,128)(2,1)} fusion(bf16[64,3584]{1,0:T(8,128)(2,1)S(1)} %copy-done.2, bf16[64,3584]{1,0:T(8,128)(2,1)S(1)} %copy-done.3, bf16[768,64]{0,1:T(8,128)(2,1)S(1)} %convert_reduce_fusion), kind=kOutput, calls=%fused_computation.2 | convolution fusion | flops 711983104 | bytes 12025856 | tf_op jit(solution)/shard_map/dot_general | solution.py:54
  17.0 1.9 scatter.6
  18.8 8.6 %all-to-all-start = ((bf16[32,24,7168]{2,1,0:T(8,128)(2,1)}), bf16[32,24,7168]{2,1,0:T(8,128)(2,1)}, u32[]{:S(2)}, u32[]{:S(2)}) async-start(bf16[32,24,7168]{2,1,0:T(8,128)(2,1)} %scatter.6), calls=%async_computation | async-start | bytes 22020096 | tf_op jit(solution)/shard_map/all_to_all | solution.py:63
  27.5 0.7 all-gather.5.cloned.1.call-update
  28.2 0.2 reduce-scatter.2.cloned.1.call-start
  28.5 131.3 %all-to-all-done = bf16[32,24,7168]{2,1,0:T(8,128)(2,1)} async-done(((bf16[32,24,7168]{2,1,0:T(8,128)(2,1)}), bf16[32,24,7168]{2,1,0:T(8,128)(2,1)}, u32[]{:S(2)}, u32[]{:S(2)}) %all-to-all-start) | async-done | bytes 11010080 | tf_op jit(solution)/shard_map/all_to_all | solution.py:63
  159.8 0.9 fusion.37
  160.8 5.6 %slice.89 = bf16[768,3584]{1,0:T(8,128)(2,1)} slice(bf16[768,7168]{1,0:T(8,128)(2,1)} %bitcast.2), slice={[0:768], [3584:7168]} | slice | bytes 11010048 | tf_op jit(solution)/shard_map/slice | solution.py:67
  166.4 10.6 %fusion.5 = f32[768,1024]{1,0:T(8,128)S(1)} fusion(bf16[1,2,3584,1024]{3,2,1,0:T(8,128)(2,1)} %all-gather.3.cloned.1.call-done, bf16[768,7168]{1,0:T(8,128)(2,1)} %bitcast.2), kind=kOutput, calls=%fused_computation.9 | convolution fusion | flops 5637144576 | bytes 15990784 | tf_op jit(solution)/shard_map/dot_general | solution.py:71
  177.0 10.3 %multiply_convert_fusion.4 = (bf16[768,1024]{1,0:T(8,128)(2,1)S(1)}, f32[768,1024]{1,0:T(8,128)}) fusion(f32[768,1024]{1,0:T(8,128)S(1)} %fusion.5, bf16[1,2,3584,1024]{3,2,1,0:T(8,128)(2,1)S(1)} %copy-done.6, bf16[768,7168]{1,0:T(8,128)(2,1)} %bitcast.2), kind=kOutput, calls=%fused_computation.35 | convolution fusion | flops 5641863168 | bytes 20709376 | tf_op jit(solution)/shard_map/dot_general | solution.py:72
  187.2 10.9 %convolution_convert_fusion.1 = bf16[1024,3584]{1,0:T(8,128)(2,1)} fusion(bf16[768,1024]{1,0:T(8,128)(2,1)S(1)} %get-tuple-element.54, f32[768]{0:T(1024)S(1)} %reshape.188, bf16[768,7168]{1,0:T(8,128)(2,1)} %bitcast.2), kind=kOutput, calls=%fused_computation.5 | convolution fusion | flops 5649072128 | bytes 14420992 | tf_op jit(solution)/shard_map/dot_general | solution.py:24
  198.2 31.2 %all-gather.5.cloned.1.call-done = bf16[1,1024,3584]{2,1,0:T(8,128)(2,1)} async-done(((bf16[1,256,3584]{2,1,0:T(8,128)(2,1)}), bf16[1,1024,3584]{2,1,0:T(8,128)(2,1)}) %all-gather.5.cloned.1.call-update) | async-done | bytes 7340048 | tf_op jit(solution)/shard_map/all_gather | solution.py:61
  229.4 13.3 %fusion.26 = (bf16[768,1,1024]{2,0,1:T(8,128)(2,1)S(1)}, bf16[768,1,1024]{2,0,1:T(8,128)(2,1)}, bf16[768]{0:T(1024)(128)(2,1)S(1)}) fusion(f32[768,1024]{1,0:T(8,128)} %copy-done.7, f32[768,1024]{1,0:T(8,128)} %get-tuple-element.55, f32[768]{0:T(1024)S(1)} %reshape.188, bf16[768,1024]{1,0:T(8,128)(2,1)S(1)} %get-tuple-element.54, ...), kind=kOutput, calls=%fused_computation.46 | convolution fusion | flops 5650512896 | bytes 23859712 | tf_op jit(solution)/shard_map/dot_general | solution.py:18
  242.7 0.1 convert_element_type.148
  242.8 17.2 %bitcast_convert_fusion = bf16[768,3584]{1,0:T(8,128)(2,1)} fusion(bf16[1,2,3584,1024]{3,2,1,0:T(8,128)(2,1)} %all-gather.3.cloned.1.call-done, bf16[768,1,1024]{2,0,1:T(8,128)(2,1)} %get-tuple-element.49, bf16[768,1,1024]{2,0,1:T(8,128)(2,1)S(1)} %get-tuple-element.48), kind=kOutput, calls=%fused_computation.3 | convolution fusion | flops 11278614528 | bytes 23330816 | tf_op jit(solution)/shard_map/dot_general | solution.py:90
  260.0 1.9 scatter.9
  261.9 72.7 %all_to_all.10 = bf16[32,24,3584]{2,1,0:T(8,128)(2,1)S(1)} all-to-all(bf16[32,24,3584]{2,1,0:T(8,128)(2,1)} %scatter.9), channel_id=1, replica_groups=mesh['expert'=32,'dp'=4] {'expert'}, dimensions={0} | all-to-all | bytes 11010048 | tf_op jit(solution)/shard_map/all_to_all | solution.py:95
  334.6 2.4 copy-done
  337.1 0.3 select_reduce_fusion
  337.6 0.6 multiply_divide_fusion
  338.2 4.4 %convolution_convert_fusion.2 = bf16[64,3584]{1,0:T(8,128)(2,1)} fusion(bf16[768,3584]{1,0:T(8,128)(2,1)} %bitcast.69, bf16[768,64]{0,1:T(8,128)(2,1)S(1)} %convert_reduce_fusion), kind=kOutput, calls=%fused_computation.18 | convolution fusion | flops 352550912 | bytes 6062080 | tf_op jit(solution)/shard_map/dot_general | solution.py:24
  342.6 7.1 %fusion.24 = (bf16[1,256,3584]{2,1,0:T(8,128)(2,1)}, bf16[1,256,3584]{2,1,0:T(8,128)(2,1)}, bf16[1,256,3584]{2,1,0:T(8,128)(2,1)}) fusion(bf16[256,3584]{1,0:T(8,128)(2,1)} %reduce-scatter.2.cloned.1.call-done, bf16[1,256,3584]{2,1,0:T(8,128)(2,1)} %param.19, bf16[1,256,3584]{2,1,0:T(8,128)(2,1)} %param.18, bf16[1,256,3584]{2,1,0:T(8,128)(2,1)S(1)} %copy-done.1), kind=kLoop, calls=%fused_computation.39 | loop fusion | flops 21102592 | bytes 12845056 | tf_op jit(solution)/shard_map/convert_element_type | solution.py:120
  (39 shorter events, 1.0 us)
Async XLA Ops:
  7.2 0.8 copy-start.5
  7.2 2.9 copy-start.4
  7.2 4.0 %copy-start.2 = (bf16[64,3584]{1,0:T(8,128)(2,1)S(1)}, bf16[64,3584]{1,0:T(8,128)(2,1)}, u32[]{:S(2)}) copy-start(bf16[64,3584]{1,0:T(8,128)(2,1)} %param.13) | copy-start | bytes 1376260
  7.2 4.0 %copy-start.3 = (bf16[64,3584]{1,0:T(8,128)(2,1)S(1)}, bf16[64,3584]{1,0:T(8,128)(2,1)}, u32[]{:S(2)}) copy-start(bf16[64,3584]{1,0:T(8,128)(2,1)} %param.12) | copy-start | bytes 1376260
  7.2 159.1 %all-gather.3.cloned.1.call-start = ((), (), s32[]{:S(2)}) async-start(), calls=%async_computation.3 | async-start | bytes 18350080 | tf_op jit(solution)/shard_map/all_gather | solution.py:60
  18.8 141.0 %all-to-all-start = ((bf16[32,24,7168]{2,1,0:T(8,128)(2,1)}), bf16[32,24,7168]{2,1,0:T(8,128)(2,1)}, u32[]{:S(2)}, u32[]{:S(2)}) async-start(bf16[32,24,7168]{2,1,0:T(8,128)(2,1)} %scatter.6), calls=%async_computation | async-start | bytes 22020096 | tf_op jit(solution)/shard_map/all_to_all | solution.py:63
  27.5 201.9 %all-gather.5.cloned.1.call-start = ((), (), s32[]{:S(2)}) async-start(), calls=%async_computation.4 | async-start | bytes 9175040 | tf_op jit(solution)/shard_map/all_gather | solution.py:61
  28.2 314.4 %reduce-scatter.2.cloned.1.call-start = ((), (), s32[]{:S(2)}) async-start(), calls=%async_computation.5 | async-start | bytes 9175040 | tf_op jit(solution)/shard_map/reduce_scatter | solution.py:79
  166.4 10.6 %copy-start.6 = (bf16[1,2,3584,1024]{3,2,1,0:T(8,128)(2,1)S(1)}, bf16[1,2,3584,1024]{3,2,1,0:T(8,128)(2,1)}, u32[]{:S(2)}) copy-start(bf16[1,2,3584,1024]{3,2,1,0:T(8,128)(2,1)} %all-gather.3.cloned.1.call-done) | copy-start | bytes 44040196
  177.0 10.3 %copy-start.7 = (f32[768,1024]{1,0:T(8,128)}, f32[768,1024]{1,0:T(8,128)S(1)}, u32[]{:S(2)}) copy-start(f32[768,1024]{1,0:T(8,128)S(1)} %fusion.5) | copy-start | bytes 9437188
  334.6 2.4 copy-start
  336.9 5.7 %copy-start.1 = (bf16[1,256,3584]{2,1,0:T(8,128)(2,1)S(1)}, bf16[1,256,3584]{2,1,0:T(8,128)(2,1)}, u32[]{:S(2)}) copy-start(bf16[1,256,3584]{2,1,0:T(8,128)(2,1)} %param.17) | copy-start | bytes 5505028
Sparse Core Ops, SparseCore 0:
  9.7 142.1 all-gather.2
  153.5 75.8 all-gather.4
  231.8 73.5 reduce-scatter.1

commit v9 on v7

--- a/solution.py
+++ b/solution.py
@@ -85,6 +85,7 @@
     back_raw = contract_last(gs_rows, full_down)
     affinity = jnp.sum(hidden.astype(jnp.float32) * back_raw, axis=1).astype(jnp.bfloat16)
     grads = (back_raw[:, None, :] * factors).astype(jnp.bfloat16)
+    grads = lax.optimization_barrier(grads)
     route_in = lax.dot_general(
         grads, full_gu, (((1, 2), (0, 2)), ((), ())), preferred_element_type=jnp.float32
     ).astype(jnp.bfloat16)
@@ -100,13 +101,15 @@
     mixed = jnp.sum(route_affinity * scores, axis=1, keepdims=True) / score_sum
     router_grad = ROUTE_SCALE * scores * (1.0 - scores) * (route_affinity - mixed) / score_sum
 
-    down_grad = (grad_shard / data_ways)[None]
+    down_grad = (grad_shard * (1.0 / data_ways))[None]
     corr_one = 1.0 - BETA_ONE**STEP
     corr_two = 1.0 - BETA_TWO**STEP
     down_wide = down.astype(jnp.float32)
     first = BETA_ONE * moment1.astype(jnp.float32) + (1.0 - BETA_ONE) * down_grad
     second = BETA_TWO * moment2.astype(jnp.float32) + (1.0 - BETA_TWO) * down_grad * down_grad
-    update = first / corr_one / (jnp.sqrt(second / corr_two) + EPSILON) + DECAY * down_wide
+    update = (first * (1.0 / corr_one)) / (
+        jnp.sqrt(second) * (1.0 / corr_two**0.5) + EPSILON
+    ) + DECAY * down_wide
     new_down = (down_wide - LEARN_RATE * update).astype(jnp.bfloat16)
     return (
         token_grad,

time: 358 us -> 358 us (level)
  matrix products: 74.3 us -> 70.1 us
  other arithmetic: 14.9 us -> 18.9 us
    convert_element_type x0 -> x1, other arithmetic: none -> 4.6 us  [shards(): grads = (back_raw[:, None, :] * factors).astype(jnp.bfloat16)]
    dot_general x1, matrix products: 20.7 us -> 16.7 us  [shards(): lax.dot_general(grads, full_gu, (((1, 2), (0, 2)), ((), ())), preferred_e...]
where the time goes in v9:
time: 358 us; the launch traced here: 357 us
  waiting for transfers between devices  159 us (44%)
  blocking collectives  73 us (20%)
  matrix products  70.1 us (20%)
  other arithmetic  18.9 us (5%)
  between operations  13.9 us (4%)
  local copies, waits for them, and re-layouts  13.2 us (4%)
  starting transfers between devices  8.92 us (2%)
    all_to_all x1, waiting for transfers between devices, shards(): lax.all_to_all(send_rows, 'expert', split_axis=0, concat_axis=0, tiled=True)  131 us
    all_to_all x1, blocking collectives, shards(): lax.all_to_all(ret_rows, 'expert', split_axis=0, concat_axis=0, tiled=True)  73 us
    all_gather x1, waiting for transfers between devices, shards(): full_down = lax.all_gather(down, 'dp', axis=1, tiled=True)[0]  26.5 us
    dot_general x1, matrix products, shards(): lax.dot_general(grads, full_gu, (((1, 2), (0, 2)), ((), ())), preferred_e...  16.7 us
    dot_general x2, matrix products, contract_first(): lax.dot_general(left, right, (((0,), (0,)), ((), ())), preferred_element_...  15.4 us
    dot_general x1, matrix products, shards(): pre_up = jnp.dot(xs_rows, up_w, preferred_element_type=jnp.float32)  11.7 us
    dot_general x1, matrix products, shards(): pre_gate = jnp.dot(xs_rows, gate_w, preferred_element_type=jnp.float32)  10.6 us
    dot_general x1, matrix products, contract_last(): lax.dot_general(left, right, (((1,), (1,)), ((), ())), preferred_element_...  9.92 us
  transfers between devices with their start and end apart: 4, of which 2 were waited for; matrix products, arithmetic and copies ran while one was open for 26% of the time, Pallas kernels for 0%

profile of v9, /device:TPU:1, one launch (start us, length us, event | category | flops | bytes accessed | tf_op | source)
XLA Modules:
  0.0 357.4 jit_solution(432645323670457254)
XLA Ops:
  7.3 0.7 all-gather.3.cloned.1.call-update
  8.2 1.2 reduce-window.6
  9.4 0.2 slice_reduce_fusion
  9.8 0.1 reshape.188
  9.9 0.1 fusion.27
  10.1 0.2 select_reduce_fusion.1
  10.4 0.1 convert_element_type.143
  10.6 0.5 convert_reduce_fusion
  11.2 5.7 %convolution_convert_fusion = bf16[768,7168]{1,0:T(8,128)(2,1)} fusion(bf16[64,3584]{1,0:T(8,128)(2,1)S(1)} %copy-done.2, bf16[64,3584]{1,0:T(8,128)(2,1)S(1)} %copy-done.3, bf16[768,64]{0,1:T(8,128)(2,1)S(1)} %convert_reduce_fusion), kind=kOutput, calls=%fused_computation.2 | convolution fusion | flops 711983104 | bytes 12025856 | tf_op jit(solution)/shard_map/dot_general | solution.py:54
  16.9 1.9 scatter.6
  18.9 8.6 %all-to-all-start = ((bf16[32,24,7168]{2,1,0:T(8,128)(2,1)}), bf16[32,24,7168]{2,1,0:T(8,128)(2,1)}, u32[]{:S(2)}, u32[]{:S(2)}) async-start(bf16[32,24,7168]{2,1,0:T(8,128)(2,1)} %scatter.6), calls=%async_computation | async-start | bytes 22020096 | tf_op jit(solution)/shard_map/all_to_all | solution.py:63
  27.5 0.7 all-gather.5.cloned.1.call-update
  28.2 0.2 reduce-scatter.2.cloned.1.call-start
  28.5 131.3 %all-to-all-done = bf16[32,24,7168]{2,1,0:T(8,128)(2,1)} async-done(((bf16[32,24,7168]{2,1,0:T(8,128)(2,1)}), bf16[32,24,7168]{2,1,0:T(8,128)(2,1)}, u32[]{:S(2)}, u32[]{:S(2)}) %all-to-all-start) | async-done | bytes 11010080 | tf_op jit(solution)/shard_map/all_to_all | solution.py:63
  159.8 0.9 fusion.32
  160.8 5.6 %slice.89 = bf16[768,3584]{1,0:T(8,128)(2,1)} slice(bf16[768,7168]{1,0:T(8,128)(2,1)} %bitcast.2), slice={[0:768], [3584:7168]} | slice | bytes 11010048 | tf_op jit(solution)/shard_map/slice | solution.py:67
  166.4 11.7 %fusion.4 = f32[768,1024]{1,0:T(8,128)} fusion(bf16[1,2,3584,1024]{3,2,1,0:T(8,128)(2,1)} %all-gather.3.cloned.1.call-done, bf16[768,7168]{1,0:T(8,128)(2,1)} %bitcast.2), kind=kOutput, calls=%fused_computation.7 | convolution fusion | flops 5637144576 | bytes 15990784 | tf_op jit(solution)/shard_map/dot_general | solution.py:72
  178.1 10.6 %multiply_bitcast_fusion.1 = (f32[768,1,1024]{2,0,1:T(8,128)S(1)}, bf16[768,1024]{1,0:T(8,128)(2,1)}, f32[768,1,1024]{2,0,1:T(8,128)S(1)}) fusion(f32[768,1024]{1,0:T(8,128)} %fusion.4, f32[768]{0:T(1024)S(1)} %reshape.189, bf16[1,2,3584,1024]{3,2,1,0:T(8,128)(2,1)S(1)} %copy-done.6, bf16[768,7168]{1,0:T(8,128)(2,1)} %bitcast.2), kind=kOutput, calls=%fused_computation.33 | convolution fusion | flops 5647368192 | bytes 23859200 | tf_op jit(solution)/shard_map/dot_general | solution.py:71
  188.8 3.2 pad_maximum_fusion
  191.9 11.0 %convolution_convert_fusion.1 = bf16[1024,3584]{1,0:T(8,128)(2,1)} fusion(bf16[768,1024]{1,0:T(8,128)(2,1)S(1)} %copy-done.7, f32[768]{0:T(1024)S(1)} %reshape.189, bf16[768,7168]{1,0:T(8,128)(2,1)} %bitcast.2), kind=kOutput, calls=%fused_computation.5 | convolution fusion | flops 5649072128 | bytes 14420992 | tf_op jit(solution)/shard_map/dot_general | solution.py:24
  202.9 26.5 %all-gather.5.cloned.1.call-done = bf16[1,1024,3584]{2,1,0:T(8,128)(2,1)} async-done(((bf16[1,256,3584]{2,1,0:T(8,128)(2,1)}), bf16[1,1024,3584]{2,1,0:T(8,128)(2,1)}) %all-gather.5.cloned.1.call-update) | async-done | bytes 7340048 | tf_op jit(solution)/shard_map/all_gather | solution.py:61
  229.4 9.9 %multiply_reduce_fusion = (bf16[768]{0:T(1024)(128)(2,1)S(1)}, f32[768,1024]{1,0:T(8,128)S(1)}) fusion(bf16[768,1024]{1,0:T(8,128)(2,1)S(1)} %copy-done.7, bf16[768,3584]{1,0:T(8,128)(2,1)} %slice.89, bf16[1,1024,3584]{2,1,0:T(8,128)(2,1)} %all-gather.5.cloned.1.call-done), kind=kOutput, calls=%fused_computation.31 | convolution fusion | flops 5639502848 | bytes 17565184 | tf_op jit(solution)/shard_map/dot_general | solution.py:18
  239.4 4.6 %multiply_convert_fusion.1 = bf16[768,2,1024]{2,0,1:T(8,128)(2,1)S(1)} fusion(f32[768,2,1024]{2,0,1:T(8,128)} %pad_maximum_fusion, f32[768,1024]{1,0:T(8,128)S(1)} %get-tuple-element.57), kind=kLoop, calls=%fused_computation.13 | loop fusion | flops 3145728 | bytes 12582912 | tf_op jit(solution)/shard_map/convert_element_type | solution.py:87
  244.0 0.1 convert_element_type.144
  244.1 16.7 %bitcast_convert_fusion = bf16[768,3584]{1,0:T(8,128)(2,1)} fusion(bf16[768,2,1024]{2,0,1:T(8,128)(2,1)S(1)} %multiply_convert_fusion.1, bf16[1,2,3584,1024]{3,2,1,0:T(8,128)(2,1)} %all-gather.3.cloned.1.call-done), kind=kOutput, calls=%fused_computation.3 | convolution fusion | flops 11277041664 | bytes 23330816 | tf_op jit(solution)/shard_map/dot_general | solution.py:89
  260.7 1.9 scatter.9
  262.7 73.0 %all_to_all.10 = bf16[32,24,3584]{2,1,0:T(8,128)(2,1)S(1)} all-to-all(bf16[32,24,3584]{2,1,0:T(8,128)(2,1)} %scatter.9), channel_id=1, replica_groups=mesh['expert'=32,'dp'=4] {'expert'}, dimensions={0} | all-to-all | bytes 11010048 | tf_op jit(solution)/shard_map/all_to_all | solution.py:94
  335.7 2.4 copy-done
  338.2 0.3 select_reduce_fusion
  338.7 0.6 multiply_divide_fusion
  339.3 4.4 %convolution_convert_fusion.2 = bf16[64,3584]{1,0:T(8,128)(2,1)} fusion(bf16[768,3584]{1,0:T(8,128)(2,1)} %bitcast.70, bf16[768,64]{0,1:T(8,128)(2,1)S(1)} %convert_reduce_fusion), kind=kOutput, calls=%fused_computation.20 | convolution fusion | flops 352550912 | bytes 6062080 | tf_op jit(solution)/shard_map/dot_general | solution.py:24
  343.7 7.1 %fusion.21 = (bf16[1,256,3584]{2,1,0:T(8,128)(2,1)}, bf16[1,256,3584]{2,1,0:T(8,128)(2,1)}, bf16[1,256,3584]{2,1,0:T(8,128)(2,1)}) fusion(bf16[256,3584]{1,0:T(8,128)(2,1)} %reduce-scatter.2.cloned.1.call-done, bf16[1,256,3584]{2,1,0:T(8,128)(2,1)} %param.19, bf16[1,256,3584]{2,1,0:T(8,128)(2,1)} %param.18, bf16[1,256,3584]{2,1,0:T(8,128)(2,1)S(1)} %copy-done.1), kind=kLoop, calls=%fused_computation.38 | loop fusion | flops 21102592 | bytes 12845056 | tf_op jit(solution)/shard_map/convert_element_type | solution.py:119
  (41 shorter events, 1.2 us)
Async XLA Ops:
  7.2 0.8 copy-start.5
  7.2 2.5 copy-start.4
  7.2 4.0 %copy-start.3 = (bf16[64,3584]{1,0:T(8,128)(2,1)S(1)}, bf16[64,3584]{1,0:T(8,128)(2,1)}, u32[]{:S(2)}) copy-start(bf16[64,3584]{1,0:T(8,128)(2,1)} %param.12) | copy-start | bytes 1376260
  7.2 4.0 %copy-start.2 = (bf16[64,3584]{1,0:T(8,128)(2,1)S(1)}, bf16[64,3584]{1,0:T(8,128)(2,1)}, u32[]{:S(2)}) copy-start(bf16[64,3584]{1,0:T(8,128)(2,1)} %param.13) | copy-start | bytes 1376260
  7.2 159.2 %all-gather.3.cloned.1.call-start = ((), (), s32[]{:S(2)}) async-start(), calls=%async_computation.3 | async-start | bytes 18350080 | tf_op jit(solution)/shard_map/all_gather | solution.py:60
  18.9 141.0 %all-to-all-start = ((bf16[32,24,7168]{2,1,0:T(8,128)(2,1)}), bf16[32,24,7168]{2,1,0:T(8,128)(2,1)}, u32[]{:S(2)}, u32[]{:S(2)}) async-start(bf16[32,24,7168]{2,1,0:T(8,128)(2,1)} %scatter.6), calls=%async_computation | async-start | bytes 22020096 | tf_op jit(solution)/shard_map/all_to_all | solution.py:63
  27.5 202.0 %all-gather.5.cloned.1.call-start = ((), (), s32[]{:S(2)}) async-start(), calls=%async_computation.4 | async-start | bytes 9175040 | tf_op jit(solution)/shard_map/all_gather | solution.py:61
  28.2 315.5 %reduce-scatter.2.cloned.1.call-start = ((), (), s32[]{:S(2)}) async-start(), calls=%async_computation.5 | async-start | bytes 9175040 | tf_op jit(solution)/shard_map/reduce_scatter | solution.py:82
  166.4 11.7 %copy-start.6 = (bf16[1,2,3584,1024]{3,2,1,0:T(8,128)(2,1)S(1)}, bf16[1,2,3584,1024]{3,2,1,0:T(8,128)(2,1)}, u32[]{:S(2)}) copy-start(bf16[1,2,3584,1024]{3,2,1,0:T(8,128)(2,1)} %all-gather.3.cloned.1.call-done) | copy-start | bytes 44040196
  188.7 3.2 copy-start.7
  335.7 2.4 copy-start
  338.1 5.7 %copy-start.1 = (bf16[1,256,3584]{2,1,0:T(8,128)(2,1)S(1)}, bf16[1,256,3584]{2,1,0:T(8,128)(2,1)}, u32[]{:S(2)}) copy-start(bf16[1,256,3584]{2,1,0:T(8,128)(2,1)} %param.17) | copy-start | bytes 5505028
Sparse Core Ops, SparseCore 0:
  9.7 142.1 all-gather.2
  153.6 75.8 all-gather.4
  231.9 73.5 reduce-scatter.1

commit v10 on v8

--- a/solution.py
+++ b/solution.py
@@ -93,15 +93,6 @@
     ret_rows = route_in.reshape(experts, capacity, model_width)
     ret_rows = ret_rows.at[:, side_row, :capacity].set(affinity.reshape(experts, capacity))
     back_rows = lax.all_to_all(ret_rows, "expert", split_axis=0, concat_axis=0, tiled=True)
-    back_affinity = back_rows[:, side_row, :capacity].reshape(slot_count).astype(jnp.float32)
-    token_grad = contract_first(tok_match, back_rows.reshape(slot_count, model_width)).astype(
-        jnp.bfloat16
-    )
-    route_affinity = jnp.sum(matched * back_affinity[:, None], axis=0)
-    route_affinity = route_affinity.reshape(tok_rows, top_count)
-    mixed = jnp.sum(route_affinity * scores, axis=1, keepdims=True) / score_sum
-    router_grad = ROUTE_SCALE * scores * (1.0 - scores) * (route_affinity - mixed) / score_sum
-
     down_grad = (grad_shard * (1.0 / data_ways))[None]
     corr_one = 1.0 - BETA_ONE**STEP
     corr_two = 1.0 - BETA_TWO**STEP
@@ -112,6 +103,16 @@
         jnp.sqrt(second) * (1.0 / corr_two**0.5) + EPSILON
     ) + DECAY * down_wide
     new_down = (down_wide - LEARN_RATE * update).astype(jnp.bfloat16)
+    back_rows, new_down, first, second = lax.optimization_barrier((back_rows, new_down, first, second))
+    back_affinity = back_rows[:, side_row, :capacity].reshape(slot_count).astype(jnp.float32)
+    token_grad = contract_first(tok_match, back_rows.reshape(slot_count, model_width)).astype(
+        jnp.bfloat16
+    )
+    route_affinity = jnp.sum(matched * back_affinity[:, None], axis=0)
+    route_affinity = route_affinity.reshape(tok_rows, top_count)
+    mixed = jnp.sum(route_affinity * scores, axis=1, keepdims=True) / score_sum
+    router_grad = ROUTE_SCALE * scores * (1.0 - scores) * (route_affinity - mixed) / score_sum
+
     return (
         token_grad,
         router_grad,

time: 357 us -> 351 us (0.983)
  blocking collectives: 72.7 us -> 0 us
  waiting for transfers between devices: 164 us -> 218 us
  starting transfers between devices: 8.92 us -> 16.6 us
  other arithmetic: 11.2 us -> 15.3 us
    all_to_all x1 -> x0, blocking collectives: 72.7 us -> none  [shards(): lax.all_to_all(ret_rows, 'expert', split_axis=0, concat_axis=0, tiled=True)]
    reduce_scatter x1, waiting for transfers between devices: 0.01 us -> 35.8 us  [shards(): lax.psum_scatter(local_grad, 'dp', scatter_dimension=0, tiled=True)]
    all_to_all x0 -> x1, waiting for transfers between devices: none -> 18.5 us  [shards(): lax.all_to_all(ret_rows, 'expert', split_axis=0, concat_axis=0, tiled=True)]
    all_to_all x0 -> x1, starting transfers between devices: none -> 7.66 us  [shards(): lax.all_to_all(ret_rows, 'expert', split_axis=0, concat_axis=0, tiled=True)]
    add x0 -> x1, other arithmetic: none -> 6.04 us  [shards(): BETA_TWO * moment2.astype(jnp.float32)]
  transfers between devices with their start and end apart: 4 -> 5, of which waited for: 2 -> 4; matrix products, arithmetic and copies ran while one was open for 24% -> 26% of each run, Pallas kernels for 0% -> 0%
where the time goes in v10:
time: 351 us; the launch traced here: 347 us
  waiting for transfers between devices  218 us (62%)
  matrix products  72.4 us (21%)
  starting transfers between devices  16.6 us (5%)
  other arithmetic  15.3 us (4%)
  between operations  14 us (4%)
  local copies, waits for them, and re-layouts  10.8 us (3%)
    all_to_all x1, waiting for transfers between devices, shards(): lax.all_to_all(send_rows, 'expert', split_axis=0, concat_axis=0, tiled=True)  131 us
    reduce_scatter x1, waiting for transfers between devices, shards(): lax.psum_scatter(local_grad, 'dp', scatter_dimension=0, tiled=True)  35.8 us
    all_gather x1, waiting for transfers between devices, shards(): full_down = lax.all_gather(down, 'dp', axis=1, tiled=True)[0]  31.2 us
    all_to_all x1, waiting for transfers between devices, shards(): lax.all_to_all(ret_rows, 'expert', split_axis=0, concat_axis=0, tiled=True)  18.5 us
    dot_general x1, matrix products, shards(): lax.dot_general(grads, full_gu, (((1, 2), (0, 2)), ((), ())), preferred_e...  17.2 us
    dot_general x2, matrix products, contract_first(): lax.dot_general(left, right, (((0,), (0,)), ((), ())), preferred_element_...  15.3 us
    dot_general x1, matrix products, contract_last(): lax.dot_general(left, right, (((1,), (1,)), ((), ())), preferred_element_...  13.3 us
    dot_general x1, matrix products, shards(): pre_gate = jnp.dot(xs_rows, gate_w, preferred_element_type=jnp.float32)  10.6 us
  transfers between devices with their start and end apart: 5, of which 4 were waited for; matrix products, arithmetic and copies ran while one was open for 26% of the time, Pallas kernels for 0%

profile of v10, /device:TPU:1, one launch (start us, length us, event | category | flops | bytes accessed | tf_op | source)
XLA Modules:
  0.0 347.4 jit_solution(3607806218977885183)
XLA Ops:
  7.3 0.7 all-gather.3.cloned.1.call-update
  8.2 1.2 reduce-window.6
  9.4 0.2 slice_reduce_fusion
  9.7 0.1 fusion.30
  10.2 0.1 reshape.187
  10.3 0.2 select_reduce_fusion.1
  10.5 0.1 convert_element_type.147
  10.6 0.5 convert_reduce_fusion
  11.2 5.8 %convolution_convert_fusion = bf16[768,7168]{1,0:T(8,128)(2,1)} fusion(bf16[64,3584]{1,0:T(8,128)(2,1)S(1)} %copy-done.4, bf16[64,3584]{1,0:T(8,128)(2,1)S(1)} %copy-done.5, bf16[768,64]{0,1:T(8,128)(2,1)S(1)} %convert_reduce_fusion), kind=kOutput, calls=%fused_computation.2 | convolution fusion | flops 711983104 | bytes 12025856 | tf_op jit(solution)/shard_map/dot_general | solution.py:54
  17.0 1.9 scatter.6
  18.8 8.6 %all-to-all-start = ((bf16[32,24,7168]{2,1,0:T(8,128)(2,1)}), bf16[32,24,7168]{2,1,0:T(8,128)(2,1)}, u32[]{:S(2)}, u32[]{:S(2)}) async-start(bf16[32,24,7168]{2,1,0:T(8,128)(2,1)} %scatter.6), calls=%async_computation | async-start | bytes 22020096 | tf_op jit(solution)/shard_map/all_to_all | solution.py:63
  27.5 0.7 all-gather.5.cloned.1.call-update
  28.2 0.2 reduce-scatter.2.cloned.1.call-start
  28.5 131.3 %all-to-all-done = bf16[32,24,7168]{2,1,0:T(8,128)(2,1)} async-done(((bf16[32,24,7168]{2,1,0:T(8,128)(2,1)}), bf16[32,24,7168]{2,1,0:T(8,128)(2,1)}, u32[]{:S(2)}, u32[]{:S(2)}) %all-to-all-start) | async-done | bytes 11010080 | tf_op jit(solution)/shard_map/all_to_all | solution.py:63
  159.8 0.9 fusion.34
  160.8 5.6 %slice.89 = bf16[768,3584]{1,0:T(8,128)(2,1)} slice(bf16[768,7168]{1,0:T(8,128)(2,1)} %bitcast.2), slice={[0:768], [3584:7168]} | slice | bytes 11010048 | tf_op jit(solution)/shard_map/slice | solution.py:67
  166.4 10.6 %fusion.5 = f32[768,1024]{1,0:T(8,128)S(1)} fusion(bf16[1,2,3584,1024]{3,2,1,0:T(8,128)(2,1)} %all-gather.3.cloned.1.call-done, bf16[768,7168]{1,0:T(8,128)(2,1)} %bitcast.2), kind=kOutput, calls=%fused_computation.9 | convolution fusion | flops 5637144576 | bytes 15990784 | tf_op jit(solution)/shard_map/dot_general | solution.py:71
  177.0 10.3 %multiply_convert_fusion.4 = (bf16[768,1024]{1,0:T(8,128)(2,1)S(1)}, f32[768,1024]{1,0:T(8,128)}) fusion(f32[768,1024]{1,0:T(8,128)S(1)} %fusion.5, bf16[1,2,3584,1024]{3,2,1,0:T(8,128)(2,1)S(1)} %copy-done.8, bf16[768,7168]{1,0:T(8,128)(2,1)} %bitcast.2), kind=kOutput, calls=%fused_computation.35 | convolution fusion | flops 5641863168 | bytes 20709376 | tf_op jit(solution)/shard_map/dot_general | solution.py:72
  187.2 10.9 %convolution_convert_fusion.1 = bf16[1024,3584]{1,0:T(8,128)(2,1)} fusion(bf16[768,1024]{1,0:T(8,128)(2,1)S(1)} %get-tuple-element.61, f32[768]{0:T(1024)S(1)} %reshape.188, bf16[768,7168]{1,0:T(8,128)(2,1)} %bitcast.2), kind=kOutput, calls=%fused_computation.5 | convolution fusion | flops 5649072128 | bytes 14420992 | tf_op jit(solution)/shard_map/dot_general | solution.py:24
  198.2 31.2 %all-gather.5.cloned.1.call-done = bf16[1,1024,3584]{2,1,0:T(8,128)(2,1)} async-done(((bf16[1,256,3584]{2,1,0:T(8,128)(2,1)}), bf16[1,1024,3584]{2,1,0:T(8,128)(2,1)}) %all-gather.5.cloned.1.call-update) | async-done | bytes 7340048 | tf_op jit(solution)/shard_map/all_gather | solution.py:61
  229.4 13.3 %fusion.24 = (bf16[768,1,1024]{2,0,1:T(8,128)(2,1)S(1)}, bf16[768,1,1024]{2,0,1:T(8,128)(2,1)}, bf16[768]{0:T(1024)(128)(2,1)S(1)}) fusion(f32[768,1024]{1,0:T(8,128)} %copy-done.9, f32[768,1024]{1,0:T(8,128)} %get-tuple-element.62, f32[768]{0:T(1024)S(1)} %reshape.188, bf16[768,1024]{1,0:T(8,128)(2,1)S(1)} %get-tuple-element.61, ...), kind=kOutput, calls=%fused_computation.44 | convolution fusion | flops 5650512896 | bytes 23859712 | tf_op jit(solution)/shard_map/dot_general | solution.py:18
  242.8 17.2 %bitcast_convert_fusion = bf16[768,3584]{1,0:T(8,128)(2,1)} fusion(bf16[1,2,3584,1024]{3,2,1,0:T(8,128)(2,1)} %all-gather.3.cloned.1.call-done, bf16[768,1,1024]{2,0,1:T(8,128)(2,1)} %get-tuple-element.57, bf16[768,1,1024]{2,0,1:T(8,128)(2,1)S(1)} %get-tuple-element.56), kind=kOutput, calls=%fused_computation.3 | convolution fusion | flops 11278614528 | bytes 23330816 | tf_op jit(solution)/shard_map/dot_general | solution.py:90
  260.0 1.9 scatter.9
  261.9 7.7 %all-to-all-start.1 = ((bf16[32,24,3584]{2,1,0:T(8,128)(2,1)}), bf16[32,24,3584]{2,1,0:T(8,128)(2,1)}, u32[]{:S(2)}, u32[]{:S(2)}) async-start(bf16[32,24,3584]{2,1,0:T(8,128)(2,1)} %scatter.9), calls=%async_computation.1 | async-start | bytes 11010048 | tf_op jit(solution)/shard_map/all_to_all | solution.py:95
  269.6 35.8 %reduce-scatter.2.cloned.1.call-done = bf16[256,3584]{1,0:T(8,128)(2,1)} async-done(((bf16[1024,3584]{1,0:T(8,128)(2,1)}), bf16[256,3584]{1,0:T(8,128)(2,1)}) %reduce-scatter.2.cloned.1.call-update) | async-done | bytes 1835024 | tf_op jit(solution)/shard_map/reduce_scatter | solution.py:79
  305.4 6.0 %fusion.18 = (bf16[1,256,3584]{2,1,0:T(8,128)(2,1)}, bf16[1,256,3584]{2,1,0:T(8,128)(2,1)}) fusion(bf16[256,3584]{1,0:T(8,128)(2,1)} %reduce-scatter.2.cloned.1.call-done, bf16[1,256,3584]{2,1,0:T(8,128)(2,1)} %param.19, bf16[1,256,3584]{2,1,0:T(8,128)(2,1)} %param.18), kind=kLoop, calls=%fused_computation.28 | loop fusion | flops 11927552 | bytes 9175040 | tf_op jit(solution)/shard_map/add | solution.py:101
  311.5 4.3 %fusion.13 = bf16[1,256,3584]{2,1,0:T(8,128)(2,1)} fusion(bf16[1,256,3584]{2,1,0:T(8,128)(2,1)S(1)} %copy-done, bf16[256,3584]{1,0:T(8,128)(2,1)S(1)} %copy-done.3, bf16[1,256,3584]{2,1,0:T(8,128)(2,1)S(1)} %copy-done.1, bf16[1,256,3584]{2,1,0:T(8,128)(2,1)S(1)} %copy-done.2), kind=kLoop, calls=%fused_computation.23 | loop fusion | flops 19267584 | bytes 9175040 | tf_op jit(solution)/shard_map/convert_element_type | solution.py:105
  315.8 18.5 %all-to-all-done.1 = bf16[32,24,3584]{2,1,0:T(8,128)(2,1)} async-done(((bf16[32,24,3584]{2,1,0:T(8,128)(2,1)}), bf16[32,24,3584]{2,1,0:T(8,128)(2,1)}, u32[]{:S(2)}, u32[]{:S(2)}) %all-to-all-start.1) | async-done | bytes 5505056 | tf_op jit(solution)/shard_map/all_to_all | solution.py:95
  334.3 0.9 convert_reduce_fusion.1
  335.2 4.4 %convolution_convert_fusion.2 = bf16[64,3584]{1,0:T(8,128)(2,1)} fusion(bf16[768,3584]{1,0:T(8,128)(2,1)} %bitcast.13, bf16[768,64]{0,1:T(8,128)(2,1)S(1)} %convert_reduce_fusion), kind=kOutput, calls=%fused_computation.18 | convolution fusion | flops 352550912 | bytes 6062080 | tf_op jit(solution)/shard_map/dot_general | solution.py:24
  339.7 0.3 select_reduce_fusion
  340.2 0.6 multiply_divide_fusion
  (45 shorter events, 1.3 us)
Async XLA Ops:
  7.2 0.8 copy-start.7
  7.2 2.9 copy-start.6
  7.2 4.0 %copy-start.4 = (bf16[64,3584]{1,0:T(8,128)(2,1)S(1)}, bf16[64,3584]{1,0:T(8,128)(2,1)}, u32[]{:S(2)}) copy-start(bf16[64,3584]{1,0:T(8,128)(2,1)} %param.13) | copy-start | bytes 1376260
  7.2 4.0 %copy-start.5 = (bf16[64,3584]{1,0:T(8,128)(2,1)S(1)}, bf16[64,3584]{1,0:T(8,128)(2,1)}, u32[]{:S(2)}) copy-start(bf16[64,3584]{1,0:T(8,128)(2,1)} %param.12) | copy-start | bytes 1376260
  7.2 159.2 %all-gather.3.cloned.1.call-start = ((), (), s32[]{:S(2)}) async-start(), calls=%async_computation.3 | async-start | bytes 18350080 | tf_op jit(solution)/shard_map/all_gather | solution.py:60
  18.8 141.0 %all-to-all-start = ((bf16[32,24,7168]{2,1,0:T(8,128)(2,1)}), bf16[32,24,7168]{2,1,0:T(8,128)(2,1)}, u32[]{:S(2)}, u32[]{:S(2)}) async-start(bf16[32,24,7168]{2,1,0:T(8,128)(2,1)} %scatter.6), calls=%async_computation | async-start | bytes 22020096 | tf_op jit(solution)/shard_map/all_to_all | solution.py:63
  27.5 201.9 %all-gather.5.cloned.1.call-start = ((), (), s32[]{:S(2)}) async-start(), calls=%async_computation.4 | async-start | bytes 9175040 | tf_op jit(solution)/shard_map/all_gather | solution.py:61
  28.2 277.1 %reduce-scatter.2.cloned.1.call-start = ((), (), s32[]{:S(2)}) async-start(), calls=%async_computation.5 | async-start | bytes 9175040 | tf_op jit(solution)/shard_map/reduce_scatter | solution.py:79
  166.4 10.6 %copy-start.8 = (bf16[1,2,3584,1024]{3,2,1,0:T(8,128)(2,1)S(1)}, bf16[1,2,3584,1024]{3,2,1,0:T(8,128)(2,1)}, u32[]{:S(2)}) copy-start(bf16[1,2,3584,1024]{3,2,1,0:T(8,128)(2,1)} %all-gather.3.cloned.1.call-done) | copy-start | bytes 44040196
  177.0 10.3 %copy-start.9 = (f32[768,1024]{1,0:T(8,128)}, f32[768,1024]{1,0:T(8,128)S(1)}, u32[]{:S(2)}) copy-start(f32[768,1024]{1,0:T(8,128)S(1)} %fusion.5) | copy-start | bytes 9437188
  261.9 72.4 %all-to-all-start.1 = ((bf16[32,24,3584]{2,1,0:T(8,128)(2,1)}), bf16[32,24,3584]{2,1,0:T(8,128)(2,1)}, u32[]{:S(2)}, u32[]{:S(2)}) async-start(bf16[32,24,3584]{2,1,0:T(8,128)(2,1)} %scatter.9), calls=%async_computation.1 | async-start | bytes 11010048 | tf_op jit(solution)/shard_map/all_to_all | solution.py:95
  269.6 41.9 %copy-start = (bf16[1,256,3584]{2,1,0:T(8,128)(2,1)S(1)}, bf16[1,256,3584]{2,1,0:T(8,128)(2,1)}, u32[]{:S(2)}) copy-start(bf16[1,256,3584]{2,1,0:T(8,128)(2,1)} %param.17) | copy-start | bytes 5505028
  305.4 6.1 %copy-start.1 = (bf16[1,256,3584]{2,1,0:T(8,128)(2,1)S(1)}, bf16[1,256,3584]{2,1,0:T(8,128)(2,1)}, u32[]{:S(2)}) copy-start(bf16[1,256,3584]{2,1,0:T(8,128)(2,1)} %param.18) | copy-start | bytes 5505028
  305.4 6.1 %copy-start.2 = (bf16[1,256,3584]{2,1,0:T(8,128)(2,1)S(1)}, bf16[1,256,3584]{2,1,0:T(8,128)(2,1)}, u32[]{:S(2)}) copy-start(bf16[1,256,3584]{2,1,0:T(8,128)(2,1)} %param.19) | copy-start | bytes 5505028
  305.4 6.1 %copy-start.3 = (bf16[256,3584]{1,0:T(8,128)(2,1)S(1)}, bf16[256,3584]{1,0:T(8,128)(2,1)}, u32[]{:S(2)}) copy-start(bf16[256,3584]{1,0:T(8,128)(2,1)} %reduce-scatter.2.cloned.1.call-done) | copy-start | bytes 5505028
Sparse Core Ops, SparseCore 0:
  9.7 142.1 all-gather.2
  153.5 75.8 all-gather.4
  231.8 73.5 reduce-scatter.1
